TPU v7x, 256 devices: a whole 4x4x8 slice. The times are simulated.
256 devices in a mesh: sec: 2 (over core), gx: 16 (over y, x), gy: 8 (over z).
Axes of the slice: x: 4, y: 4, z: 8, core: 2. Of those that a mesh axis runs over, the one named last changes fastest.
Arguments:
- adjoint_state: float32 [2, 10, 2048, 1024], P('sec', None, 'gx', 'gy'), may hold values from -6 to 6
- forcing: float32 [2, 10, 2048, 1024], P('sec', None, 'gx', 'gy'), may hold values from -6 to 6
- viscosity: float32 [2, 2048, 1024], P('sec', 'gx', 'gy'), may hold values from 0.5 to 4
- reaction: float32 [2, 2048, 1024], P('sec', 'gx', 'gy'), may hold values from 0.1 to 1
- source_patch: int32 [2, 16384], P('sec', ('gx', 'gy')), may hold values from 0 to 63
- owner: int32 [2, 16384, 1], P('sec', ('gx', 'gy')), may hold values from 0 to 127; in each aligned block of 128 rows (0 to 127, 128 to 255, ..., all dimensions but the last counted through in order) at most 2 rows name the same one
- cavity_map: int32 [2, 128, 128, 2], P('sec', ('gx', 'gy')), may hold values from 0 to 63
Outputs:
- adjoint_field: float32 [2, 10, 2048, 1024], P('sec', None, 'gx', 'gy')
Inputs may be any that keep to these rules, and one draw needn't show every extreme that they name: The entries of one device name each owner at most 2 times, a bound that some block reaches.
All inputs are finite; a program needn't handle non-finite values.
Results may differ from a plain program's by a relative error of at most 0.00002.
Values sent between devices are 32-bit elements; how exact they have to be, the bound alone decides.
No kernel may reach another device: no remote copies, remote signals or barrier semaphores. Data moves between devices by JAX's collectives and lax.ppermute only.
A program may use at most 64 MiB of HBM per device.

v0:
```python
import jax
import jax.numpy as jnp
from jax import lax
from jax.sharding import PartitionSpec as P

PATCH = 2
PW = 128
SWEEPS = 8


OMEGA = 0.8
KAPPA = 0.5


def extended(cells, sides, width):
    for axis, dim in sides:
        count = lax.axis_size(axis)
        ends = count - 1
        head = lax.slice_in_dim(cells, 0, width, axis=dim)
        tail = lax.slice_in_dim(cells, cells.shape[dim] - width, cells.shape[dim], axis=dim)
        cells = jnp.concatenate(
            [
                lax.ppermute(tail, axis, [(i, (i + 1) % count) for i in range(ends)]),
                cells,
                lax.ppermute(head, axis, [((i + 1) % count, i) for i in range(ends)]),
            ],
            axis=dim,
        )
    return cells


def from_partner(block, axis, stride):
    count = lax.axis_size(axis)
    route = []
    for low in range(count):
        high = low | 1 << stride
        if high != low and high < count:
            route += [(low, high), (high, low)]
    return lax.ppermute(block, axis, route)


def relax(padded, visc, invd, force):
    center = padded[:, :, 1:-1, 1:-1]
    beside = padded[:, :, 2:, 1:-1] + padded[:, :, :-2, 1:-1]
    beside = beside + padded[:, :, 1:-1, 2:] + padded[:, :, 1:-1, :-2]
    return (1.0 - OMEGA) * center + OMEGA * invd * (force + visc * beside)


def single_sweep(field, visc, invd, force):
    padded = extended(field, (("gx", 2), ("gy", 3)), 1)
    return relax(padded, visc, invd, force)


def couple(field, source_patch, owner, cavity_map):
    levels, rows, cols = (field.shape[1], field.shape[2], field.shape[3])
    band_count = rows // PATCH
    strip_count = cols // PW
    grid = field[0].reshape(levels, band_count, PATCH, strip_count, PW)
    groups = cavity_map.shape[2]
    slots_per = cavity_map.shape[3]
    sources = source_patch[0]
    dest = owner[0, :, 0]
    onehot = (dest[:, None] == jnp.arange(groups, dtype=jnp.int32)[None, :]).astype(jnp.int32)
    before = jnp.cumsum(onehot, axis=0) - onehot
    rank = jnp.sum(before * onehot, axis=1)
    slot = dest * slots_per + rank
    src_band = sources // strip_count
    src_strip = sources % strip_count
    own = grid[:, src_band, :, src_strip, :]
    outgoing = jnp.zeros((groups * slots_per, levels, PATCH, PW), jnp.float32).at[slot].set(own)
    outgoing = outgoing.reshape(groups, slots_per, levels, PATCH, PW)
    crossed = from_partner(outgoing, "sec", 0)
    incoming = lax.all_to_all(crossed, ("gx", "gy"), split_axis=0, concat_axis=0, tiled=True)
    targets = cavity_map[0, 0].reshape(-1)
    tgt_band = targets // strip_count
    tgt_strip = targets % strip_count
    arrived = incoming.reshape(groups * slots_per, levels, PATCH, PW)
    local = grid[:, tgt_band, :, tgt_strip, :]
    answer = (local * jnp.tanh(arrived)).reshape(groups, slots_per, levels, PATCH, PW)
    updated = grid.at[:, tgt_band, :, tgt_strip, :].add(KAPPA * arrived)
    replies = lax.all_to_all(answer, ("gx", "gy"), split_axis=0, concat_axis=0, tiled=True)
    home = from_partner(replies, "sec", 0)
    back = home.reshape(groups * slots_per, levels, PATCH, PW)[slot]
    updated = updated.at[:, src_band, :, src_strip, :].add(back)
    return updated.reshape(1, levels, rows, cols)


def body(adjoint_state, forcing, viscosity, reaction, source_patch, owner, cavity_map):
    invd = 1.0 / (4.0 * viscosity + reaction)
    field = adjoint_state
    half = SWEEPS // 2
    visc = viscosity[:, None]
    inv_wide = invd[:, None]
    for step in range(half):
        field = single_sweep(field, visc, inv_wide, forcing)
    field = couple(field, source_patch, owner, cavity_map)
    for step in range(half):
        field = single_sweep(field, visc, inv_wide, forcing)
    return field


def solution(mesh):
    return jax.shard_map(
        body,
        mesh=mesh,
        in_specs=(
            P("sec", None, "gx", "gy"),
            P("sec", None, "gx", "gy"),
            P("sec", "gx", "gy"),
            P("sec", "gx", "gy"),
            P("sec", ("gx", "gy")),
            P("sec", ("gx", "gy"), None),
            P("sec", ("gx", "gy"), None, None),
        ),
        out_specs=P("sec", None, "gx", "gy"),
        check_vma=False,
    )
```

profile of v0, /device:TPU:54, one launch (start us, length us, event | category | flops | bytes accessed | tf_op | source)
XLA Modules:
  0.0 400.8 jit_solution(390232487160361227)
XLA Ops:
  3.6 5.3 %collective-permute-start.1 = (f32[1,10,1,128]{3,2,1,0:T(1,128)S(1)}, f32[1,10,1,128]{3,2,1,0:T(1,128)S(1)}, u32[]{:S(2)}, u32[]{:S(2)}) collective-permute-start(f32[1,10,1,128]{3,2,1,0:T(1,128)S(1)} %get-tuple-element.39), channel_id=1, source_target_pairs={{0,8},{8,16},{16,24},{24,32},{32,40},{40,48},{48,56},{56,64},{64,7... | collective-permute-start | bytes 15368 | tf_op jit(solution)/shard_map/ppermute | solution.py:23
  12.3 3.8 collective-permute-start.3
  19.1 3.3 collective-permute-done.2
  27.5 6.3 %collective-permute-start.5 = (f32[1,10,1,128]{3,2,1,0:T(1,128)S(1)}, f32[1,10,1,128]{3,2,1,0:T(1,128)S(1)}, u32[]{:S(2)}, u32[]{:S(2)}) collective-permute-start(f32[1,10,1,128]{3,2,1,0:T(1,128)S(1)} %get-tuple-element.37), channel_id=1, source_target_pairs={{0,8},{8,16},{16,24},{24,32},{32,40},{40,48},{48,56},{56,64},{64,7... | collective-permute-start | bytes 15368 | tf_op jit(solution)/shard_map/ppermute | solution.py:23
  36.0 4.9 %collective-permute-start.7 = (f32[1,10,130,1]{2,1,3,0:T(8,128)S(1)}, f32[1,10,130,1]{2,1,3,0:T(8,128)S(1)}, u32[]{:S(2)}, u32[]{:S(2)}) collective-permute-start(f32[1,10,130,1]{2,1,3,0:T(8,128)S(1)} %copy.33), channel_id=1, source_target_pairs={{0,1},{1,2},{2,3},{3,4},{4,5},{5,6},{6,7},{8,9},{9,10},{10,11},{11... | collective-permute-start | bytes 15608 | tf_op jit(solution)/shard_map/ppermute | solution.py:23
  44.0 4.6 %collective-permute-done.6 = f32[1,10,130,1]{2,1,3,0:T(8,128)S(1)} collective-permute-done((f32[1,10,130,1]{2,1,3,0:T(8,128)S(1)}, f32[1,10,130,1]{2,1,3,0:T(8,128)S(1)}, u32[]{:S(2)}, u32[]{:S(2)}) %collective-permute-start.6) | collective-permute-done | bytes 5232 | tf_op jit(solution)/shard_map/ppermute | solution.py:25
  52.1 5.6 %collective-permute-start.9 = (f32[1,10,1,128]{3,2,1,0:T(1,128)S(1)}, f32[1,10,1,128]{3,2,1,0:T(1,128)S(1)}, u32[]{:S(2)}, u32[]{:S(2)}) collective-permute-start(f32[1,10,1,128]{3,2,1,0:T(1,128)S(1)} %get-tuple-element.35), channel_id=1, source_target_pairs={{0,8},{8,16},{16,24},{24,32},{32,40},{40,48},{48,56},{56,64},{64,7... | collective-permute-start | bytes 15368 | tf_op jit(solution)/shard_map/ppermute | solution.py:23
  60.0 3.9 collective-permute-start.11
  67.0 3.2 collective-permute-done.10
  73.7 5.6 %collective-permute-start.13 = (f32[1,10,1,128]{3,2,1,0:T(1,128)S(1)}, f32[1,10,1,128]{3,2,1,0:T(1,128)S(1)}, u32[]{:S(2)}, u32[]{:S(2)}) collective-permute-start(f32[1,10,1,128]{3,2,1,0:T(1,128)S(1)} %get-tuple-element.33), channel_id=1, source_target_pairs={{0,8},{8,16},{16,24},{24,32},{32,40},{40,48},{48,56},{56,64},{64,7... | collective-permute-start | bytes 15368 | tf_op jit(solution)/shard_map/ppermute | solution.py:23
  81.6 3.1 collective-permute-start.15
  92.0 3.5 gather_fusion
  97.7 15.5 %scatter_fusion = f32[256,10,2,128]{3,2,1,0:T(2,128)} fusion(f32[256,10,2,128]{3,2,1,0:T(2,128)} %broadcast_in_dim.2, s32[128]{0:T(128)S(1)} %fusion.57, f32[128,10,2,128]{3,2,1,0:T(2,128)S(1)} %copy-done.2), kind=kCustom, calls=%fused_computation.3 | custom fusion | bytes 3932672 | tf_op jit(solution)/shard_map/scatter | solution.py:70
  113.2 5.2 %collective-permute-done.16 = f32[128,2,10,2,128]{4,3,2,1,0:T(2,128)} collective-permute-done((f32[128,2,10,2,128]{4,3,2,1,0:T(2,128)}, f32[128,2,10,2,128]{4,3,2,1,0:T(2,128)}, u32[]{:S(2)}, u32[]{:S(2)}) %collective-permute-start.16) | collective-permute-done | bytes 2621472 | tf_op jit(solution)/shard_map/ppermute | solution.py:39
  118.5 12.2 %all-to-all-start = ((f32[128,2,10,2,128]{4,3,2,1,0:T(2,128)}), f32[128,2,10,2,128]{4,3,2,1,0:T(2,128)}, u32[]{:S(2)}, u32[]{:S(2)}) async-start(f32[128,2,10,2,128]{4,3,2,1,0:T(2,128)} %collective-permute-done.16), calls=%async_computation | async-start | bytes 5242880 | tf_op jit(solution)/shard_map/all_to_all | solution.py:73
  131.0 5.8 %gather_fusion.1 = f32[256,10,2,128]{3,2,1,0:T(2,128)} fusion(f32[10,64,2,1,128]{4,2,3,1,0:T(2,128)S(1)} %bitcast.36, s32[256]{0:T(256)S(1)} %bitcast.41), kind=kCustom, calls=%fused_computation.1 | custom fusion | bytes 5244928 | tf_op jit(solution)/shard_map/gather | solution.py:78
  136.8 54.3 %all-to-all-done = f32[128,2,10,2,128]{4,3,2,1,0:T(2,128)} async-done(((f32[128,2,10,2,128]{4,3,2,1,0:T(2,128)}), f32[128,2,10,2,128]{4,3,2,1,0:T(2,128)}, u32[]{:S(2)}, u32[]{:S(2)}) %all-to-all-start) | async-done | bytes 2621472 | tf_op jit(solution)/shard_map/all_to_all | solution.py:73
  191.1 6.3 %tanh_multiply_fusion = (f32[128,2,10,2,128]{4,3,2,1,0:T(2,128)S(1)}, f32[128,2,10,2,128]{4,3,2,1,0:T(2,128)}) fusion(f32[128,2,10,2,128]{4,3,2,1,0:T(2,128)} %bitcast.43, f32[128,2,10,2,128]{4,3,2,1,0:T(2,128)} %all-to-all-done), kind=kLoop, calls=%fused_computation.6 | loop fusion | flops 1310720 | bytes 10485760 | tf_op jit(solution)/shard_map/mul | solution.py:79
  197.3 70.1 %all_to_all.10 = f32[128,2,10,2,128]{4,3,2,1,0:T(2,128)} all-to-all(f32[128,2,10,2,128]{4,3,2,1,0:T(2,128)S(1)} %get-tuple-element.7), channel_id=1, replica_groups=mesh['sec'=2,'gx'=16,'gy'=8] {'gx','gy'}, dimensions={0} | all-to-all | bytes 5242880 | tf_op jit(solution)/shard_map/all_to_all | solution.py:81
  267.4 31.0 %scatter_fusion.1 = f32[10,64,2,128]{3,2,1,0:T(2,128)S(1)} fusion(f32[10,64,2,128]{3,2,1,0:T(2,128)S(1)} %bitcast.37, s32[256]{0:T(256)S(1)} %bitcast.53, f32[256,10,2,128]{3,2,1,0:T(2,128)} %bitcast.42), kind=kCustom, calls=%fused_computation.4 | custom fusion | flops 655360 | bytes 7865344 | tf_op jit(solution)/shard_map/scatter-add | solution.py:80
  298.5 3.7 gather_fusion.2
  302.2 11.7 %scatter_fusion.2 = f32[10,64,2,128]{3,2,1,0:T(2,128)S(1)} fusion(f32[10,64,2,128]{3,2,1,0:T(2,128)S(1)} %scatter_fusion.1, s32[128]{0:T(128)S(1)} %get-tuple-element.41, f32[128,10,2,128]{3,2,1,0:T(2,128)S(1)} %gather_fusion.2), kind=kCustom, calls=%fused_computation.5 | custom fusion | flops 327680 | bytes 3932672 | tf_op jit(solution)/shard_map/scatter-add | solution.py:84
  316.0 5.9 %collective-permute-start.19 = (f32[1,10,1,128]{3,2,1,0:T(1,128)S(1)}, f32[1,10,1,128]{3,2,1,0:T(1,128)S(1)}, u32[]{:S(2)}, u32[]{:S(2)}) collective-permute-start(f32[1,10,1,128]{3,2,1,0:T(1,128)S(1)} %get-tuple-element.31), channel_id=1, source_target_pairs={{0,8},{8,16},{16,24},{24,32},{32,40},{40,48},{48,56},{56,64},{64,7... | collective-permute-start | bytes 15368 | tf_op jit(solution)/shard_map/ppermute | solution.py:23
  327.2 3.4 collective-permute-start.20
  335.7 6.3 %collective-permute-start.23 = (f32[1,10,1,128]{3,2,1,0:T(1,128)S(1)}, f32[1,10,1,128]{3,2,1,0:T(1,128)S(1)}, u32[]{:S(2)}, u32[]{:S(2)}) collective-permute-start(f32[1,10,1,128]{3,2,1,0:T(1,128)S(1)} %get-tuple-element.29), channel_id=1, source_target_pairs={{0,8},{8,16},{16,24},{24,32},{32,40},{40,48},{48,56},{56,64},{64,7... | collective-permute-start | bytes 15368 | tf_op jit(solution)/shard_map/ppermute | solution.py:23
  347.4 3.3 collective-permute-start.24
  358.8 5.4 %collective-permute-start.27 = (f32[1,10,1,128]{3,2,1,0:T(1,128)S(1)}, f32[1,10,1,128]{3,2,1,0:T(1,128)S(1)}, u32[]{:S(2)}, u32[]{:S(2)}) collective-permute-start(f32[1,10,1,128]{3,2,1,0:T(1,128)S(1)} %get-tuple-element.27), channel_id=1, source_target_pairs={{0,8},{8,16},{16,24},{24,32},{32,40},{40,48},{48,56},{56,64},{64,7... | collective-permute-start | bytes 15368 | tf_op jit(solution)/shard_map/ppermute | solution.py:23
  366.5 3.6 collective-permute-start.29
  373.2 3.1 collective-permute-done.28
  379.2 3.1 collective-permute-start.30
  382.3 5.1 %collective-permute-start.31 = (f32[1,10,1,128]{3,2,1,0:T(1,128)S(1)}, f32[1,10,1,128]{3,2,1,0:T(1,128)S(1)}, u32[]{:S(2)}, u32[]{:S(2)}) collective-permute-start(f32[1,10,1,128]{3,2,1,0:T(1,128)S(1)} %get-tuple-element.25), channel_id=1, source_target_pairs={{0,8},{8,16},{16,24},{24,32},{32,40},{40,48},{48,56},{56,64},{64,7... | collective-permute-start | bytes 15368 | tf_op jit(solution)/shard_map/ppermute | solution.py:23
  389.7 3.1 collective-permute-start.33
  (135 shorter events, 88.6 us)
Async XLA Ops:
  0.8 8.1 %collective-permute-start = (f32[1,10,1,128]{3,2,1,0:T(1,128)S(1)}, f32[1,10,1,128]{3,2,1,0:T(1,128)S(1)}, u32[]{:S(2)}, u32[]{:S(2)}) collective-permute-start(f32[1,10,1,128]{3,2,1,0:T(1,128)S(1)} %get-tuple-element.40), channel_id=1, source_target_pairs={{8,0},{16,8},{24,16},{32,24},{40,32},{48,40},{56,48},{64,56},{72,6... | collective-permute-start | bytes 15368 | tf_op jit(solution)/shard_map/ppermute | solution.py:25
  3.6 6.7 %collective-permute-start.1 = (f32[1,10,1,128]{3,2,1,0:T(1,128)S(1)}, f32[1,10,1,128]{3,2,1,0:T(1,128)S(1)}, u32[]{:S(2)}, u32[]{:S(2)}) collective-permute-start(f32[1,10,1,128]{3,2,1,0:T(1,128)S(1)} %get-tuple-element.39), channel_id=1, source_target_pairs={{0,8},{8,16},{16,24},{24,32},{32,40},{40,48},{48,56},{56,64},{64,7... | collective-permute-start | bytes 15368 | tf_op jit(solution)/shard_map/ppermute | solution.py:23
  12.3 6.5 %collective-permute-start.3 = (f32[1,10,130,1]{2,1,3,0:T(8,128)S(1)}, f32[1,10,130,1]{2,1,3,0:T(8,128)S(1)}, u32[]{:S(2)}, u32[]{:S(2)}) collective-permute-start(f32[1,10,130,1]{2,1,3,0:T(8,128)S(1)} %copy.29), channel_id=1, source_target_pairs={{0,1},{1,2},{2,3},{3,4},{4,5},{5,6},{6,7},{8,9},{9,10},{10,11},{11... | collective-permute-start | bytes 15608 | tf_op jit(solution)/shard_map/ppermute | solution.py:23
  16.7 5.6 %collective-permute-start.2 = (f32[1,10,130,1]{2,1,3,0:T(8,128)S(1)}, f32[1,10,130,1]{2,1,3,0:T(8,128)S(1)}, u32[]{:S(2)}, u32[]{:S(2)}) collective-permute-start(f32[1,10,130,1]{2,1,3,0:T(8,128)S(1)} %copy.27), channel_id=1, source_target_pairs={{1,0},{2,1},{3,2},{4,3},{5,4},{6,5},{7,6},{9,8},{10,9},{11,10},{12... | collective-permute-start | bytes 15608 | tf_op jit(solution)/shard_map/ppermute | solution.py:25
  25.5 8.2 %collective-permute-start.4 = (f32[1,10,1,128]{3,2,1,0:T(1,128)S(1)}, f32[1,10,1,128]{3,2,1,0:T(1,128)S(1)}, u32[]{:S(2)}, u32[]{:S(2)}) collective-permute-start(f32[1,10,1,128]{3,2,1,0:T(1,128)S(1)} %get-tuple-element.38), channel_id=1, source_target_pairs={{8,0},{16,8},{24,16},{32,24},{40,32},{48,40},{56,48},{64,56},{72,6... | collective-permute-start | bytes 15368 | tf_op jit(solution)/shard_map/ppermute | solution.py:25
  27.5 7.6 %collective-permute-start.5 = (f32[1,10,1,128]{3,2,1,0:T(1,128)S(1)}, f32[1,10,1,128]{3,2,1,0:T(1,128)S(1)}, u32[]{:S(2)}, u32[]{:S(2)}) collective-permute-start(f32[1,10,1,128]{3,2,1,0:T(1,128)S(1)} %get-tuple-element.37), channel_id=1, source_target_pairs={{0,8},{8,16},{16,24},{24,32},{32,40},{40,48},{48,56},{56,64},{64,7... | collective-permute-start | bytes 15368 | tf_op jit(solution)/shard_map/ppermute | solution.py:23
  36.0 7.6 %collective-permute-start.7 = (f32[1,10,130,1]{2,1,3,0:T(8,128)S(1)}, f32[1,10,130,1]{2,1,3,0:T(8,128)S(1)}, u32[]{:S(2)}, u32[]{:S(2)}) collective-permute-start(f32[1,10,130,1]{2,1,3,0:T(8,128)S(1)} %copy.33), channel_id=1, source_target_pairs={{0,1},{1,2},{2,3},{3,4},{4,5},{5,6},{6,7},{8,9},{9,10},{10,11},{11... | collective-permute-start | bytes 15608 | tf_op jit(solution)/shard_map/ppermute | solution.py:23
  41.6 7.0 %collective-permute-start.6 = (f32[1,10,130,1]{2,1,3,0:T(8,128)S(1)}, f32[1,10,130,1]{2,1,3,0:T(8,128)S(1)}, u32[]{:S(2)}, u32[]{:S(2)}) collective-permute-start(f32[1,10,130,1]{2,1,3,0:T(8,128)S(1)} %copy.31), channel_id=1, source_target_pairs={{1,0},{2,1},{3,2},{4,3},{5,4},{6,5},{7,6},{9,8},{10,9},{11,10},{12... | collective-permute-start | bytes 15608 | tf_op jit(solution)/shard_map/ppermute | solution.py:25
  49.5 8.5 %collective-permute-start.8 = (f32[1,10,1,128]{3,2,1,0:T(1,128)S(1)}, f32[1,10,1,128]{3,2,1,0:T(1,128)S(1)}, u32[]{:S(2)}, u32[]{:S(2)}) collective-permute-start(f32[1,10,1,128]{3,2,1,0:T(1,128)S(1)} %get-tuple-element.36), channel_id=1, source_target_pairs={{8,0},{16,8},{24,16},{32,24},{40,32},{48,40},{56,48},{64,56},{72,6... | collective-permute-start | bytes 15368 | tf_op jit(solution)/shard_map/ppermute | solution.py:25
  52.1 7.0 %collective-permute-start.9 = (f32[1,10,1,128]{3,2,1,0:T(1,128)S(1)}, f32[1,10,1,128]{3,2,1,0:T(1,128)S(1)}, u32[]{:S(2)}, u32[]{:S(2)}) collective-permute-start(f32[1,10,1,128]{3,2,1,0:T(1,128)S(1)} %get-tuple-element.35), channel_id=1, source_target_pairs={{0,8},{8,16},{16,24},{24,32},{32,40},{40,48},{48,56},{56,64},{64,7... | collective-permute-start | bytes 15368 | tf_op jit(solution)/shard_map/ppermute | solution.py:23
  60.0 6.7 %collective-permute-start.11 = (f32[1,10,130,1]{2,1,3,0:T(8,128)S(1)}, f32[1,10,130,1]{2,1,3,0:T(8,128)S(1)}, u32[]{:S(2)}, u32[]{:S(2)}) collective-permute-start(f32[1,10,130,1]{2,1,3,0:T(8,128)S(1)} %copy.37), channel_id=1, source_target_pairs={{0,1},{1,2},{2,3},{3,4},{4,5},{5,6},{6,7},{8,9},{9,10},{10,11},{11... | collective-permute-start | bytes 15608 | tf_op jit(solution)/shard_map/ppermute | solution.py:23
  71.1 8.3 %collective-permute-start.12 = (f32[1,10,1,128]{3,2,1,0:T(1,128)S(1)}, f32[1,10,1,128]{3,2,1,0:T(1,128)S(1)}, u32[]{:S(2)}, u32[]{:S(2)}) collective-permute-start(f32[1,10,1,128]{3,2,1,0:T(1,128)S(1)} %get-tuple-element.34), channel_id=1, source_target_pairs={{8,0},{16,8},{24,16},{32,24},{40,32},{48,40},{56,48},{64,56},{72,6... | collective-permute-start | bytes 15368 | tf_op jit(solution)/shard_map/ppermute | solution.py:25
  73.7 7.0 %collective-permute-start.13 = (f32[1,10,1,128]{3,2,1,0:T(1,128)S(1)}, f32[1,10,1,128]{3,2,1,0:T(1,128)S(1)}, u32[]{:S(2)}, u32[]{:S(2)}) collective-permute-start(f32[1,10,1,128]{3,2,1,0:T(1,128)S(1)} %get-tuple-element.33), channel_id=1, source_target_pairs={{0,8},{8,16},{16,24},{24,32},{32,40},{40,48},{48,56},{56,64},{64,7... | collective-permute-start | bytes 15368 | tf_op jit(solution)/shard_map/ppermute | solution.py:23
  81.6 6.5 %collective-permute-start.15 = (f32[1,10,130,1]{2,1,3,0:T(8,128)S(1)}, f32[1,10,130,1]{2,1,3,0:T(8,128)S(1)}, u32[]{:S(2)}, u32[]{:S(2)}) collective-permute-start(f32[1,10,130,1]{2,1,3,0:T(8,128)S(1)} %copy.41), channel_id=1, source_target_pairs={{0,1},{1,2},{2,3},{3,4},{4,5},{5,6},{6,7},{8,9},{9,10},{10,11},{11... | collective-permute-start | bytes 15608 | tf_op jit(solution)/shard_map/ppermute | solution.py:23
  85.4 5.6 %collective-permute-start.14 = (f32[1,10,130,1]{2,1,3,0:T(8,128)S(1)}, f32[1,10,130,1]{2,1,3,0:T(8,128)S(1)}, u32[]{:S(2)}, u32[]{:S(2)}) collective-permute-start(f32[1,10,130,1]{2,1,3,0:T(8,128)S(1)} %copy.39), channel_id=1, source_target_pairs={{1,0},{2,1},{3,2},{4,3},{5,4},{6,5},{7,6},{9,8},{10,9},{11,10},{12... | collective-permute-start | bytes 15608 | tf_op jit(solution)/shard_map/ppermute | solution.py:25
  118.5 72.6 %all-to-all-start = ((f32[128,2,10,2,128]{4,3,2,1,0:T(2,128)}), f32[128,2,10,2,128]{4,3,2,1,0:T(2,128)}, u32[]{:S(2)}, u32[]{:S(2)}) async-start(f32[128,2,10,2,128]{4,3,2,1,0:T(2,128)} %collective-permute-done.16), calls=%async_computation | async-start | bytes 5242880 | tf_op jit(solution)/shard_map/all_to_all | solution.py:73
  267.4 31.1 %collective-permute-start.17 = (f32[128,2,10,2,128]{4,3,2,1,0:T(2,128)}, f32[128,2,10,2,128]{4,3,2,1,0:T(2,128)}, u32[]{:S(2)}, u32[]{:S(2)}) collective-permute-start(f32[128,2,10,2,128]{4,3,2,1,0:T(2,128)} %all_to_all.10), channel_id=1, source_target_pairs={{0,128},{128,0},{1,129},{129,1},{2,130},{130,2},{3,131},{131,3},{4... | collective-permute-start | bytes 7864328 | tf_op jit(solution)/shard_map/ppermute | solution.py:39
  313.9 8.0 %collective-permute-start.18 = (f32[1,10,1,128]{3,2,1,0:T(1,128)S(1)}, f32[1,10,1,128]{3,2,1,0:T(1,128)S(1)}, u32[]{:S(2)}, u32[]{:S(2)}) collective-permute-start(f32[1,10,1,128]{3,2,1,0:T(1,128)S(1)} %get-tuple-element.32), channel_id=1, source_target_pairs={{8,0},{16,8},{24,16},{32,24},{40,32},{48,40},{56,48},{64,56},{72,6... | collective-permute-start | bytes 15368 | tf_op jit(solution)/shard_map/ppermute | solution.py:25
  316.0 7.2 %collective-permute-start.19 = (f32[1,10,1,128]{3,2,1,0:T(1,128)S(1)}, f32[1,10,1,128]{3,2,1,0:T(1,128)S(1)}, u32[]{:S(2)}, u32[]{:S(2)}) collective-permute-start(f32[1,10,1,128]{3,2,1,0:T(1,128)S(1)} %get-tuple-element.31), channel_id=1, source_target_pairs={{0,8},{8,16},{16,24},{24,32},{32,40},{40,48},{48,56},{56,64},{64,7... | collective-permute-start | bytes 15368 | tf_op jit(solution)/shard_map/ppermute | solution.py:23
  324.2 6.5 %collective-permute-start.21 = (f32[1,10,130,1]{2,1,3,0:T(8,128)S(1)}, f32[1,10,130,1]{2,1,3,0:T(8,128)S(1)}, u32[]{:S(2)}, u32[]{:S(2)}) collective-permute-start(f32[1,10,130,1]{2,1,3,0:T(8,128)S(1)} %copy.48), channel_id=1, source_target_pairs={{0,1},{1,2},{2,3},{3,4},{4,5},{5,6},{6,7},{8,9},{9,10},{10,11},{11... | collective-permute-start | bytes 15608 | tf_op jit(solution)/shard_map/ppermute | solution.py:23
  327.2 5.6 %collective-permute-start.20 = (f32[1,10,130,1]{2,1,3,0:T(8,128)S(1)}, f32[1,10,130,1]{2,1,3,0:T(8,128)S(1)}, u32[]{:S(2)}, u32[]{:S(2)}) collective-permute-start(f32[1,10,130,1]{2,1,3,0:T(8,128)S(1)} %copy.46), channel_id=1, source_target_pairs={{1,0},{2,1},{3,2},{4,3},{5,4},{6,5},{7,6},{9,8},{10,9},{11,10},{12... | collective-permute-start | bytes 15608 | tf_op jit(solution)/shard_map/ppermute | solution.py:25
  333.8 8.2 %collective-permute-start.22 = (f32[1,10,1,128]{3,2,1,0:T(1,128)S(1)}, f32[1,10,1,128]{3,2,1,0:T(1,128)S(1)}, u32[]{:S(2)}, u32[]{:S(2)}) collective-permute-start(f32[1,10,1,128]{3,2,1,0:T(1,128)S(1)} %get-tuple-element.30), channel_id=1, source_target_pairs={{8,0},{16,8},{24,16},{32,24},{40,32},{48,40},{56,48},{64,56},{72,6... | collective-permute-start | bytes 15368 | tf_op jit(solution)/shard_map/ppermute | solution.py:25
  335.7 7.6 %collective-permute-start.23 = (f32[1,10,1,128]{3,2,1,0:T(1,128)S(1)}, f32[1,10,1,128]{3,2,1,0:T(1,128)S(1)}, u32[]{:S(2)}, u32[]{:S(2)}) collective-permute-start(f32[1,10,1,128]{3,2,1,0:T(1,128)S(1)} %get-tuple-element.29), channel_id=1, source_target_pairs={{0,8},{8,16},{16,24},{24,32},{32,40},{40,48},{48,56},{56,64},{64,7... | collective-permute-start | bytes 15368 | tf_op jit(solution)/shard_map/ppermute | solution.py:23
  344.3 6.5 %collective-permute-start.25 = (f32[1,10,130,1]{2,1,3,0:T(8,128)S(1)}, f32[1,10,130,1]{2,1,3,0:T(8,128)S(1)}, u32[]{:S(2)}, u32[]{:S(2)}) collective-permute-start(f32[1,10,130,1]{2,1,3,0:T(8,128)S(1)} %copy.52), channel_id=1, source_target_pairs={{0,1},{1,2},{2,3},{3,4},{4,5},{5,6},{6,7},{8,9},{9,10},{10,11},{11... | collective-permute-start | bytes 15608 | tf_op jit(solution)/shard_map/ppermute | solution.py:23
  347.4 5.6 %collective-permute-start.24 = (f32[1,10,130,1]{2,1,3,0:T(8,128)S(1)}, f32[1,10,130,1]{2,1,3,0:T(8,128)S(1)}, u32[]{:S(2)}, u32[]{:S(2)}) collective-permute-start(f32[1,10,130,1]{2,1,3,0:T(8,128)S(1)} %copy.50), channel_id=1, source_target_pairs={{1,0},{2,1},{3,2},{4,3},{5,4},{6,5},{7,6},{9,8},{10,9},{11,10},{12... | collective-permute-start | bytes 15608 | tf_op jit(solution)/shard_map/ppermute | solution.py:25
  356.0 8.2 %collective-permute-start.26 = (f32[1,10,1,128]{3,2,1,0:T(1,128)S(1)}, f32[1,10,1,128]{3,2,1,0:T(1,128)S(1)}, u32[]{:S(2)}, u32[]{:S(2)}) collective-permute-start(f32[1,10,1,128]{3,2,1,0:T(1,128)S(1)} %get-tuple-element.28), channel_id=1, source_target_pairs={{8,0},{16,8},{24,16},{32,24},{40,32},{48,40},{56,48},{64,56},{72,6... | collective-permute-start | bytes 15368 | tf_op jit(solution)/shard_map/ppermute | solution.py:25
  358.8 6.8 %collective-permute-start.27 = (f32[1,10,1,128]{3,2,1,0:T(1,128)S(1)}, f32[1,10,1,128]{3,2,1,0:T(1,128)S(1)}, u32[]{:S(2)}, u32[]{:S(2)}) collective-permute-start(f32[1,10,1,128]{3,2,1,0:T(1,128)S(1)} %get-tuple-element.27), channel_id=1, source_target_pairs={{0,8},{8,16},{16,24},{24,32},{32,40},{40,48},{48,56},{56,64},{64,7... | collective-permute-start | bytes 15368 | tf_op jit(solution)/shard_map/ppermute | solution.py:23
  366.5 6.5 %collective-permute-start.29 = (f32[1,10,130,1]{2,1,3,0:T(8,128)S(1)}, f32[1,10,130,1]{2,1,3,0:T(8,128)S(1)}, u32[]{:S(2)}, u32[]{:S(2)}) collective-permute-start(f32[1,10,130,1]{2,1,3,0:T(8,128)S(1)} %copy.56), channel_id=1, source_target_pairs={{0,1},{1,2},{2,3},{3,4},{4,5},{5,6},{6,7},{8,9},{9,10},{10,11},{11... | collective-permute-start | bytes 15608 | tf_op jit(solution)/shard_map/ppermute | solution.py:23
  370.7 5.6 %collective-permute-start.28 = (f32[1,10,130,1]{2,1,3,0:T(8,128)S(1)}, f32[1,10,130,1]{2,1,3,0:T(8,128)S(1)}, u32[]{:S(2)}, u32[]{:S(2)}) collective-permute-start(f32[1,10,130,1]{2,1,3,0:T(8,128)S(1)} %copy.54), channel_id=1, source_target_pairs={{1,0},{2,1},{3,2},{4,3},{5,4},{6,5},{7,6},{9,8},{10,9},{11,10},{12... | collective-permute-start | bytes 15608 | tf_op jit(solution)/shard_map/ppermute | solution.py:25
  379.2 8.2 %collective-permute-start.30 = (f32[1,10,1,128]{3,2,1,0:T(1,128)S(1)}, f32[1,10,1,128]{3,2,1,0:T(1,128)S(1)}, u32[]{:S(2)}, u32[]{:S(2)}) collective-permute-start(f32[1,10,1,128]{3,2,1,0:T(1,128)S(1)} %get-tuple-element.26), channel_id=1, source_target_pairs={{8,0},{16,8},{24,16},{32,24},{40,32},{48,40},{56,48},{64,56},{72,6... | collective-permute-start | bytes 15368 | tf_op jit(solution)/shard_map/ppermute | solution.py:25
  382.3 6.4 %collective-permute-start.31 = (f32[1,10,1,128]{3,2,1,0:T(1,128)S(1)}, f32[1,10,1,128]{3,2,1,0:T(1,128)S(1)}, u32[]{:S(2)}, u32[]{:S(2)}) collective-permute-start(f32[1,10,1,128]{3,2,1,0:T(1,128)S(1)} %get-tuple-element.25), channel_id=1, source_target_pairs={{0,8},{8,16},{16,24},{24,32},{32,40},{40,48},{48,56},{56,64},{64,7... | collective-permute-start | bytes 15368 | tf_op jit(solution)/shard_map/ppermute | solution.py:23
  389.7 6.5 %collective-permute-start.33 = (f32[1,10,130,1]{2,1,3,0:T(8,128)S(1)}, f32[1,10,130,1]{2,1,3,0:T(8,128)S(1)}, u32[]{:S(2)}, u32[]{:S(2)}) collective-permute-start(f32[1,10,130,1]{2,1,3,0:T(8,128)S(1)} %copy.60), channel_id=1, source_target_pairs={{0,1},{1,2},{2,3},{3,4},{4,5},{5,6},{6,7},{8,9},{9,10},{10,11},{11... | collective-permute-start | bytes 15608 | tf_op jit(solution)/shard_map/ppermute | solution.py:23
  (10 other events, 102.8 us)
where the time goes:
time: 409 us; the launch traced here: 401 us
  starting transfers between devices  125 us (31%)
  waiting for transfers between devices  92.9 us (23%)
  blocking collectives  70.1 us (17%)
  other arithmetic  61.3 us (15%)
  local copies, waits for them, and re-layouts  50.4 us (12%)
    ppermute x16, starting transfers between devices, extended(): lax.ppermute(tail, axis, [(i, (i + 1) % count) for i in range(ends)])  73.1 us
    all_to_all x1, blocking collectives, couple(): lax.all_to_all(answer, ('gx', 'gy'), split_axis=0, concat_axis=0, tiled=T...  70.1 us
    all_to_all x1, waiting for transfers between devices, couple(): lax.all_to_all(crossed, ('gx', 'gy'), split_axis=0, concat_axis=0, tiled=...  54.3 us
    ppermute x16, starting transfers between devices, extended(): lax.ppermute(head, axis, [((i + 1) % count, i) for i in range(ends)])  40.1 us
    scatter-add x1, other arithmetic, couple(): updated = grid.at[:, tgt_band, :, tgt_strip, :].add(KAPPA * arrived)  31 us
    ppermute x16, waiting for transfers between devices, extended(): lax.ppermute(head, axis, [((i + 1) % count, i) for i in range(ends)])  23.3 us
    scatter x1, local copies, waits for them, and re-layouts, couple(): jnp.zeros((groups * slots_per, levels, PATCH, PW), jnp.float32).at[slot]  15.5 us
    all_to_all x1, starting transfers between devices, couple(): lax.all_to_all(crossed, ('gx', 'gy'), split_axis=0, concat_axis=0, tiled=...  12.2 us
  transfers between devices with their start and end apart: 35, of which 18 were waited for; matrix products, arithmetic and copies ran while one was open for 11% of the time, Pallas kernels for 0%

commit v1 on v0

v1 whole, which is shorter than its diff:
```python
import jax
import jax.numpy as jnp
from jax import lax
from jax.sharding import PartitionSpec as P

PATCH = 2
PW = 128
SWEEPS = 8


OMEGA = 0.8
KAPPA = 0.5
HIGHEST = lax.Precision.HIGHEST


def shifted(block, dx, dy):
    nx = lax.axis_size("gx")
    ny = lax.axis_size("gy")
    pairs = []
    for a in range(nx):
        for b in range(ny):
            sa, sb = a + dx, b + dy
            if 0 <= sa < nx and 0 <= sb < ny:
                pairs.append((sa * ny + sb, a * ny + b))
    return lax.ppermute(block, ("gx", "gy"), pairs)


def halo(cells, w):
    top, bot = cells[:, :w], cells[:, -w:]
    left, right = cells[:, :, :w], cells[:, :, -w:]
    north = shifted(bot, -1, 0)
    south = shifted(top, 1, 0)
    west = shifted(right, 0, -1)
    east = shifted(left, 0, 1)
    nw = shifted(cells[:, -w:, -w:], -1, -1)
    ne = shifted(cells[:, -w:, :w], -1, 1)
    sw = shifted(cells[:, :w, -w:], 1, -1)
    se = shifted(cells[:, :w, :w], 1, 1)
    rows = [
        jnp.concatenate([nw, north, ne], axis=2),
        jnp.concatenate([west, cells, east], axis=2),
        jnp.concatenate([sw, south, se], axis=2),
    ]
    return jnp.concatenate(rows, axis=1)


def relax(field, visc, invd, force):
    padded = jnp.pad(field, ((0, 0), (1, 1), (1, 1)))
    beside = padded[:, 2:, 1:-1] + padded[:, :-2, 1:-1]
    beside = beside + padded[:, 1:-1, 2:] + padded[:, 1:-1, :-2]
    return (1.0 - OMEGA) * field + OMEGA * invd * (force + visc * beside)


def sweeps(ext, visc, invd, force, count, w):
    for _ in range(count):
        ext = relax(ext, visc, invd, force)
    return ext[:, w:-w, w:-w]


def swap_sec(x):
    return lax.ppermute(x, "sec", [(0, 1), (1, 0)])


def onehot(index, size):
    return (index[:, None] == jnp.arange(size, dtype=jnp.int32)[None, :]).astype(jnp.float32)


def pick(sel, patches):
    return jnp.einsum("jk,lkrc->jlrc", sel, patches, precision=HIGHEST)


def spread(sel, values):
    return jnp.einsum("jk,jlrc->lkrc", sel, values, precision=HIGHEST)


def couple(x1, source_patch, owner, cavity_map):
    levels, rows, cols = x1.shape
    npatch = rows // PATCH
    groups, slots_per = cavity_map.shape[2], cavity_map.shape[3]
    nslot = groups * slots_per
    mine = x1.reshape(levels, npatch, PATCH, cols)
    other = swap_sec(mine)
    sources = source_patch[0]
    dest = owner[0, :, 0]
    count = dest.shape[0]
    earlier = jnp.arange(count)[None, :] < jnp.arange(count)[:, None]
    rank = jnp.sum((dest[:, None] == dest[None, :]) & earlier, axis=1).astype(jnp.int32)
    slot = dest * slots_per + rank
    send_sel = jnp.dot(onehot(slot, nslot).T, onehot(sources, npatch), precision=HIGHEST)
    cav_other = swap_sec(cavity_map[0, 0].reshape(-1))
    recv_sel = onehot(cav_other, npatch)
    sent = pick(send_sel, mine)
    local = pick(recv_sel, other)
    chunk = (groups, slots_per * levels * PATCH, cols)
    outgoing = jnp.concatenate([sent.reshape(chunk), local.reshape(chunk)], axis=1)
    incoming = lax.all_to_all(outgoing, ("gx", "gy"), 0, 0, tiled=True)
    half = slots_per * levels * PATCH
    arrived = incoming[:, :half].reshape(nslot, levels, PATCH, cols)
    answer = incoming[:, half:].reshape(nslot, levels, PATCH, cols)
    for_other = spread(recv_sel, KAPPA * arrived)
    for_mine = spread(send_sel, answer * jnp.tanh(sent))
    updated = mine + swap_sec(for_other) + for_mine
    return updated.reshape(levels, rows, cols)


def body(adjoint_state, forcing, viscosity, reaction, source_patch, owner, cavity_map):
    w = SWEEPS // 2
    levels = adjoint_state.shape[1]
    invd = 1.0 / (4.0 * viscosity + reaction)
    stacked = jnp.concatenate([adjoint_state[0], forcing[0], viscosity, invd], axis=0)
    ext = halo(stacked, w)
    field = ext[:levels]
    force = ext[levels:2 * levels]
    visc = ext[2 * levels:2 * levels + 1]
    inv_wide = ext[2 * levels + 1:]
    x1 = sweeps(field, visc, inv_wide, force, w, w)
    x2 = couple(x1, source_patch, owner, cavity_map)
    out = sweeps(halo(x2, w), visc, inv_wide, force, SWEEPS - w, w)
    return out[None]


def solution(mesh):
    return jax.shard_map(
        body,
        mesh=mesh,
        in_specs=(
            P("sec", None, "gx", "gy"),
            P("sec", None, "gx", "gy"),
            P("sec", "gx", "gy"),
            P("sec", "gx", "gy"),
            P("sec", ("gx", "gy")),
            P("sec", ("gx", "gy"), None),
            P("sec", ("gx", "gy"), None, None),
        ),
        out_specs=P("sec", None, "gx", "gy"),
        check_vma=False,
    )
```

time: 409 us -> 258 us (0.63)
  waiting for transfers between devices: 92.9 us -> 3.65 us
  starting transfers between devices: 125 us -> 59.4 us
  blocking collectives: 70.1 us -> 134 us
  other arithmetic: 61.3 us -> 23.1 us
  local copies, waits for them, and re-layouts: 50.4 us -> 24.6 us
  matrix products: 0 us -> 6.98 us
    all_to_all x1, blocking collectives: 70.1 us -> 134 us  [couple(): incoming = lax.all_to_all(outgoing, ('gx', 'gy'), 0, 0, tiled=True)]
    all_to_all x1 -> x0, waiting for transfers between devices: 54.3 us -> none  [couple(): lax.all_to_all(crossed, ('gx', 'gy'), split_axis=0, concat_axis=0, tiled=...]
    ppermute x34 -> x19, starting transfers between devices: 113 us -> 59.4 us  [the longest x16 58.8 us: shifted(): return lax.ppermute(block, ('gx', 'gy'), pairs)]
    scatter-add x2 -> x0, other arithmetic: 42.7 us -> none  [the longest x1 31 us: couple(): updated = grid.at[:, tgt_band, :, tgt_strip, :].add(KAPPA * arrived)]
    ppermute x34 -> x19, waiting for transfers between devices: 38.7 us -> 3.65 us  [the longest x16 3.62 us: shifted(): return lax.ppermute(block, ('gx', 'gy'), pairs)]
    scatter x1 -> x0, local copies, waits for them, and re-layouts: 15.5 us -> none  [couple(): jnp.zeros((groups * slots_per, levels, PATCH, PW), jnp.float32).at[slot]]
    gather x3 -> x0, local copies, waits for them, and re-layouts: 13.1 us -> none  [the longest x1 5.85 us: couple(): local = grid[:, tgt_band, :, tgt_strip, :]]
    all_to_all x1 -> x0, starting transfers between devices: 12.2 us -> none  [couple(): lax.all_to_all(crossed, ('gx', 'gy'), split_axis=0, concat_axis=0, tiled=...]
  transfers between devices with their start and end apart: 35 -> 19, of which waited for: 18 -> 3; matrix products, arithmetic and copies ran while one was open for 11% -> 14% of each run, Pallas kernels for 0% -> 0%
where the time goes in v1:
time: 258 us; the launch traced here: 252 us
  blocking collectives  134 us (52%)
  starting transfers between devices  59.4 us (23%)
  local copies, waits for them, and re-layouts  24.6 us (10%)
  other arithmetic  23.1 us (9%)
  matrix products  6.98 us (3%)
  waiting for transfers between devices  3.65 us (1%)
    all_to_all x1, blocking collectives, couple(): incoming = lax.all_to_all(outgoing, ('gx', 'gy'), 0, 0, tiled=True)  134 us
    ppermute x16, starting transfers between devices, shifted(): return lax.ppermute(block, ('gx', 'gy'), pairs)  58.8 us
    slice x6, local copies, waits for them, and re-layouts, halo(): left, right = (cells[:, :, :w], cells[:, :, -w:])  9.53 us
    concatenate x2, other arithmetic, halo(): return jnp.concatenate(rows, axis=1)  8.72 us
    ppermute x4, local copies, waits for them, and re-layouts, shifted(): return lax.ppermute(block, ('gx', 'gy'), pairs)  6.86 us
  transfers between devices with their start and end apart: 19, of which 3 were waited for; matrix products, arithmetic and copies ran while one was open for 14% of the time, Pallas kernels for 0%

profile of v1, /device:TPU:54, one launch (start us, length us, event | category | flops | bytes accessed | tf_op | source)
XLA Modules:
  0.0 252.4 jit_solution(7029444604803550799)
XLA Ops:
  1.9 3.1 %collective-permute-start.1 = (f32[22,4,128]{2,1,0:T(4,128)S(1)}, f32[22,4,128]{2,1,0:T(4,128)S(1)}, u32[]{:S(2)}, u32[]{:S(2)}) collective-permute-start(f32[22,4,128]{2,1,0:T(4,128)S(1)} %get-tuple-element.15), channel_id=1, source_target_pairs={{0,8},{1,9},{2,10},{3,11},{4,12},{5,13},{6,14},{7,15},{8,16},{9,17... | collective-permute-start | bytes 135176 | tf_op jit(solution)/shard_map/ppermute | solution.py:25
  5.0 2.7 %collective-permute-start.6 = (f32[22,4,128]{2,1,0:T(4,128)S(1)}, f32[22,4,128]{2,1,0:T(4,128)S(1)}, u32[]{:S(2)}, u32[]{:S(2)}) collective-permute-start(f32[22,4,128]{2,1,0:T(4,128)S(1)} %get-tuple-element.16), channel_id=1, source_target_pairs={{8,0},{9,1},{10,2},{11,3},{12,4},{13,5},{14,6},{15,7},{16,8},{17,9... | collective-permute-start | bytes 135176 | tf_op jit(solution)/shard_map/ppermute | solution.py:25
  7.9 2.1 fusion.30
  10.0 1.9 copy.35
  11.9 2.0 collective-permute-start.4
  14.4 3.8 %collective-permute-start.3 = (f32[22,128,4]{1,2,0:T(4,128)S(1)}, f32[22,128,4]{1,2,0:T(4,128)S(1)}, u32[]{:S(2)}, u32[]{:S(2)}) collective-permute-start(f32[22,128,4]{1,2,0:T(4,128)S(1)} %copy.34), channel_id=1, source_target_pairs={{0,1},{1,2},{2,3},{3,4},{4,5},{5,6},{6,7},{8,9},{9,10},{10,11},{11... | collective-permute-start | bytes 135176 | tf_op jit(solution)/shard_map/ppermute | solution.py:25
  18.4 6.6 %collective-permute-start = (f32[22,4,4]{2,1,0:T(4,128)S(1)}, f32[22,4,4]{2,1,0:T(4,128)S(1)}, u32[]{:S(2)}, u32[]{:S(2)}) collective-permute-start(f32[22,4,4]{2,1,0:T(4,128)S(1)} %get-tuple-element.11), channel_id=1, source_target_pairs={{0,9},{1,10},{2,11},{3,12},{4,13},{5,14},{6,15},{8,17},{9,18},{10,... | collective-permute-start | bytes 4232 | tf_op jit(solution)/shard_map/ppermute | solution.py:25
  25.0 1.7 collective-permute-done
  26.6 1.9 collective-permute-start.7
  28.6 3.2 %collective-permute-start.5 = (f32[22,4,4]{2,1,0:T(4,128)S(1)}, f32[22,4,4]{2,1,0:T(4,128)S(1)}, u32[]{:S(2)}, u32[]{:S(2)}) collective-permute-start(f32[22,4,4]{2,1,0:T(4,128)S(1)} %get-tuple-element.13), channel_id=1, source_target_pairs={{8,1},{9,2},{10,3},{11,4},{12,5},{13,6},{14,7},{16,9},{17,10},{18,... | collective-permute-start | bytes 4232 | tf_op jit(solution)/shard_map/ppermute | solution.py:25
  31.8 5.7 %collective-permute-start.2 = (f32[22,4,4]{2,1,0:T(4,128)S(1)}, f32[22,4,4]{2,1,0:T(4,128)S(1)}, u32[]{:S(2)}, u32[]{:S(2)}) collective-permute-start(f32[22,4,4]{2,1,0:T(4,128)S(1)} %get-tuple-element.14), channel_id=1, source_target_pairs={{1,8},{2,9},{3,10},{4,11},{5,12},{6,13},{7,14},{9,16},{10,17},{11,... | collective-permute-start | bytes 4232 | tf_op jit(solution)/shard_map/ppermute | solution.py:25
  39.3 1.6 copy.37
  42.0 6.6 %maximum_maximum_fusion = f32[22,136,136]{2,1,0:T(8,128)S(1)} fusion(f32[22,4,4]{2,1,0:T(4,128)S(1)} %collective-permute-done.7, f32[22,4,128]{2,1,0:T(4,128)S(1)} %collective-permute-done.6, f32[22,4,4]{2,1,0:T(4,128)S(1)} %collective-permute-done.5, f32[22,128,4]{2,1,0:T(8,128)} %copy.37, f32[1,128,128]{2,1,0:T(8,128)S(1)} %add_divide_fusion, ...), kind=kLoop, calls=%fused_computation.1 | loop fusion | flops 4476032 | bytes 3255296 | tf_op jit(solution)/shard_map/concatenate | solution.py:44
  54.3 2.3 fusion.27
  56.6 2.0 copy.39
  59.9 2.0 copy.42
  62.3 134.1 %all_to_all.5 = f32[128,80,128]{2,1,0:T(8,128)S(1)} all-to-all(f32[128,80,128]{2,1,0:T(8,128)S(1)} %pad_maximum_fusion), channel_id=1, replica_groups=mesh['sec'=2,'gx'=16,'gy'=8] {'gx','gy'}, dimensions={0} | all-to-all | bytes 10485760 | tf_op jit(solution)/shard_map/all_to_all | solution.py:96
  198.2 2.1 fusion.4
  203.1 5.2 %collective-permute-start.12 = (f32[10,4,128]{2,1,0:T(4,128)}, f32[10,4,128]{2,1,0:T(4,128)S(1)}, u32[]{:S(2)}, u32[]{:S(2)}) collective-permute-start(f32[10,4,128]{2,1,0:T(4,128)} %get-tuple-element.29), channel_id=1, source_target_pairs={{0,8},{1,9},{2,10},{3,11},{4,12},{5,13},{6,14},{7,15},{8,16},{9,17... | collective-permute-start | bytes 61448 | tf_op jit(solution)/shard_map/ppermute | solution.py:25
  208.3 1.9 collective-permute-start.17
  210.3 1.9 copy.47
  212.2 1.9 copy.48
  214.1 3.4 %collective-permute-start.15 = (f32[10,128,4]{1,2,0:T(4,128)}, f32[10,128,4]{1,2,0:T(4,128)}, u32[]{:S(2)}, u32[]{:S(2)}) collective-permute-start(f32[10,128,4]{1,2,0:T(4,128)} %copy.48), channel_id=1, source_target_pairs={{1,0},{2,1},{3,2},{4,3},{5,4},{6,5},{7,6},{9,8},{10,9},{11,10},{12... | collective-permute-start | bytes 61448 | tf_op jit(solution)/shard_map/ppermute | solution.py:25
  217.5 2.5 collective-permute-start.14
  221.5 5.5 %collective-permute-start.11 = (f32[10,4,4]{2,1,0:T(4,128)S(1)}, f32[10,4,4]{2,1,0:T(4,128)S(1)}, u32[]{:S(2)}, u32[]{:S(2)}) collective-permute-start(f32[10,4,4]{2,1,0:T(4,128)S(1)} %get-tuple-element.25), channel_id=1, source_target_pairs={{0,9},{1,10},{2,11},{3,12},{4,13},{5,14},{6,15},{8,17},{9,18},{10,... | collective-permute-start | bytes 1928 | tf_op jit(solution)/shard_map/ppermute | solution.py:25
  228.4 1.9 collective-permute-start.18
  230.4 4.8 %collective-permute-start.16 = (f32[10,4,4]{2,1,0:T(4,128)}, f32[10,4,4]{2,1,0:T(4,128)}, u32[]{:S(2)}, u32[]{:S(2)}) collective-permute-start(f32[10,4,4]{2,1,0:T(4,128)} %get-tuple-element.27), channel_id=1, source_target_pairs={{8,1},{9,2},{10,3},{11,4},{12,5},{13,6},{14,7},{16,9},{17,10},{18,... | collective-permute-start | bytes 1928 | tf_op jit(solution)/shard_map/ppermute | solution.py:25
  235.2 4.6 %collective-permute-start.13 = (f32[10,4,4]{2,1,0:T(4,128)}, f32[10,4,4]{2,1,0:T(4,128)}, u32[]{:S(2)}, u32[]{:S(2)}) collective-permute-start(f32[10,4,4]{2,1,0:T(4,128)} %get-tuple-element.28), channel_id=1, source_target_pairs={{1,8},{2,9},{3,10},{4,11},{5,12},{6,13},{7,14},{9,16},{10,17},{11,... | collective-permute-start | bytes 1928 | tf_op jit(solution)/shard_map/ppermute | solution.py:25
  239.8 1.8 copy.49
  241.6 1.8 copy.50
  243.5 2.2 maximum_maximum_fusion.1
  249.1 3.3 %fusion.9 = f32[1,10,128,128]{3,2,1,0:T(8,128)} fusion(f32[10,136,136]{2,1,0:T(8,128)S(1)} %multiply_add_fusion, f32[10,136,136]{2,1,0:T(8,128)S(1)} %get-tuple-element.21, f32[10,136,136]{2,1,0:T(8,128)S(1)} %get-tuple-element.20, f32[10,136,136]{2,1,0:T(8,128)S(1)} %get-tuple-element.19, f32[10,136,136]{2,1,0:T(8,128)} %copy-done.4, ...), kind=kLoop, calls=%fused_computation.33 | loop fusion | flops 1146880 | bytes 4063232 | tf_op jit(solution)/shard_map/broadcast_in_dim | solution.py:119
  (75 shorter events, 23.8 us)
Async XLA Ops:
  0.0 7.8 %copy-start.5 = (f32[1,128,128]{2,1,0:T(8,128)S(1)}, f32[1,128,128]{2,1,0:T(8,128)}, u32[]{:S(2)}) copy-start(f32[1,128,128]{2,1,0:T(8,128)} %param.9) | copy-start | bytes 196612
  0.0 7.8 %copy-start.1 = (f32[1,10,128,128]{3,2,1,0:T(8,128)S(1)}, f32[1,10,128,128]{3,2,1,0:T(8,128)}, u32[]{:S(2)}) copy-start(f32[1,10,128,128]{3,2,1,0:T(8,128)} %param.8) | copy-start | bytes 1966084
  0.0 7.8 %copy-start.2 = (f32[1,10,128,128]{3,2,1,0:T(8,128)S(1)}, f32[1,10,128,128]{3,2,1,0:T(8,128)}, u32[]{:S(2)}) copy-start(f32[1,10,128,128]{3,2,1,0:T(8,128)} %param.7) | copy-start | bytes 1966084
  1.9 39.5 %collective-permute-start.1 = (f32[22,4,128]{2,1,0:T(4,128)S(1)}, f32[22,4,128]{2,1,0:T(4,128)S(1)}, u32[]{:S(2)}, u32[]{:S(2)}) collective-permute-start(f32[22,4,128]{2,1,0:T(4,128)S(1)} %get-tuple-element.15), channel_id=1, source_target_pairs={{0,8},{1,9},{2,10},{3,11},{4,12},{5,13},{6,14},{7,15},{8,16},{9,17... | collective-permute-start | bytes 135176 | tf_op jit(solution)/shard_map/ppermute | solution.py:25
  5.0 37.0 %collective-permute-start.6 = (f32[22,4,128]{2,1,0:T(4,128)S(1)}, f32[22,4,128]{2,1,0:T(4,128)S(1)}, u32[]{:S(2)}, u32[]{:S(2)}) collective-permute-start(f32[22,4,128]{2,1,0:T(4,128)S(1)} %get-tuple-element.16), channel_id=1, source_target_pairs={{8,0},{9,1},{10,2},{11,3},{12,4},{13,5},{14,6},{15,7},{16,8},{17,9... | collective-permute-start | bytes 135176 | tf_op jit(solution)/shard_map/ppermute | solution.py:25
  10.0 3.9 %copy-start.3 = (f32[22,128,4]{2,1,0:T(8,128)S(1)}, f32[22,128,4]{2,1,0:T(8,128)}, u32[]{:S(2)}) copy-start(f32[22,128,4]{2,1,0:T(8,128)} %get-tuple-element.17) | copy-start | bytes 135172
  11.9 16.6 %collective-permute-start.4 = (f32[22,128,4]{1,2,0:T(4,128)S(1)}, f32[22,128,4]{1,2,0:T(4,128)S(1)}, u32[]{:S(2)}, u32[]{:S(2)}) collective-permute-start(f32[22,128,4]{1,2,0:T(4,128)S(1)} %copy.35), channel_id=1, source_target_pairs={{1,0},{2,1},{3,2},{4,3},{5,4},{6,5},{7,6},{9,8},{10,9},{11,10},{12... | collective-permute-start | bytes 135176 | tf_op jit(solution)/shard_map/ppermute | solution.py:25
  14.0 23.5 %copy-start.7 = (s32[1,1,128,2]{2,3,1,0:T(2,128)S(1)}, s32[1,1,128,2]{2,3,1,0:T(2,128)}, u32[]{:S(2)}) copy-start(s32[1,1,128,2]{2,3,1,0:T(2,128)} %param.13) | copy-start | bytes 3076
  14.4 17.4 %collective-permute-start.3 = (f32[22,128,4]{1,2,0:T(4,128)S(1)}, f32[22,128,4]{1,2,0:T(4,128)S(1)}, u32[]{:S(2)}, u32[]{:S(2)}) collective-permute-start(f32[22,128,4]{1,2,0:T(4,128)S(1)} %copy.34), channel_id=1, source_target_pairs={{0,1},{1,2},{2,3},{3,4},{4,5},{5,6},{6,7},{8,9},{9,10},{10,11},{11... | collective-permute-start | bytes 135176 | tf_op jit(solution)/shard_map/ppermute | solution.py:25
  18.4 8.3 %collective-permute-start = (f32[22,4,4]{2,1,0:T(4,128)S(1)}, f32[22,4,4]{2,1,0:T(4,128)S(1)}, u32[]{:S(2)}, u32[]{:S(2)}) collective-permute-start(f32[22,4,4]{2,1,0:T(4,128)S(1)} %get-tuple-element.11), channel_id=1, source_target_pairs={{0,9},{1,10},{2,11},{3,12},{4,13},{5,14},{6,15},{8,17},{9,18},{10,... | collective-permute-start | bytes 4232 | tf_op jit(solution)/shard_map/ppermute | solution.py:25
  26.6 14.3 %collective-permute-start.7 = (f32[22,4,4]{2,1,0:T(4,128)S(1)}, f32[22,4,4]{2,1,0:T(4,128)S(1)}, u32[]{:S(2)}, u32[]{:S(2)}) collective-permute-start(f32[22,4,4]{2,1,0:T(4,128)S(1)} %get-tuple-element.12), channel_id=1, source_target_pairs={{9,0},{10,1},{11,2},{12,3},{13,4},{14,5},{15,6},{17,8},{18,9},{19,... | collective-permute-start | bytes 4232 | tf_op jit(solution)/shard_map/ppermute | solution.py:25
  28.6 12.3 %collective-permute-start.5 = (f32[22,4,4]{2,1,0:T(4,128)S(1)}, f32[22,4,4]{2,1,0:T(4,128)S(1)}, u32[]{:S(2)}, u32[]{:S(2)}) collective-permute-start(f32[22,4,4]{2,1,0:T(4,128)S(1)} %get-tuple-element.13), channel_id=1, source_target_pairs={{8,1},{9,2},{10,3},{11,4},{12,5},{13,6},{14,7},{16,9},{17,10},{18,... | collective-permute-start | bytes 4232 | tf_op jit(solution)/shard_map/ppermute | solution.py:25
  31.8 9.6 %collective-permute-start.2 = (f32[22,4,4]{2,1,0:T(4,128)S(1)}, f32[22,4,4]{2,1,0:T(4,128)S(1)}, u32[]{:S(2)}, u32[]{:S(2)}) collective-permute-start(f32[22,4,4]{2,1,0:T(4,128)S(1)} %get-tuple-element.14), channel_id=1, source_target_pairs={{1,8},{2,9},{3,10},{4,11},{5,12},{6,13},{7,14},{9,16},{10,17},{11,... | collective-permute-start | bytes 4232 | tf_op jit(solution)/shard_map/ppermute | solution.py:25
  40.9 17.7 %collective-permute-start.8 = (s32[256]{0:T(256)S(1)}, s32[256]{0:T(256)S(1)}, u32[]{:S(2)}, u32[]{:S(2)}) collective-permute-start(s32[256]{0:T(256)S(1)} %reshape_squeeze.3), channel_id=1, source_target_pairs={{0,128},{128,0},{1,129},{129,1},{2,130},{130,2},{3,131},{131,3},{4... | collective-permute-start | bytes 3080 | tf_op jit(solution)/shard_map/ppermute | solution.py:61
  41.4 0.6 copy-start.6
  49.7 2.6 %copy-start.4 = (f32[10,136,136]{2,1,0:T(8,128)}, f32[10,136,136]{2,1,0:T(8,128)S(1)}, u32[]{:S(2)}) copy-start(f32[10,136,136]{2,1,0:T(8,128)S(1)} %get-tuple-element.7) | copy-start | bytes 2219524
  52.3 1.5 copy-start.8
  52.3 1.7 copy-start.9
  53.5 5.1 %collective-permute-start.9 = (f32[10,64,2,128]{3,1,2,0:T(8,128)S(1)}, f32[10,64,2,128]{3,1,2,0:T(8,128)S(1)}, u32[]{:S(2)}, u32[]{:S(2)}) collective-permute-start(f32[10,64,2,128]{3,1,2,0:T(8,128)S(1)} %copy.44), channel_id=1, source_target_pairs={{0,128},{128,0},{1,129},{129,1},{2,130},{130,2},{3,131},{131,3},{4... | collective-permute-start | bytes 1966088 | tf_op jit(solution)/shard_map/ppermute | solution.py:61
  197.9 2.4 collective-permute-start.10
  201.0 0.9 copy-start
  203.1 40.4 %collective-permute-start.12 = (f32[10,4,128]{2,1,0:T(4,128)}, f32[10,4,128]{2,1,0:T(4,128)S(1)}, u32[]{:S(2)}, u32[]{:S(2)}) collective-permute-start(f32[10,4,128]{2,1,0:T(4,128)} %get-tuple-element.29), channel_id=1, source_target_pairs={{0,8},{1,9},{2,10},{3,11},{4,12},{5,13},{6,14},{7,15},{8,16},{9,17... | collective-permute-start | bytes 61448 | tf_op jit(solution)/shard_map/ppermute | solution.py:25
  208.3 35.2 %collective-permute-start.17 = (f32[10,4,128]{2,1,0:T(4,128)}, f32[10,4,128]{2,1,0:T(4,128)S(1)}, u32[]{:S(2)}, u32[]{:S(2)}) collective-permute-start(f32[10,4,128]{2,1,0:T(4,128)} %get-tuple-element.30), channel_id=1, source_target_pairs={{8,0},{9,1},{10,2},{11,3},{12,4},{13,5},{14,6},{15,7},{16,8},{17,9... | collective-permute-start | bytes 61448 | tf_op jit(solution)/shard_map/ppermute | solution.py:25
  214.1 16.3 %collective-permute-start.15 = (f32[10,128,4]{1,2,0:T(4,128)}, f32[10,128,4]{1,2,0:T(4,128)}, u32[]{:S(2)}, u32[]{:S(2)}) collective-permute-start(f32[10,128,4]{1,2,0:T(4,128)} %copy.48), channel_id=1, source_target_pairs={{1,0},{2,1},{3,2},{4,3},{5,4},{6,5},{7,6},{9,8},{10,9},{11,10},{12... | collective-permute-start | bytes 61448 | tf_op jit(solution)/shard_map/ppermute | solution.py:25
  217.5 17.7 %collective-permute-start.14 = (f32[10,128,4]{1,2,0:T(4,128)}, f32[10,128,4]{1,2,0:T(4,128)}, u32[]{:S(2)}, u32[]{:S(2)}) collective-permute-start(f32[10,128,4]{1,2,0:T(4,128)} %copy.47), channel_id=1, source_target_pairs={{0,1},{1,2},{2,3},{3,4},{4,5},{5,6},{6,7},{8,9},{9,10},{10,11},{11... | collective-permute-start | bytes 61448 | tf_op jit(solution)/shard_map/ppermute | solution.py:25
  221.5 6.9 %collective-permute-start.11 = (f32[10,4,4]{2,1,0:T(4,128)S(1)}, f32[10,4,4]{2,1,0:T(4,128)S(1)}, u32[]{:S(2)}, u32[]{:S(2)}) collective-permute-start(f32[10,4,4]{2,1,0:T(4,128)S(1)} %get-tuple-element.25), channel_id=1, source_target_pairs={{0,9},{1,10},{2,11},{3,12},{4,13},{5,14},{6,15},{8,17},{9,18},{10,... | collective-permute-start | bytes 1928 | tf_op jit(solution)/shard_map/ppermute | solution.py:25
  228.4 15.0 %collective-permute-start.18 = (f32[10,4,4]{2,1,0:T(4,128)}, f32[10,4,4]{2,1,0:T(4,128)S(1)}, u32[]{:S(2)}, u32[]{:S(2)}) collective-permute-start(f32[10,4,4]{2,1,0:T(4,128)} %get-tuple-element.26), channel_id=1, source_target_pairs={{9,0},{10,1},{11,2},{12,3},{13,4},{14,5},{15,6},{17,8},{18,9},{19,... | collective-permute-start | bytes 1928 | tf_op jit(solution)/shard_map/ppermute | solution.py:25
  230.4 13.1 %collective-permute-start.16 = (f32[10,4,4]{2,1,0:T(4,128)}, f32[10,4,4]{2,1,0:T(4,128)}, u32[]{:S(2)}, u32[]{:S(2)}) collective-permute-start(f32[10,4,4]{2,1,0:T(4,128)} %get-tuple-element.27), channel_id=1, source_target_pairs={{8,1},{9,2},{10,3},{11,4},{12,5},{13,6},{14,7},{16,9},{17,10},{18,... | collective-permute-start | bytes 1928 | tf_op jit(solution)/shard_map/ppermute | solution.py:25
  235.2 8.3 %collective-permute-start.13 = (f32[10,4,4]{2,1,0:T(4,128)}, f32[10,4,4]{2,1,0:T(4,128)}, u32[]{:S(2)}, u32[]{:S(2)}) collective-permute-start(f32[10,4,4]{2,1,0:T(4,128)} %get-tuple-element.28), channel_id=1, source_target_pairs={{1,8},{2,9},{3,10},{4,11},{5,12},{6,13},{7,14},{9,16},{10,17},{11,... | collective-permute-start | bytes 1928 | tf_op jit(solution)/shard_map/ppermute | solution.py:25

commit v2 on v1

v2 whole, which is shorter than its diff:
```python
import jax
import jax.numpy as jnp
from jax import lax
from jax.sharding import PartitionSpec as P

PATCH = 2
PW = 128
SWEEPS = 8


OMEGA = 0.8
KAPPA = 0.5
HIGHEST = lax.Precision.HIGHEST


def shifted(block, dx, dy):
    nx = lax.axis_size("gx")
    ny = lax.axis_size("gy")
    pairs = []
    for a in range(nx):
        for b in range(ny):
            sa, sb = a + dx, b + dy
            if 0 <= sa < nx and 0 <= sb < ny:
                pairs.append((sa * ny + sb, a * ny + b))
    return lax.ppermute(block, ("gx", "gy"), pairs)


def halo(cells, w):
    west = shifted(cells[:, :, -w:], 0, -1)
    east = shifted(cells[:, :, :w], 0, 1)
    wide = jnp.concatenate([west, cells, east], axis=2)
    north = shifted(wide[:, -w:], -1, 0)
    south = shifted(wide[:, :w], 1, 0)
    return jnp.concatenate([north, wide, south], axis=1)


def relax(field, visc, invd, force):
    padded = jnp.pad(field, ((0, 0), (1, 1), (1, 1)))
    beside = padded[:, 2:, 1:-1] + padded[:, :-2, 1:-1]
    beside = beside + padded[:, 1:-1, 2:] + padded[:, 1:-1, :-2]
    return (1.0 - OMEGA) * field + OMEGA * invd * (force + visc * beside)


def sweeps(ext, visc, invd, force, count, w):
    for _ in range(count):
        ext = relax(ext, visc, invd, force)
    return ext[:, w:-w, w:-w]


def swap_sec(x):
    return lax.ppermute(x, "sec", [(0, 1), (1, 0)])


def onehot(index, size):
    return (index[:, None] == jnp.arange(size, dtype=jnp.int32)[None, :]).astype(jnp.float32)


def mm(a, b):
    return jnp.dot(a, b, precision=HIGHEST)


def selectors(source_patch, owner, cavity_map, npatch):
    groups, slots_per = cavity_map.shape[2], cavity_map.shape[3]
    sources = source_patch[0]
    dest = owner[0, :, 0]
    count = dest.shape[0]
    earlier = jnp.arange(count)[None, :] < jnp.arange(count)[:, None]
    rank = jnp.sum((dest[:, None] == dest[None, :]) & earlier, axis=1).astype(jnp.int32)
    by_owner = onehot(dest, groups)
    by_source = onehot(sources, npatch)
    send = [mm((by_owner * (rank == r).astype(jnp.float32)[:, None]).T, by_source) for r in range(slots_per)]
    cav_other = swap_sec(cavity_map[0, 0])
    recv = [onehot(cav_other[:, r], npatch) for r in range(slots_per)]
    return send, recv


def couple(x1, sel):
    send, recv = sel
    levels, rows, cols = x1.shape
    npatch = rows // PATCH
    width = levels * PATCH * cols
    mine = x1.reshape(levels, npatch, PATCH * cols).transpose(1, 0, 2).reshape(npatch, width)
    other = swap_sec(mine)
    sent = [mm(g, mine) for g in send]
    local = [mm(g, other) for g in recv]
    outgoing = jnp.concatenate(sent + local, axis=1)
    incoming = lax.all_to_all(outgoing, ("gx", "gy"), 0, 0, tiled=True)
    nr = len(send)
    arrived = [incoming[:, r * width:(r + 1) * width] for r in range(nr)]
    answer = [incoming[:, (nr + r) * width:(nr + r + 1) * width] for r in range(nr)]
    for_other = mm(recv[0].T, KAPPA * arrived[0])
    for_mine = mm(send[0].T, answer[0] * jnp.tanh(sent[0]))
    for r in range(1, nr):
        for_other = for_other + mm(recv[r].T, KAPPA * arrived[r])
        for_mine = for_mine + mm(send[r].T, answer[r] * jnp.tanh(sent[r]))
    updated = mine + swap_sec(for_other) + for_mine
    return updated.reshape(npatch, levels, PATCH * cols).transpose(1, 0, 2).reshape(levels, rows, cols)


def body(adjoint_state, forcing, viscosity, reaction, source_patch, owner, cavity_map):
    w = SWEEPS // 2
    levels, rows, cols = adjoint_state.shape[1:]
    invd = 1.0 / (4.0 * viscosity + reaction)
    stacked = jnp.concatenate([adjoint_state[0], forcing[0], viscosity, invd], axis=0)
    ext = halo(stacked, w)
    field = ext[:levels]
    force = ext[levels:2 * levels]
    visc = ext[2 * levels:2 * levels + 1]
    inv_wide = ext[2 * levels + 1:]
    sel = selectors(source_patch, owner, cavity_map, rows // PATCH)
    x1 = sweeps(field, visc, inv_wide, force, w, w)
    x2 = couple(x1, sel)
    out = sweeps(halo(x2, w), visc, inv_wide, force, SWEEPS - w, w)
    return out[None]


def solution(mesh):
    return jax.shard_map(
        body,
        mesh=mesh,
        in_specs=(
            P("sec", None, "gx", "gy"),
            P("sec", None, "gx", "gy"),
            P("sec", "gx", "gy"),
            P("sec", "gx", "gy"),
            P("sec", ("gx", "gy")),
            P("sec", ("gx", "gy"), None),
            P("sec", ("gx", "gy"), None, None),
        ),
        out_specs=P("sec", None, "gx", "gy"),
        check_vma=False,
    )
```

time: 258 us -> 243 us (0.942)
  starting transfers between devices: 59.4 us -> 24.7 us
  waiting for transfers between devices: 3.65 us -> 14.2 us
  local copies, waits for them, and re-layouts: 24.6 us -> 34.9 us
    ppermute x16 -> x8, starting transfers between devices: 58.8 us -> 24.3 us  [shifted(): return lax.ppermute(block, ('gx', 'gy'), pairs)]
    ppermute x16 -> x8, waiting for transfers between devices: 3.62 us -> 14.2 us  [shifted(): return lax.ppermute(block, ('gx', 'gy'), pairs)]
    all_to_all x0 -> x1, local copies, waits for them, and re-layouts: none -> 10.2 us  [couple(): incoming = lax.all_to_all(outgoing, ('gx', 'gy'), 0, 0, tiled=True)]
    reshape x1 -> x3, local copies, waits for them, and re-layouts: 0.07 us -> 6.3 us  [the longest x2 4.19 us: couple(): updated.reshape(npatch, levels, PATCH * cols).transpose(1, 0, 2)]
    concatenate x3 -> x2, other arithmetic: 9.13 us -> 3.66 us  [halo(): return jnp.concatenate([north, wide, south], axis=1)]
    dot_general x2 -> x0, local copies, waits for them, and re-layouts: 4.05 us -> none  [pick(): return jnp.einsum('jk,lkrc->jlrc', sel, patches, precision=HIGHEST)]
    ppermute x4, local copies, waits for them, and re-layouts: 6.86 us -> 3.16 us  [shifted(): return lax.ppermute(block, ('gx', 'gy'), pairs)]
    slice x8 -> x6, local copies, waits for them, and re-layouts: 11.7 us -> 9.07 us  [the longest x4 5.94 us: halo(): west = shifted(cells[:, :, -w:], 0, -1)]
  transfers between devices with their start and end apart: 19 -> 11, of which waited for: 3 -> 5; matrix products, arithmetic and copies ran while one was open for 14% -> 12% of each run, Pallas kernels for 0% -> 0%
where the time goes in v2:
time: 243 us; the launch traced here: 240 us
  blocking collectives  133 us (55%)
  local copies, waits for them, and re-layouts  34.9 us (14%)
  starting transfers between devices  24.7 us (10%)
  other arithmetic  24.1 us (10%)
  waiting for transfers between devices  14.2 us (6%)
  matrix products  7.85 us (3%)
    all_to_all x1, blocking collectives, couple(): incoming = lax.all_to_all(outgoing, ('gx', 'gy'), 0, 0, tiled=True)  133 us
    ppermute x8, starting transfers between devices, shifted(): return lax.ppermute(block, ('gx', 'gy'), pairs)  24.3 us
    ppermute x8, waiting for transfers between devices, shifted(): return lax.ppermute(block, ('gx', 'gy'), pairs)  14.2 us
    all_to_all x1, local copies, waits for them, and re-layouts, couple(): incoming = lax.all_to_all(outgoing, ('gx', 'gy'), 0, 0, tiled=True)  10.2 us
    dot_general x10, matrix products, mm(): return jnp.dot(a, b, precision=HIGHEST)  7.85 us
    add x6, other arithmetic, relax(): return (1.0 - OMEGA) * field + OMEGA * invd * (force + visc * beside)  5.98 us
    slice x4, local copies, waits for them, and re-layouts, halo(): west = shifted(cells[:, :, -w:], 0, -1)  5.94 us
  transfers between devices with their start and end apart: 11, of which 5 were waited for; matrix products, arithmetic and copies ran while one was open for 12% of the time, Pallas kernels for 0%

profile of v2, /device:TPU:54, one launch (start us, length us, event | category | flops | bytes accessed | tf_op | source)
XLA Modules:
  0.0 239.6 jit_solution(12573022020883155282)
XLA Ops:
  0.9 1.4 pad_maximum_fusion.1
  2.3 1.6 fusion.40
  4.0 1.8 copy.25
  5.8 2.0 collective-permute-start.1
  8.3 3.8 %collective-permute-start = (f32[22,128,4]{1,2,0:T(4,128)S(1)}, f32[22,128,4]{1,2,0:T(4,128)S(1)}, u32[]{:S(2)}, u32[]{:S(2)}) collective-permute-start(f32[22,128,4]{1,2,0:T(4,128)S(1)} %copy.24), channel_id=1, source_target_pairs={{0,1},{1,2},{2,3},{3,4},{4,5},{5,6},{6,7},{8,9},{9,10},{10,11},{11... | collective-permute-start | bytes 135176 | tf_op jit(solution)/shard_map/ppermute | solution.py:25
  12.6 1.6 collective-permute-done
  15.2 1.3 pad_maximum_fusion.8
  16.6 3.1 %collective-permute-start.2 = (f32[22,4,136]{2,1,0:T(4,128)S(1)}, f32[22,4,136]{2,1,0:T(4,128)S(1)}, u32[]{:S(2)}, u32[]{:S(2)}) collective-permute-start(f32[22,4,136]{2,1,0:T(4,128)S(1)} %get-tuple-element.5), channel_id=1, source_target_pairs={{0,8},{1,9},{2,10},{3,11},{4,12},{5,13},{6,14},{7,15},{8,16},{9,17... | collective-permute-start | bytes 143624 | tf_op jit(solution)/shard_map/ppermute | solution.py:25
  19.7 2.7 %collective-permute-start.3 = (f32[22,4,136]{2,1,0:T(4,128)S(1)}, f32[22,4,136]{2,1,0:T(4,128)S(1)}, u32[]{:S(2)}, u32[]{:S(2)}) collective-permute-start(f32[22,4,136]{2,1,0:T(4,128)S(1)} %get-tuple-element.6), channel_id=1, source_target_pairs={{8,0},{9,1},{10,2},{11,3},{12,4},{13,5},{14,6},{15,7},{16,8},{17,9... | collective-permute-start | bytes 143624 | tf_op jit(solution)/shard_map/ppermute | solution.py:25
  23.0 5.2 %collective-permute-done.3 = f32[22,4,136]{2,1,0:T(4,128)S(1)} collective-permute-done((f32[22,4,136]{2,1,0:T(4,128)S(1)}, f32[22,4,136]{2,1,0:T(4,128)S(1)}, u32[]{:S(2)}, u32[]{:S(2)}) %collective-permute-start.3) | collective-permute-done | bytes 47904 | tf_op jit(solution)/shard_map/ppermute | solution.py:25
  28.2 3.0 %pad_maximum_fusion = f32[22,136,136]{2,1,0:T(8,128)S(1)} fusion(f32[22,4,136]{2,1,0:T(4,128)S(1)} %collective-permute-done.3, f32[22,128,4]{2,1,0:T(8,128)} %copy-done.2, f32[1,128,128]{2,1,0:T(8,128)S(1)} %add_divide_fusion, f32[1,128,128]{2,1,0:T(8,128)S(1)} %copy-done.14, f32[10,128,128]{2,1,0:T(8,128)S(1)} %bitcast.43, f32[10,128,128]{2,1,0:T(8,128)S(1)} %bitcast.46, ...), kind=kLoop, calls=%fused_computation.4 | loop fusion | flops 2848384 | bytes 3255296 | tf_op jit(solution)/shard_map/concatenate | solution.py:34
  35.1 1.9 fusion.9
  37.0 2.1 reshape.25
  40.5 1.2 fusion.43
  41.8 1.2 fusion.42
  44.5 2.5 %maximum_bitcast_fusion = f32[128,1,10240]{2,0,1:T(8,128)} fusion(f32[128,2560]{1,0:T(8,128)S(1)} %fusion.16, f32[128,2560]{1,0:T(8,128)S(1)} %fusion.21, f32[128,2560]{1,0:T(8,128)S(1)} %fusion.43, f32[128,2560]{1,0:T(8,128)S(1)} %fusion.42), kind=kLoop, calls=%fused_computation | loop fusion | flops 3932160 | bytes 10485760 | tf_op jit(solution)/shard_map/all_to_all | solution.py:87
  47.1 10.2 %copy.29 = f32[128,1,10240]{2,1,0:T(1,128)} copy(f32[128,1,10240]{2,0,1:T(8,128)} %maximum_bitcast_fusion) | data formatting | bytes 10485760 | tf_op jit(solution)/shard_map/all_to_all | solution.py:87
  57.3 133.3 %all_to_all.12 = f32[128,1,10240]{2,1,0:T(1,128)S(1)} all-to-all(f32[128,1,10240]{2,1,0:T(1,128)} %copy.29), channel_id=1, replica_groups=mesh['sec'=2,'gx'=16,'gy'=8] {'gx','gy'}, dimensions={0} | all-to-all | bytes 10485760 | tf_op jit(solution)/shard_map/all_to_all | solution.py:87
  190.6 1.6 copy.39
  197.3 2.2 reshape.27
  199.5 2.4 %copy.30 = f32[10,64,256]{2,1,0:T(8,128)} copy(f32[10,64,256]{2,0,1:T(8,128)} %bitcast.47) | data formatting | bytes 1310720 | tf_op jit(solution)/shard_map/transpose | solution.py:97
  202.0 2.0 reshape.28
  204.0 2.6 %fusion.41 = (f32[10,128,4]{2,1,0:T(8,128)}, f32[10,128,4]{2,1,0:T(8,128)}) fusion(f32[10,128,128]{2,1,0:T(8,128)} %reshape.28), kind=kLoop, calls=%fused_computation.99 | loop fusion | bytes 81920 | tf_op jit(solution)/shard_map/slice | solution.py:29
  206.5 1.3 copy.31
  207.8 2.6 %collective-permute-start.7 = (f32[10,128,4]{1,2,0:T(4,128)S(1)}, f32[10,128,4]{1,2,0:T(4,128)S(1)}, u32[]{:S(2)}, u32[]{:S(2)}) collective-permute-start(f32[10,128,4]{1,2,0:T(4,128)S(1)} %copy.31), channel_id=1, source_target_pairs={{0,1},{1,2},{2,3},{3,4},{4,5},{5,6},{6,7},{8,9},{9,10},{10,11},{11... | collective-permute-start | bytes 61448 | tf_op jit(solution)/shard_map/ppermute | solution.py:25
  210.4 1.3 copy.32
  211.7 3.3 %collective-permute-start.8 = (f32[10,128,4]{1,2,0:T(4,128)S(1)}, f32[10,128,4]{1,2,0:T(4,128)S(1)}, u32[]{:S(2)}, u32[]{:S(2)}) collective-permute-start(f32[10,128,4]{1,2,0:T(4,128)S(1)} %copy.32), channel_id=1, source_target_pairs={{1,0},{2,1},{3,2},{4,3},{5,4},{6,5},{7,6},{9,8},{10,9},{11,10},{12... | collective-permute-start | bytes 61448 | tf_op jit(solution)/shard_map/ppermute | solution.py:25
  216.1 1.3 collective-permute-done.8
  219.7 4.6 %collective-permute-start.9 = (f32[10,4,136]{2,1,0:T(4,128)S(1)}, f32[10,4,136]{2,1,0:T(4,128)S(1)}, u32[]{:S(2)}, u32[]{:S(2)}) collective-permute-start(f32[10,4,136]{2,1,0:T(4,128)S(1)} %get-tuple-element.11), channel_id=1, source_target_pairs={{0,8},{1,9},{2,10},{3,11},{4,12},{5,13},{6,14},{7,15},{8,16},{9,17... | collective-permute-start | bytes 65288 | tf_op jit(solution)/shard_map/ppermute | solution.py:25
  224.2 2.2 collective-permute-start.10
  226.4 5.8 %collective-permute-done.10 = f32[10,4,136]{2,1,0:T(4,128)S(1)} collective-permute-done((f32[10,4,136]{2,1,0:T(4,128)S(1)}, f32[10,4,136]{2,1,0:T(4,128)S(1)}, u32[]{:S(2)}, u32[]{:S(2)}) %collective-permute-start.10) | collective-permute-done | bytes 21792 | tf_op jit(solution)/shard_map/ppermute | solution.py:25
  236.3 3.3 %fusion.5 = f32[1,10,128,128]{3,2,1,0:T(8,128)} fusion(f32[10,136,136]{2,1,0:T(8,128)S(1)} %multiply_add_fusion, f32[10,136,136]{2,1,0:T(8,128)S(1)} %get-tuple-element.17, f32[10,136,136]{2,1,0:T(8,128)S(1)} %get-tuple-element.16, f32[10,136,136]{2,1,0:T(8,128)S(1)} %get-tuple-element.15, f32[10,136,136]{2,1,0:T(8,128)} %copy-done.13, ...), kind=kLoop, calls=%fused_computation.35 | loop fusion | flops 1146880 | bytes 4063232 | tf_op jit(solution)/shard_map/broadcast_in_dim | solution.py:114
  (77 shorter events, 22.3 us)
Async XLA Ops:
  0.0 40.5 %collective-permute-start.4 = (s32[128,2]{0,1:T(2,128)}, s32[128,2]{0,1:T(2,128)S(1)}, u32[]{:S(2)}, u32[]{:S(2)}) collective-permute-start(s32[128,2]{0,1:T(2,128)} %bitcast.49), channel_id=1, source_target_pairs={{0,128},{128,0},{1,129},{129,1},{2,130},{130,2},{3,131},{131,3},{4... | collective-permute-start | bytes 3080 | tf_op jit(solution)/shard_map/ppermute | solution.py:51
  4.0 8.1 %copy-start.16 = (s32[1,128,1]{1,2,0:T(1,128)S(1)}, s32[1,128,1]{1,2,0:T(1,128)}, u32[]{:S(2)}) copy-start(s32[1,128,1]{1,2,0:T(1,128)} %param.12) | copy-start | bytes 1540
  4.0 8.3 %copy-start.15 = (s32[1,128]{1,0:T(1,128)S(1)}, s32[1,128]{1,0:T(1,128)}, u32[]{:S(2)}) copy-start(s32[1,128]{1,0:T(1,128)} %param.11) | copy-start | bytes 1540
  5.8 8.9 %collective-permute-start.1 = (f32[22,128,4]{1,2,0:T(4,128)S(1)}, f32[22,128,4]{1,2,0:T(4,128)S(1)}, u32[]{:S(2)}, u32[]{:S(2)}) collective-permute-start(f32[22,128,4]{1,2,0:T(4,128)S(1)} %copy.25), channel_id=1, source_target_pairs={{1,0},{2,1},{3,2},{4,3},{5,4},{6,5},{7,6},{9,8},{10,9},{11,10},{12... | collective-permute-start | bytes 135176 | tf_op jit(solution)/shard_map/ppermute | solution.py:25
  8.3 5.9 %collective-permute-start = (f32[22,128,4]{1,2,0:T(4,128)S(1)}, f32[22,128,4]{1,2,0:T(4,128)S(1)}, u32[]{:S(2)}, u32[]{:S(2)}) collective-permute-start(f32[22,128,4]{1,2,0:T(4,128)S(1)} %copy.24), channel_id=1, source_target_pairs={{0,1},{1,2},{2,3},{3,4},{4,5},{5,6},{6,7},{8,9},{9,10},{10,11},{11... | collective-permute-start | bytes 135176 | tf_op jit(solution)/shard_map/ppermute | solution.py:25
  12.6 2.6 %copy-start.14 = (f32[1,128,128]{2,1,0:T(8,128)S(1)}, f32[1,128,128]{2,1,0:T(8,128)}, u32[]{:S(2)}) copy-start(f32[1,128,128]{2,1,0:T(8,128)} %param.9) | copy-start | bytes 196612
  14.7 1.9 copy-start.1
  15.2 1.4 copy-start.2
  15.2 13.0 %copy-start.11 = (f32[1,10,128,128]{3,2,1,0:T(8,128)S(1)}, f32[1,10,128,128]{3,2,1,0:T(8,128)}, u32[]{:S(2)}) copy-start(f32[1,10,128,128]{3,2,1,0:T(8,128)} %param.8) | copy-start | bytes 1966084
  15.2 13.0 %copy-start.12 = (f32[1,10,128,128]{3,2,1,0:T(8,128)S(1)}, f32[1,10,128,128]{3,2,1,0:T(8,128)}, u32[]{:S(2)}) copy-start(f32[1,10,128,128]{3,2,1,0:T(8,128)} %param.7) | copy-start | bytes 1966084
  16.6 6.4 %collective-permute-start.2 = (f32[22,4,136]{2,1,0:T(4,128)S(1)}, f32[22,4,136]{2,1,0:T(4,128)S(1)}, u32[]{:S(2)}, u32[]{:S(2)}) collective-permute-start(f32[22,4,136]{2,1,0:T(4,128)S(1)} %get-tuple-element.5), channel_id=1, source_target_pairs={{0,8},{1,9},{2,10},{3,11},{4,12},{5,13},{6,14},{7,15},{8,16},{9,17... | collective-permute-start | bytes 143624 | tf_op jit(solution)/shard_map/ppermute | solution.py:25
  19.7 8.5 %collective-permute-start.3 = (f32[22,4,136]{2,1,0:T(4,128)S(1)}, f32[22,4,136]{2,1,0:T(4,128)S(1)}, u32[]{:S(2)}, u32[]{:S(2)}) collective-permute-start(f32[22,4,136]{2,1,0:T(4,128)S(1)} %get-tuple-element.6), channel_id=1, source_target_pairs={{8,0},{9,1},{10,2},{11,3},{12,4},{13,5},{14,6},{15,7},{16,8},{17,9... | collective-permute-start | bytes 143624 | tf_op jit(solution)/shard_map/ppermute | solution.py:25
  32.4 2.6 %copy-start.13 = (f32[10,136,136]{2,1,0:T(8,128)}, f32[10,136,136]{2,1,0:T(8,128)S(1)}, u32[]{:S(2)}) copy-start(f32[10,136,136]{2,1,0:T(8,128)S(1)} %get-tuple-element.7) | copy-start | bytes 2219524
  40.2 2.8 %copy-start.7 = (f32[8,8,10,256]{3,1,2,0:T(8,128)}, f32[8,8,10,256]{3,1,2,0:T(8,128)S(1)}, u32[]{:S(2)}) copy-start(f32[8,8,10,256]{3,1,2,0:T(8,128)S(1)} %copy.36) | copy-start | bytes 1966084
  40.2 2.8 %collective-permute-start.5 = (f32[64,2560]{1,0:T(8,128)S(1)}, f32[64,2560]{1,0:T(8,128)S(1)}, u32[]{:S(2)}, u32[]{:S(2)}) collective-permute-start(f32[64,2560]{1,0:T(8,128)S(1)} %bitcast.37), channel_id=1, source_target_pairs={{0,128},{128,0},{1,129},{129,1},{2,130},{130,2},{3,131},{131,3},{4... | collective-permute-start | bytes 1966088 | tf_op jit(solution)/shard_map/ppermute | solution.py:51
  41.8 2.7 %copy-start.5 = (f32[128,2560]{1,0:T(8,128)}, f32[128,2560]{1,0:T(8,128)S(1)}, u32[]{:S(2)}) copy-start(f32[128,2560]{1,0:T(8,128)S(1)} %fusion.43) | copy-start | bytes 3932164
  43.0 1.5 copy-start.3
  193.0 1.3 copy-start.4
  193.7 1.6 copy-start.6
  193.7 2.6 %collective-permute-start.6 = (f32[64,2560]{1,0:T(8,128)S(1)}, f32[64,2560]{1,0:T(8,128)S(1)}, u32[]{:S(2)}, u32[]{:S(2)}) collective-permute-start(f32[64,2560]{1,0:T(8,128)S(1)} %convolution_add_fusion.1), channel_id=1, source_target_pairs={{0,128},{128,0},{1,129},{129,1},{2,130},{130,2},{3,131},{131,3},{4... | collective-permute-start | bytes 1966088 | tf_op jit(solution)/shard_map/ppermute | solution.py:51
  195.3 1.1 copy-start.8
  207.8 7.2 %collective-permute-start.7 = (f32[10,128,4]{1,2,0:T(4,128)S(1)}, f32[10,128,4]{1,2,0:T(4,128)S(1)}, u32[]{:S(2)}, u32[]{:S(2)}) collective-permute-start(f32[10,128,4]{1,2,0:T(4,128)S(1)} %copy.31), channel_id=1, source_target_pairs={{0,1},{1,2},{2,3},{3,4},{4,5},{5,6},{6,7},{8,9},{9,10},{10,11},{11... | collective-permute-start | bytes 61448 | tf_op jit(solution)/shard_map/ppermute | solution.py:25
  211.7 5.7 %collective-permute-start.8 = (f32[10,128,4]{1,2,0:T(4,128)S(1)}, f32[10,128,4]{1,2,0:T(4,128)S(1)}, u32[]{:S(2)}, u32[]{:S(2)}) collective-permute-start(f32[10,128,4]{1,2,0:T(4,128)S(1)} %copy.32), channel_id=1, source_target_pairs={{1,0},{2,1},{3,2},{4,3},{5,4},{6,5},{7,6},{9,8},{10,9},{11,10},{12... | collective-permute-start | bytes 61448 | tf_op jit(solution)/shard_map/ppermute | solution.py:25
  218.5 13.8 %copy-start = (f32[10,128,128]{2,1,0:T(8,128)S(1)}, f32[10,128,128]{2,1,0:T(8,128)}, u32[]{:S(2)}) copy-start(f32[10,128,128]{2,1,0:T(8,128)} %reshape.28) | copy-start | bytes 1966084
  218.5 13.8 %copy-start.9 = (f32[10,128,4]{2,1,0:T(8,128)S(1)}, f32[10,128,4]{2,1,0:T(8,128)}, u32[]{:S(2)}) copy-start(f32[10,128,4]{2,1,0:T(8,128)} %copy.33) | copy-start | bytes 61444
  218.5 13.8 %copy-start.10 = (f32[10,128,4]{2,1,0:T(8,128)S(1)}, f32[10,128,4]{2,1,0:T(8,128)}, u32[]{:S(2)}) copy-start(f32[10,128,4]{2,1,0:T(8,128)} %copy.34) | copy-start | bytes 61444
  219.7 6.8 %collective-permute-start.9 = (f32[10,4,136]{2,1,0:T(4,128)S(1)}, f32[10,4,136]{2,1,0:T(4,128)S(1)}, u32[]{:S(2)}, u32[]{:S(2)}) collective-permute-start(f32[10,4,136]{2,1,0:T(4,128)S(1)} %get-tuple-element.11), channel_id=1, source_target_pairs={{0,8},{1,9},{2,10},{3,11},{4,12},{5,13},{6,14},{7,15},{8,16},{9,17... | collective-permute-start | bytes 65288 | tf_op jit(solution)/shard_map/ppermute | solution.py:25
  224.2 8.0 %collective-permute-start.10 = (f32[10,4,136]{2,1,0:T(4,128)S(1)}, f32[10,4,136]{2,1,0:T(4,128)S(1)}, u32[]{:S(2)}, u32[]{:S(2)}) collective-permute-start(f32[10,4,136]{2,1,0:T(4,128)S(1)} %get-tuple-element.12), channel_id=1, source_target_pairs={{8,0},{9,1},{10,2},{11,3},{12,4},{13,5},{14,6},{15,7},{16,8},{17,9... | collective-permute-start | bytes 65288 | tf_op jit(solution)/shard_map/ppermute | solution.py:25

commit v3 on v1

--- a/solution.py
+++ b/solution.py
@@ -26,22 +26,12 @@
 
 
 def halo(cells, w):
-    top, bot = cells[:, :w], cells[:, -w:]
-    left, right = cells[:, :, :w], cells[:, :, -w:]
-    north = shifted(bot, -1, 0)
-    south = shifted(top, 1, 0)
-    west = shifted(right, 0, -1)
-    east = shifted(left, 0, 1)
-    nw = shifted(cells[:, -w:, -w:], -1, -1)
-    ne = shifted(cells[:, -w:, :w], -1, 1)
-    sw = shifted(cells[:, :w, -w:], 1, -1)
-    se = shifted(cells[:, :w, :w], 1, 1)
-    rows = [
-        jnp.concatenate([nw, north, ne], axis=2),
-        jnp.concatenate([west, cells, east], axis=2),
-        jnp.concatenate([sw, south, se], axis=2),
-    ]
-    return jnp.concatenate(rows, axis=1)
+    west = shifted(cells[:, :, -w:], 0, -1)
+    east = shifted(cells[:, :, :w], 0, 1)
+    wide = jnp.concatenate([west, cells, east], axis=2)
+    north = shifted(wide[:, -w:], -1, 0)
+    south = shifted(wide[:, :w], 1, 0)
+    return jnp.concatenate([north, wide, south], axis=1)
 
 
 def relax(field, visc, invd, force):
@@ -73,13 +63,9 @@
     return jnp.einsum("jk,jlrc->lkrc", sel, values, precision=HIGHEST)
 
 
-def couple(x1, source_patch, owner, cavity_map):
-    levels, rows, cols = x1.shape
-    npatch = rows // PATCH
+def selectors(source_patch, owner, cavity_map, npatch):
     groups, slots_per = cavity_map.shape[2], cavity_map.shape[3]
     nslot = groups * slots_per
-    mine = x1.reshape(levels, npatch, PATCH, cols)
-    other = swap_sec(mine)
     sources = source_patch[0]
     dest = owner[0, :, 0]
     count = dest.shape[0]
@@ -89,12 +75,22 @@
     send_sel = jnp.dot(onehot(slot, nslot).T, onehot(sources, npatch), precision=HIGHEST)
     cav_other = swap_sec(cavity_map[0, 0].reshape(-1))
     recv_sel = onehot(cav_other, npatch)
+    return send_sel, recv_sel, groups, slots_per
+
+
+def couple(x1, sel):
+    send_sel, recv_sel, groups, slots_per = sel
+    levels, rows, cols = x1.shape
+    npatch = rows // PATCH
+    nslot = groups * slots_per
+    mine = x1.reshape(levels, npatch, PATCH, cols)
+    other = swap_sec(mine)
     sent = pick(send_sel, mine)
     local = pick(recv_sel, other)
-    chunk = (groups, slots_per * levels * PATCH, cols)
+    half = slots_per * levels * PATCH
+    chunk = (groups, half, cols)
     outgoing = jnp.concatenate([sent.reshape(chunk), local.reshape(chunk)], axis=1)
     incoming = lax.all_to_all(outgoing, ("gx", "gy"), 0, 0, tiled=True)
-    half = slots_per * levels * PATCH
     arrived = incoming[:, :half].reshape(nslot, levels, PATCH, cols)
     answer = incoming[:, half:].reshape(nslot, levels, PATCH, cols)
     for_other = spread(recv_sel, KAPPA * arrived)
@@ -105,7 +101,7 @@
 
 def body(adjoint_state, forcing, viscosity, reaction, source_patch, owner, cavity_map):
     w = SWEEPS // 2
-    levels = adjoint_state.shape[1]
+    levels, rows, cols = adjoint_state.shape[1:]
     invd = 1.0 / (4.0 * viscosity + reaction)
     stacked = jnp.concatenate([adjoint_state[0], forcing[0], viscosity, invd], axis=0)
     ext = halo(stacked, w)
@@ -113,8 +109,9 @@
     force = ext[levels:2 * levels]
     visc = ext[2 * levels:2 * levels + 1]
     inv_wide = ext[2 * levels + 1:]
+    sel = selectors(source_patch, owner, cavity_map, rows // PATCH)
     x1 = sweeps(field, visc, inv_wide, force, w, w)
-    x2 = couple(x1, source_patch, owner, cavity_map)
+    x2 = couple(x1, sel)
     out = sweeps(halo(x2, w), visc, inv_wide, force, SWEEPS - w, w)
     return out[None]
 

time: 258 us -> 221 us (0.86); the launches traced: 252 us -> 218 us
  starting transfers between devices: 59.4 us -> 24.8 us
  waiting for transfers between devices: 3.65 us -> 16.2 us
  local copies, waits for them, and re-layouts: 24.6 us -> 16.9 us
    ppermute x16 -> x8, starting transfers between devices: 58.8 us -> 24.1 us  [shifted(): return lax.ppermute(block, ('gx', 'gy'), pairs)]
    ppermute x16 -> x8, waiting for transfers between devices: 3.62 us -> 16.2 us  [shifted(): return lax.ppermute(block, ('gx', 'gy'), pairs)]
    concatenate x2, other arithmetic: 8.72 us -> 4.05 us  [halo(): return jnp.concatenate([north, wide, south], axis=1)]
    slice x8 -> x6, local copies, waits for them, and re-layouts: 11.7 us -> 7.75 us  [the longest x4 6.01 us: halo(): west = shifted(cells[:, :, -w:], 0, -1)]
    ppermute x4, local copies, waits for them, and re-layouts: 6.86 us -> 3.14 us  [shifted(): return lax.ppermute(block, ('gx', 'gy'), pairs)]
  transfers between devices with their start and end apart: 19 -> 11, of which waited for: 3 -> 5; matrix products, arithmetic and copies ran while one was open for 14% -> 9% of each run, Pallas kernels for 0% -> 0%
where the time goes in v3:
time: 221 us; the launch traced here: 218 us
  blocking collectives  132 us (60%)
  starting transfers between devices  24.8 us (11%)
  other arithmetic  21.1 us (10%)
  local copies, waits for them, and re-layouts  16.9 us (8%)
  waiting for transfers between devices  16.2 us (7%)
  matrix products  6.99 us (3%)
    all_to_all x1, blocking collectives, couple(): incoming = lax.all_to_all(outgoing, ('gx', 'gy'), 0, 0, tiled=True)  132 us
    ppermute x8, starting transfers between devices, shifted(): return lax.ppermute(block, ('gx', 'gy'), pairs)  24.1 us
    ppermute x8, waiting for transfers between devices, shifted(): return lax.ppermute(block, ('gx', 'gy'), pairs)  16.2 us
    slice x4, local copies, waits for them, and re-layouts, halo(): west = shifted(cells[:, :, -w:], 0, -1)  6.01 us
    add x6, other arithmetic, relax(): return (1.0 - OMEGA) * field + OMEGA * invd * (force + visc * beside)  5.14 us
  transfers between devices with their start and end apart: 11, of which 5 were waited for; matrix products, arithmetic and copies ran while one was open for 9% of the time, Pallas kernels for 0%

profile of v3, /device:TPU:54, one launch (start us, length us, event | category | flops | bytes accessed | tf_op | source)
XLA Modules:
  0.0 218.3 jit_solution(16750449026557625206)
XLA Ops:
  0.9 1.5 pad_maximum_fusion.2
  2.4 1.6 fusion.30
  4.0 1.8 copy.34
  5.8 3.8 %collective-permute-start = (f32[22,128,4]{1,2,0:T(4,128)S(1)}, f32[22,128,4]{1,2,0:T(4,128)S(1)}, u32[]{:S(2)}, u32[]{:S(2)}) collective-permute-start(f32[22,128,4]{1,2,0:T(4,128)S(1)} %copy.34), channel_id=1, source_target_pairs={{0,1},{1,2},{2,3},{3,4},{4,5},{5,6},{6,7},{8,9},{9,10},{10,11},{11... | collective-permute-start | bytes 135176 | tf_op jit(solution)/shard_map/ppermute | solution.py:25
  10.1 2.1 collective-permute-start.1
  12.7 3.4 %collective-permute-done.1 = f32[22,128,4]{1,2,0:T(4,128)S(1)} collective-permute-done((f32[22,128,4]{1,2,0:T(4,128)S(1)}, f32[22,128,4]{1,2,0:T(4,128)S(1)}, u32[]{:S(2)}, u32[]{:S(2)}) %collective-permute-start.1) | collective-permute-done | bytes 45088 | tf_op jit(solution)/shard_map/ppermute | solution.py:25
  16.7 1.3 pad_maximum_fusion.9
  18.0 3.1 %collective-permute-start.2 = (f32[22,4,136]{2,1,0:T(4,128)S(1)}, f32[22,4,136]{2,1,0:T(4,128)S(1)}, u32[]{:S(2)}, u32[]{:S(2)}) collective-permute-start(f32[22,4,136]{2,1,0:T(4,128)S(1)} %get-tuple-element.7), channel_id=1, source_target_pairs={{0,8},{1,9},{2,10},{3,11},{4,12},{5,13},{6,14},{7,15},{8,16},{9,17... | collective-permute-start | bytes 143624 | tf_op jit(solution)/shard_map/ppermute | solution.py:25
  21.1 2.7 %collective-permute-start.3 = (f32[22,4,136]{2,1,0:T(4,128)S(1)}, f32[22,4,136]{2,1,0:T(4,128)S(1)}, u32[]{:S(2)}, u32[]{:S(2)}) collective-permute-start(f32[22,4,136]{2,1,0:T(4,128)S(1)} %get-tuple-element.8), channel_id=1, source_target_pairs={{8,0},{9,1},{10,2},{11,3},{12,4},{13,5},{14,6},{15,7},{16,8},{17,9... | collective-permute-start | bytes 143624 | tf_op jit(solution)/shard_map/ppermute | solution.py:25
  24.4 5.2 %collective-permute-done.3 = f32[22,4,136]{2,1,0:T(4,128)S(1)} collective-permute-done((f32[22,4,136]{2,1,0:T(4,128)S(1)}, f32[22,4,136]{2,1,0:T(4,128)S(1)}, u32[]{:S(2)}, u32[]{:S(2)}) %collective-permute-start.3) | collective-permute-done | bytes 47904 | tf_op jit(solution)/shard_map/ppermute | solution.py:25
  29.6 3.4 %pad_maximum_fusion.1 = f32[22,136,136]{2,1,0:T(8,128)S(1)} fusion(f32[22,4,136]{2,1,0:T(4,128)S(1)} %collective-permute-done.3, f32[22,128,4]{2,1,0:T(8,128)} %copy-done.3, f32[1,128,128]{2,1,0:T(8,128)S(1)} %add_divide_fusion, f32[1,128,128]{2,1,0:T(8,128)S(1)} %copy-done.7, f32[10,128,128]{2,1,0:T(8,128)} %bitcast.48, f32[10,128,128]{2,1,0:T(8,128)} %bitcast.51, ...), kind=kLoop, calls=%fused_computation.1 | loop fusion | flops 2848384 | bytes 3255296 | tf_op jit(solution)/shard_map/concatenate | solution.py:34
  36.9 1.1 fusion.13
  38.8 2.3 %fusion.27 = f32[256,10,2,128]{3,0,2,1:T(8,128)S(1)} fusion(f32[256,64,1,1]{0,1,3,2:T(8,128)S(1)} %convolution_bitcast_fusion, f32[10,64,2,128]{3,2,1,0:T(2,128)S(1)} %bitcast.40), kind=kOutput, calls=%fused_computation.73 | convolution fusion | flops 503316480 | bytes 3342336 | tf_op jit(solution)/shard_map/jk,lkrc->jlrc/dot_general | solution.py:59
  41.0 2.0 copy.39
  43.1 1.2 fusion.22
  44.3 2.0 copy.42
  46.8 131.8 %all_to_all.5 = f32[128,80,128]{2,1,0:T(8,128)S(1)} all-to-all(f32[128,80,128]{2,1,0:T(8,128)S(1)} %pad_maximum_fusion), channel_id=1, replica_groups=mesh['sec'=2,'gx'=16,'gy'=8] {'gx','gy'}, dimensions={0} | all-to-all | bytes 10485760 | tf_op jit(solution)/shard_map/all_to_all | solution.py:93
  178.9 1.2 fusion.5
  180.4 2.1 fusion.4
  184.0 1.3 fusion.31
  185.2 1.3 copy.47
  186.5 2.6 %collective-permute-start.7 = (f32[10,128,4]{1,2,0:T(4,128)S(1)}, f32[10,128,4]{1,2,0:T(4,128)S(1)}, u32[]{:S(2)}, u32[]{:S(2)}) collective-permute-start(f32[10,128,4]{1,2,0:T(4,128)S(1)} %copy.47), channel_id=1, source_target_pairs={{0,1},{1,2},{2,3},{3,4},{4,5},{5,6},{6,7},{8,9},{9,10},{10,11},{11... | collective-permute-start | bytes 61448 | tf_op jit(solution)/shard_map/ppermute | solution.py:25
  189.1 1.3 copy.48
  190.5 3.2 %collective-permute-start.8 = (f32[10,128,4]{1,2,0:T(4,128)S(1)}, f32[10,128,4]{1,2,0:T(4,128)S(1)}, u32[]{:S(2)}, u32[]{:S(2)}) collective-permute-start(f32[10,128,4]{1,2,0:T(4,128)S(1)} %copy.48), channel_id=1, source_target_pairs={{1,0},{2,1},{3,2},{4,3},{5,4},{6,5},{7,6},{9,8},{10,9},{11,10},{12... | collective-permute-start | bytes 61448 | tf_op jit(solution)/shard_map/ppermute | solution.py:25
  193.7 1.1 copy.49
  194.8 1.3 collective-permute-done.8
  196.1 1.1 copy.50
  197.2 1.2 pad_maximum_fusion.12
  198.4 4.6 %collective-permute-start.9 = (f32[10,4,136]{2,1,0:T(4,128)S(1)}, f32[10,4,136]{2,1,0:T(4,128)S(1)}, u32[]{:S(2)}, u32[]{:S(2)}) collective-permute-start(f32[10,4,136]{2,1,0:T(4,128)S(1)} %get-tuple-element.13), channel_id=1, source_target_pairs={{0,8},{1,9},{2,10},{3,11},{4,12},{5,13},{6,14},{7,15},{8,16},{9,17... | collective-permute-start | bytes 65288 | tf_op jit(solution)/shard_map/ppermute | solution.py:25
  203.0 1.9 collective-permute-start.10
  204.9 6.1 %collective-permute-done.10 = f32[10,4,136]{2,1,0:T(4,128)S(1)} collective-permute-done((f32[10,4,136]{2,1,0:T(4,128)S(1)}, f32[10,4,136]{2,1,0:T(4,128)S(1)}, u32[]{:S(2)}, u32[]{:S(2)}) %collective-permute-start.10) | collective-permute-done | bytes 21792 | tf_op jit(solution)/shard_map/ppermute | solution.py:25
  215.0 3.3 %fusion.9 = f32[1,10,128,128]{3,2,1,0:T(8,128)} fusion(f32[10,136,136]{2,1,0:T(8,128)S(1)} %multiply_add_fusion, f32[10,136,136]{2,1,0:T(8,128)S(1)} %get-tuple-element.19, f32[10,136,136]{2,1,0:T(8,128)S(1)} %get-tuple-element.18, f32[10,136,136]{2,1,0:T(8,128)S(1)} %get-tuple-element.17, f32[10,136,136]{2,1,0:T(8,128)} %copy-done.6, ...), kind=kLoop, calls=%fused_computation.33 | loop fusion | flops 1146880 | bytes 4063232 | tf_op jit(solution)/shard_map/broadcast_in_dim | solution.py:116
  (59 shorter events, 13.9 us)
Async XLA Ops:
  5.8 6.4 %collective-permute-start = (f32[22,128,4]{1,2,0:T(4,128)S(1)}, f32[22,128,4]{1,2,0:T(4,128)S(1)}, u32[]{:S(2)}, u32[]{:S(2)}) collective-permute-start(f32[22,128,4]{1,2,0:T(4,128)S(1)} %copy.34), channel_id=1, source_target_pairs={{0,1},{1,2},{2,3},{3,4},{4,5},{5,6},{6,7},{8,9},{9,10},{10,11},{11... | collective-permute-start | bytes 135176 | tf_op jit(solution)/shard_map/ppermute | solution.py:25
  10.1 6.5 %copy-start.7 = (f32[1,128,128]{2,1,0:T(8,128)S(1)}, f32[1,128,128]{2,1,0:T(8,128)}, u32[]{:S(2)}) copy-start(f32[1,128,128]{2,1,0:T(8,128)} %param.9) | copy-start | bytes 196612
  10.1 6.1 %collective-permute-start.1 = (f32[22,128,4]{1,2,0:T(4,128)S(1)}, f32[22,128,4]{1,2,0:T(4,128)S(1)}, u32[]{:S(2)}, u32[]{:S(2)}) collective-permute-start(f32[22,128,4]{1,2,0:T(4,128)S(1)} %copy.35), channel_id=1, source_target_pairs={{1,0},{2,1},{3,2},{4,3},{5,4},{6,5},{7,6},{9,8},{10,9},{11,10},{12... | collective-permute-start | bytes 135176 | tf_op jit(solution)/shard_map/ppermute | solution.py:25
  12.7 5.2 %copy-start.2 = (f32[22,128,4]{2,1,0:T(8,128)}, f32[22,128,4]{2,1,0:T(8,128)S(1)}, u32[]{:S(2)}) copy-start(f32[22,128,4]{2,1,0:T(8,128)S(1)} %copy.36) | copy-start | bytes 135172
  16.6 1.3 copy-start.3
  16.6 7.2 %copy-start.8 = (s32[1,1,128,2]{2,3,1,0:T(2,128)S(1)}, s32[1,1,128,2]{2,3,1,0:T(2,128)}, u32[]{:S(2)}) copy-start(s32[1,1,128,2]{2,3,1,0:T(2,128)} %param.13) | copy-start | bytes 3076
  18.0 6.4 %collective-permute-start.2 = (f32[22,4,136]{2,1,0:T(4,128)S(1)}, f32[22,4,136]{2,1,0:T(4,128)S(1)}, u32[]{:S(2)}, u32[]{:S(2)}) collective-permute-start(f32[22,4,136]{2,1,0:T(4,128)S(1)} %get-tuple-element.7), channel_id=1, source_target_pairs={{0,8},{1,9},{2,10},{3,11},{4,12},{5,13},{6,14},{7,15},{8,16},{9,17... | collective-permute-start | bytes 143624 | tf_op jit(solution)/shard_map/ppermute | solution.py:25
  21.1 8.5 %collective-permute-start.3 = (f32[22,4,136]{2,1,0:T(4,128)S(1)}, f32[22,4,136]{2,1,0:T(4,128)S(1)}, u32[]{:S(2)}, u32[]{:S(2)}) collective-permute-start(f32[22,4,136]{2,1,0:T(4,128)S(1)} %get-tuple-element.8), channel_id=1, source_target_pairs={{8,0},{9,1},{10,2},{11,3},{12,4},{13,5},{14,6},{15,7},{16,8},{17,9... | collective-permute-start | bytes 143624 | tf_op jit(solution)/shard_map/ppermute | solution.py:25
  24.1 19.0 %collective-permute-start.4 = (s32[256]{0:T(256)S(1)}, s32[256]{0:T(256)S(1)}, u32[]{:S(2)}, u32[]{:S(2)}) collective-permute-start(s32[256]{0:T(256)S(1)} %reshape_squeeze.3), channel_id=1, source_target_pairs={{0,128},{128,0},{1,129},{129,1},{2,130},{130,2},{3,131},{131,3},{4... | collective-permute-start | bytes 3080 | tf_op jit(solution)/shard_map/ppermute | solution.py:51
  34.2 2.6 %copy-start.6 = (f32[10,136,136]{2,1,0:T(8,128)}, f32[10,136,136]{2,1,0:T(8,128)S(1)}, u32[]{:S(2)}) copy-start(f32[10,136,136]{2,1,0:T(8,128)S(1)} %get-tuple-element.9) | copy-start | bytes 2219524
  36.8 1.5 copy-start.9
  36.8 1.6 copy-start.10
  38.0 5.1 %collective-permute-start.5 = (f32[10,64,2,128]{3,1,2,0:T(8,128)S(1)}, f32[10,64,2,128]{3,1,2,0:T(8,128)S(1)}, u32[]{:S(2)}, u32[]{:S(2)}) collective-permute-start(f32[10,64,2,128]{3,1,2,0:T(8,128)S(1)} %copy.44), channel_id=1, source_target_pairs={{0,128},{128,0},{1,129},{129,1},{2,130},{130,2},{3,131},{131,3},{4... | collective-permute-start | bytes 1966088 | tf_op jit(solution)/shard_map/ppermute | solution.py:51
  180.0 2.4 %collective-permute-start.6 = (f32[10,64,2,128]{3,1,2,0:T(8,128)S(1)}, f32[10,64,2,128]{3,1,2,0:T(8,128)S(1)}, u32[]{:S(2)}, u32[]{:S(2)}) collective-permute-start(f32[10,64,2,128]{3,1,2,0:T(8,128)S(1)} %fusion.5), channel_id=1, source_target_pairs={{0,128},{128,0},{1,129},{129,1},{2,130},{130,2},{3,131},{131,3},{4... | collective-permute-start | bytes 1966088 | tf_op jit(solution)/shard_map/ppermute | solution.py:51
  183.1 0.8 copy-start
  186.5 7.2 %collective-permute-start.7 = (f32[10,128,4]{1,2,0:T(4,128)S(1)}, f32[10,128,4]{1,2,0:T(4,128)S(1)}, u32[]{:S(2)}, u32[]{:S(2)}) collective-permute-start(f32[10,128,4]{1,2,0:T(4,128)S(1)} %copy.47), channel_id=1, source_target_pairs={{0,1},{1,2},{2,3},{3,4},{4,5},{5,6},{6,7},{8,9},{9,10},{10,11},{11... | collective-permute-start | bytes 61448 | tf_op jit(solution)/shard_map/ppermute | solution.py:25
  190.5 5.7 %collective-permute-start.8 = (f32[10,128,4]{1,2,0:T(4,128)S(1)}, f32[10,128,4]{1,2,0:T(4,128)S(1)}, u32[]{:S(2)}, u32[]{:S(2)}) collective-permute-start(f32[10,128,4]{1,2,0:T(4,128)S(1)} %copy.48), channel_id=1, source_target_pairs={{1,0},{2,1},{3,2},{4,3},{5,4},{6,5},{7,6},{9,8},{10,9},{11,10},{12... | collective-permute-start | bytes 61448 | tf_op jit(solution)/shard_map/ppermute | solution.py:25
  197.2 13.8 %copy-start.1 = (f32[10,64,2,128]{3,2,1,0:T(2,128)S(1)}, f32[10,64,2,128]{3,2,1,0:T(2,128)}, u32[]{:S(2)}) copy-start(f32[10,64,2,128]{3,2,1,0:T(2,128)} %copy-done) | copy-start | bytes 1966084
  197.2 13.8 %copy-start.4 = (f32[10,128,4]{2,1,0:T(8,128)S(1)}, f32[10,128,4]{2,1,0:T(8,128)}, u32[]{:S(2)}) copy-start(f32[10,128,4]{2,1,0:T(8,128)} %copy.49) | copy-start | bytes 61444
  197.2 13.8 %copy-start.5 = (f32[10,128,4]{2,1,0:T(8,128)S(1)}, f32[10,128,4]{2,1,0:T(8,128)}, u32[]{:S(2)}) copy-start(f32[10,128,4]{2,1,0:T(8,128)} %copy.50) | copy-start | bytes 61444
  198.4 6.5 %collective-permute-start.9 = (f32[10,4,136]{2,1,0:T(4,128)S(1)}, f32[10,4,136]{2,1,0:T(4,128)S(1)}, u32[]{:S(2)}, u32[]{:S(2)}) collective-permute-start(f32[10,4,136]{2,1,0:T(4,128)S(1)} %get-tuple-element.13), channel_id=1, source_target_pairs={{0,8},{1,9},{2,10},{3,11},{4,12},{5,13},{6,14},{7,15},{8,16},{9,17... | collective-permute-start | bytes 65288 | tf_op jit(solution)/shard_map/ppermute | solution.py:25
  203.0 8.0 %collective-permute-start.10 = (f32[10,4,136]{2,1,0:T(4,128)S(1)}, f32[10,4,136]{2,1,0:T(4,128)S(1)}, u32[]{:S(2)}, u32[]{:S(2)}) collective-permute-start(f32[10,4,136]{2,1,0:T(4,128)S(1)} %get-tuple-element.14), channel_id=1, source_target_pairs={{8,0},{9,1},{10,2},{11,3},{12,4},{13,5},{14,6},{15,7},{16,8},{17,9... | collective-permute-start | bytes 65288 | tf_op jit(solution)/shard_map/ppermute | solution.py:25

commit v4 on v3

--- a/solution.py
+++ b/solution.py
@@ -2,6 +2,8 @@
 import jax.numpy as jnp
 from jax import lax
 from jax.sharding import PartitionSpec as P
+from jax.experimental import pallas as pl
+from jax.experimental.pallas import tpu as pltpu
 
 PATCH = 2
 PW = 128
@@ -26,25 +28,38 @@
 
 
 def halo(cells, w):
+    chans, rows, cols = cells.shape
     west = shifted(cells[:, :, -w:], 0, -1)
     east = shifted(cells[:, :, :w], 0, 1)
-    wide = jnp.concatenate([west, cells, east], axis=2)
+    gap = jnp.zeros((chans, rows, cols - 2 * w), cells.dtype)
+    wide = jnp.concatenate([cells, east, gap, west], axis=2)
     north = shifted(wide[:, -w:], -1, 0)
     south = shifted(wide[:, :w], 1, 0)
-    return jnp.concatenate([north, wide, south], axis=1)
+    return jnp.concatenate([wide, south, north], axis=1)
 
 
-def relax(field, visc, invd, force):
-    padded = jnp.pad(field, ((0, 0), (1, 1), (1, 1)))
-    beside = padded[:, 2:, 1:-1] + padded[:, :-2, 1:-1]
-    beside = beside + padded[:, 1:-1, 2:] + padded[:, 1:-1, :-2]
-    return (1.0 - OMEGA) * field + OMEGA * invd * (force + visc * beside)
+def sweeps(ext, visc, invd, force, count, rows, cols):
+    levels, height, lanes = ext.shape
 
+    def kernel(x_ref, v_ref, i_ref, f_ref, o_ref):
+        v = v_ref[0]
+        inv = i_ref[0]
 
-def sweeps(ext, visc, invd, force, count, w):
-    for _ in range(count):
-        ext = relax(ext, visc, invd, force)
-    return ext[:, w:-w, w:-w]
+        def level(l, carry):
+            x = x_ref[l]
+            f = f_ref[l]
+            for _ in range(count):
+                beside = pltpu.roll(x, 1, 0) + pltpu.roll(x, height - 1, 0)
+                beside = beside + pltpu.roll(x, 1, 1) + pltpu.roll(x, lanes - 1, 1)
+                x = (1.0 - OMEGA) * x + OMEGA * inv * (f + v * beside)
+            o_ref[l] = x[:rows, :cols]
+            return carry
+
+        lax.fori_loop(0, levels, level, 0)
+
+    return pl.pallas_call(
+        kernel, out_shape=jax.ShapeDtypeStruct((levels, rows, cols), jnp.float32)
+    )(ext, visc, invd, force)
 
 
 def swap_sec(x):
@@ -110,9 +125,9 @@
     visc = ext[2 * levels:2 * levels + 1]
     inv_wide = ext[2 * levels + 1:]
     sel = selectors(source_patch, owner, cavity_map, rows // PATCH)
-    x1 = sweeps(field, visc, inv_wide, force, w, w)
+    x1 = sweeps(field, visc, inv_wide, force, w, rows, cols)
     x2 = couple(x1, sel)
-    out = sweeps(halo(x2, w), visc, inv_wide, force, SWEEPS - w, w)
+    out = sweeps(halo(x2, w), visc, inv_wide, force, SWEEPS - w, rows, cols)
     return out[None]
 
 

time: 221 us -> 224 us (1.014)
  Pallas kernels: 0 us -> 17.1 us
  other arithmetic: 21.1 us -> 9.42 us
  waiting for transfers between devices: 16.2 us -> 11.3 us
  starting transfers between devices: 24.8 us -> 27.5 us
    pallas_call x0 -> x2, Pallas kernels: none -> 17.1 us  [sweeps(): pl.pallas_call(kernel, out_shape=jax.ShapeDtypeStruct((levels, rows, cols...]
    add x8 -> x0, other arithmetic: 7.05 us -> none  [the longest x6 5.14 us: relax(): return (1.0 - OMEGA) * field + OMEGA * invd * (force + visc * beside)]
    slice x4 -> x2, local copies, waits for them, and re-layouts: 6.01 us -> 0.66 us  [halo(): west = shifted(cells[:, :, -w:], 0, -1)]
    ppermute x8, waiting for transfers between devices: 16.2 us -> 11.3 us  [shifted(): return lax.ppermute(block, ('gx', 'gy'), pairs)]
    broadcast_in_dim x1 -> x0, other arithmetic: 3.27 us -> none  [body(): return out[None]]
    ppermute x8, starting transfers between devices: 24.1 us -> 26.8 us  [shifted(): return lax.ppermute(block, ('gx', 'gy'), pairs)]
    all_to_all x1, blocking collectives: 132 us -> 134 us  [couple(): incoming = lax.all_to_all(outgoing, ('gx', 'gy'), 0, 0, tiled=True)]
  transfers between devices with their start and end apart: 11 -> 11, of which waited for: 5 -> 4; matrix products, arithmetic and copies ran while one was open for 9% -> 8% of each run, Pallas kernels for 0% -> 4%
where the time goes in v4:
time: 224 us; the launch traced here: 223 us
  blocking collectives  134 us (60%)
  starting transfers between devices  27.5 us (12%)
  Pallas kernels  17.1 us (8%)
  local copies, waits for them, and re-layouts  15.7 us (7%)
  waiting for transfers between devices  11.3 us (5%)
  other arithmetic  9.42 us (4%)
  matrix products  8.08 us (4%)
    all_to_all x1, blocking collectives, couple(): incoming = lax.all_to_all(outgoing, ('gx', 'gy'), 0, 0, tiled=True)  134 us
    ppermute x8, starting transfers between devices, shifted(): return lax.ppermute(block, ('gx', 'gy'), pairs)  26.8 us
    pallas_call x2, Pallas kernels, sweeps(): pl.pallas_call(kernel, out_shape=jax.ShapeDtypeStruct((levels, rows, cols...  17.1 us
    ppermute x8, waiting for transfers between devices, shifted(): return lax.ppermute(block, ('gx', 'gy'), pairs)  11.3 us
    dot_general x2, matrix products, pick(): return jnp.einsum('jk,lkrc->jlrc', sel, patches, precision=HIGHEST)  4.6 us
  transfers between devices with their start and end apart: 11, of which 4 were waited for; matrix products, arithmetic and copies ran while one was open for 8% of the time, Pallas kernels for 4%

profile of v4, /device:TPU:54, one launch (start us, length us, event | category | flops | bytes accessed | tf_op | source)
XLA Modules:
  0.0 223.5 jit_solution(1358072000305857961)
XLA Ops:
  0.0 0.9 add_divide_fusion
  1.5 1.4 pad_maximum_fusion.2
  3.5 1.1 copy.38
  4.5 2.0 collective-permute-start
  7.0 3.8 %collective-permute-start.1 = (f32[22,128,4]{1,2,0:T(4,128)S(1)}, f32[22,128,4]{1,2,0:T(4,128)}, u32[]{:S(2)}, u32[]{:S(2)}) collective-permute-start(f32[22,128,4]{1,2,0:T(4,128)S(1)} %copy.39), channel_id=1, source_target_pairs={{0,1},{1,2},{2,3},{3,4},{4,5},{5,6},{6,7},{8,9},{9,10},{10,11},{11... | collective-permute-start | bytes 135176 | tf_op jit(solution)/shard_map/ppermute | solution.py:27
  11.3 1.7 collective-permute-done.1
  13.1 1.2 copy.41
  14.5 1.9 pad_maximum_fusion.10
  16.4 2.7 %collective-permute-start.2 = (f32[22,4,256]{2,1,0:T(4,128)}, f32[22,4,256]{2,1,0:T(4,128)}, u32[]{:S(2)}, u32[]{:S(2)}) collective-permute-start(f32[22,4,256]{2,1,0:T(4,128)} %get-tuple-element.5), channel_id=1, source_target_pairs={{8,0},{9,1},{10,2},{11,3},{12,4},{13,5},{14,6},{15,7},{16,8},{17,9... | collective-permute-start | bytes 270344 | tf_op jit(solution)/shard_map/ppermute | solution.py:27
  19.1 5.2 %collective-permute-start.3 = (f32[22,4,256]{2,1,0:T(4,128)}, f32[22,4,256]{2,1,0:T(4,128)}, u32[]{:S(2)}, u32[]{:S(2)}) collective-permute-start(f32[22,4,256]{2,1,0:T(4,128)} %get-tuple-element.6), channel_id=1, source_target_pairs={{0,8},{1,9},{2,10},{3,11},{4,12},{5,13},{6,14},{7,15},{8,16},{9,17... | collective-permute-start | bytes 270344 | tf_op jit(solution)/shard_map/ppermute | solution.py:27
  24.4 0.7 copy.44
  25.1 1.0 reshape_squeeze.3
  26.8 2.5 %pad_maximum_fusion.1 = f32[22,136,256]{2,1,0:T(8,128)S(1)} fusion(f32[22,4,256]{2,1,0:T(4,128)} %collective-permute-done.3, f32[22,4,256]{2,1,0:T(4,128)} %collective-permute-done.2, f32[22,128,4]{2,1,0:T(8,128)S(1)} %copy.41, f32[22,128,120]{2,1,0:T(8,128)} %copy-done, f32[22,128,4]{2,1,0:T(8,128)S(1)} %copy.40, f32[1,128,128]{2,1,0:T(8,128)} %copy-done.3, ...), kind=kLoop, calls=%fused_computation.1 | loop fusion | flops 6127616 | bytes 6127616 | tf_op jit(solution)/shard_map/concatenate | solution.py:38
  29.3 1.8 fusion.19
  31.1 0.7 fusion.20
  31.8 8.5 %shard_map.73 = f32[10,128,128]{2,1,0:T(8,128)} custom-call(f32[10,136,256]{2,1,0:T(8,128)} %get-tuple-element.10.x_ref, f32[1,136,256]{2,1,0:T(8,128)} %get-tuple-element.12.v_ref, f32[1,136,256]{2,1,0:T(8,128)} %get-tuple-element.11.i_ref, f32[10,136,256]{2,1,0:T(8,128)} %get-tuple-element.9.f_ref), custom_call_target="tpu_custom_call" | custom-call | tf_op jit(solution)/shard_map/pallas_call | solution.py:60
  40.4 1.1 copy.48
  42.3 3.4 %fusion.17 = f32[256,10,2,128]{3,0,2,1:T(8,128)S(1)} fusion(f32[256,64,1,1]{0,1,3,2:T(8,128)S(1)} %convolution_bitcast_fusion, f32[10,64,2,128]{3,2,1,0:T(2,128)} %bitcast.35), kind=kOutput, calls=%fused_computation.39 | convolution fusion | flops 503316480 | bytes 3342336 | tf_op jit(solution)/shard_map/jk,lkrc->jlrc/dot_general | solution.py:74
  45.6 2.0 copy.43
  47.7 1.2 fusion.12
  48.9 2.0 copy.46
  51.4 134.1 %all_to_all.5 = f32[128,80,128]{2,1,0:T(8,128)S(1)} all-to-all(f32[128,80,128]{2,1,0:T(8,128)S(1)} %pad_maximum_fusion), channel_id=1, replica_groups=mesh['sec'=2,'gx'=16,'gy'=8] {'gx','gy'}, dimensions={0} | all-to-all | bytes 10485760 | tf_op jit(solution)/shard_map/all_to_all | solution.py:108
  185.8 1.2 fusion.5
  187.3 2.1 fusion.4
  190.5 3.4 %collective-permute-start.7 = (f32[10,128,4]{1,2,0:T(4,128)S(1)}, f32[10,128,4]{1,2,0:T(4,128)S(1)}, u32[]{:S(2)}, u32[]{:S(2)}) collective-permute-start(f32[10,128,4]{1,2,0:T(4,128)S(1)} %copy.51), channel_id=1, source_target_pairs={{1,0},{2,1},{3,2},{4,3},{5,4},{6,5},{7,6},{9,8},{10,9},{11,10},{12... | collective-permute-start | bytes 61448 | tf_op jit(solution)/shard_map/ppermute | solution.py:27
  194.1 2.5 %collective-permute-start.8 = (f32[10,128,4]{1,2,0:T(4,128)S(1)}, f32[10,128,4]{1,2,0:T(4,128)S(1)}, u32[]{:S(2)}, u32[]{:S(2)}) collective-permute-start(f32[10,128,4]{1,2,0:T(4,128)S(1)} %copy.52), channel_id=1, source_target_pairs={{0,1},{1,2},{2,3},{3,4},{4,5},{5,6},{6,7},{8,9},{9,10},{10,11},{11... | collective-permute-start | bytes 61448 | tf_op jit(solution)/shard_map/ppermute | solution.py:27
  196.8 2.9 %collective-permute-done.8 = f32[10,128,4]{1,2,0:T(4,128)S(1)} collective-permute-done((f32[10,128,4]{1,2,0:T(4,128)S(1)}, f32[10,128,4]{1,2,0:T(4,128)S(1)}, u32[]{:S(2)}, u32[]{:S(2)}) %collective-permute-start.8) | collective-permute-done | bytes 20512 | tf_op jit(solution)/shard_map/ppermute | solution.py:27
  200.2 5.2 %collective-permute-start.10 = (f32[10,4,256]{2,1,0:T(4,128)S(1)}, f32[10,4,256]{2,1,0:T(4,128)S(1)}, u32[]{:S(2)}, u32[]{:S(2)}) collective-permute-start(f32[10,4,256]{2,1,0:T(4,128)S(1)} %get-tuple-element.14), channel_id=1, source_target_pairs={{0,8},{1,9},{2,10},{3,11},{4,12},{5,13},{6,14},{7,15},{8,16},{9,17... | collective-permute-start | bytes 122888 | tf_op jit(solution)/shard_map/ppermute | solution.py:27
  205.4 1.9 collective-permute-start.9
  207.4 6.1 %collective-permute-done.9 = f32[10,4,256]{2,1,0:T(4,128)S(1)} collective-permute-done((f32[10,4,256]{2,1,0:T(4,128)S(1)}, f32[10,4,256]{2,1,0:T(4,128)S(1)}, u32[]{:S(2)}, u32[]{:S(2)}) %collective-permute-start.9) | collective-permute-done | bytes 40992 | tf_op jit(solution)/shard_map/ppermute | solution.py:27
  213.4 1.5 pad_maximum_fusion.3.x_ref
  215.0 8.5 %shard_map.74 = f32[10,128,128]{2,1,0:T(8,128)} custom-call(f32[10,136,256]{2,1,0:T(8,128)} %pad_maximum_fusion.3.x_ref, f32[1,136,256]{2,1,0:T(8,128)} %get-tuple-element.12.v_ref, f32[1,136,256]{2,1,0:T(8,128)} %get-tuple-element.11.i_ref, f32[10,136,256]{2,1,0:T(8,128)} %get-tuple-element.9.f_ref), custom_call_target="tpu_custom_call" | custom-call | tf_op jit(solution)/shard_map/pallas_call | solution.py:60
  (43 shorter events, 6.7 us)
Async XLA Ops:
  0.9 0.6 copy-start.3
  4.5 6.3 %collective-permute-start = (f32[22,128,4]{1,2,0:T(4,128)}, f32[22,128,4]{1,2,0:T(4,128)S(1)}, u32[]{:S(2)}, u32[]{:S(2)}) collective-permute-start(f32[22,128,4]{1,2,0:T(4,128)} %copy.38), channel_id=1, source_target_pairs={{1,0},{2,1},{3,2},{4,3},{5,4},{6,5},{7,6},{9,8},{10,9},{11,10},{12... | collective-permute-start | bytes 135176 | tf_op jit(solution)/shard_map/ppermute | solution.py:27
  6.6 7.9 %copy-start.2 = (f32[1,10,128,128]{3,2,1,0:T(8,128)S(1)}, f32[1,10,128,128]{3,2,1,0:T(8,128)}, u32[]{:S(2)}) copy-start(f32[1,10,128,128]{3,2,1,0:T(8,128)} %param.8) | copy-start | bytes 1966084
  7.0 6.0 %collective-permute-start.1 = (f32[22,128,4]{1,2,0:T(4,128)S(1)}, f32[22,128,4]{1,2,0:T(4,128)}, u32[]{:S(2)}, u32[]{:S(2)}) collective-permute-start(f32[22,128,4]{1,2,0:T(4,128)S(1)} %copy.39), channel_id=1, source_target_pairs={{0,1},{1,2},{2,3},{3,4},{4,5},{5,6},{6,7},{8,9},{9,10},{10,11},{11... | collective-permute-start | bytes 135176 | tf_op jit(solution)/shard_map/ppermute | solution.py:27
  14.5 1.9 copy-start
  14.5 9.9 %copy-start.4 = (s32[1,1,128,2]{2,3,1,0:T(2,128)S(1)}, s32[1,1,128,2]{2,3,1,0:T(2,128)}, u32[]{:S(2)}) copy-start(s32[1,1,128,2]{2,3,1,0:T(2,128)} %param.13) | copy-start | bytes 3076
  16.4 9.8 %collective-permute-start.2 = (f32[22,4,256]{2,1,0:T(4,128)}, f32[22,4,256]{2,1,0:T(4,128)}, u32[]{:S(2)}, u32[]{:S(2)}) collective-permute-start(f32[22,4,256]{2,1,0:T(4,128)} %get-tuple-element.5), channel_id=1, source_target_pairs={{8,0},{9,1},{10,2},{11,3},{12,4},{13,5},{14,6},{15,7},{16,8},{17,9... | collective-permute-start | bytes 270344 | tf_op jit(solution)/shard_map/ppermute | solution.py:27
  19.1 7.7 %collective-permute-start.3 = (f32[22,4,256]{2,1,0:T(4,128)}, f32[22,4,256]{2,1,0:T(4,128)}, u32[]{:S(2)}, u32[]{:S(2)}) collective-permute-start(f32[22,4,256]{2,1,0:T(4,128)} %get-tuple-element.6), channel_id=1, source_target_pairs={{0,8},{1,9},{2,10},{3,11},{4,12},{5,13},{6,14},{7,15},{8,16},{9,17... | collective-permute-start | bytes 270344 | tf_op jit(solution)/shard_map/ppermute | solution.py:27
  26.1 21.6 %collective-permute-start.4 = (s32[256]{0:T(256)S(1)}, s32[256]{0:T(256)S(1)}, u32[]{:S(2)}, u32[]{:S(2)}) collective-permute-start(s32[256]{0:T(256)S(1)} %reshape_squeeze.3), channel_id=1, source_target_pairs={{0,128},{128,0},{1,129},{129,1},{2,130},{130,2},{3,131},{131,3},{4... | collective-permute-start | bytes 3080 | tf_op jit(solution)/shard_map/ppermute | solution.py:66
  31.8 10.0 %copy-start.5 = (s32[1,128,1]{1,2,0:T(1,128)S(1)}, s32[1,128,1]{1,2,0:T(1,128)}, u32[]{:S(2)}) copy-start(s32[1,128,1]{1,2,0:T(1,128)} %param.12) | copy-start | bytes 1540
  31.8 10.2 %copy-start.6 = (s32[1,128]{1,0:T(1,128)S(1)}, s32[1,128]{1,0:T(1,128)}, u32[]{:S(2)}) copy-start(s32[1,128]{1,0:T(1,128)} %param.11) | copy-start | bytes 1540
  41.5 6.2 %collective-permute-start.5 = (f32[10,64,2,128]{3,1,2,0:T(8,128)S(1)}, f32[10,64,2,128]{3,1,2,0:T(8,128)S(1)}, u32[]{:S(2)}, u32[]{:S(2)}) collective-permute-start(f32[10,64,2,128]{3,1,2,0:T(8,128)S(1)} %copy.48), channel_id=1, source_target_pairs={{0,128},{128,0},{1,129},{129,1},{2,130},{130,2},{3,131},{131,3},{4... | collective-permute-start | bytes 1966088 | tf_op jit(solution)/shard_map/ppermute | solution.py:66
  186.9 2.4 %collective-permute-start.6 = (f32[10,64,2,128]{3,1,2,0:T(8,128)S(1)}, f32[10,64,2,128]{3,1,2,0:T(8,128)S(1)}, u32[]{:S(2)}, u32[]{:S(2)}) collective-permute-start(f32[10,64,2,128]{3,1,2,0:T(8,128)S(1)} %fusion.5), channel_id=1, source_target_pairs={{0,128},{128,0},{1,129},{129,1},{2,130},{130,2},{3,131},{131,3},{4... | collective-permute-start | bytes 1966088 | tf_op jit(solution)/shard_map/ppermute | solution.py:66
  187.3 2.1 copy-start.1
  190.5 6.1 %collective-permute-start.7 = (f32[10,128,4]{1,2,0:T(4,128)S(1)}, f32[10,128,4]{1,2,0:T(4,128)S(1)}, u32[]{:S(2)}, u32[]{:S(2)}) collective-permute-start(f32[10,128,4]{1,2,0:T(4,128)S(1)} %copy.51), channel_id=1, source_target_pairs={{1,0},{2,1},{3,2},{4,3},{5,4},{6,5},{7,6},{9,8},{10,9},{11,10},{12... | collective-permute-start | bytes 61448 | tf_op jit(solution)/shard_map/ppermute | solution.py:27
  194.1 5.7 %collective-permute-start.8 = (f32[10,128,4]{1,2,0:T(4,128)S(1)}, f32[10,128,4]{1,2,0:T(4,128)S(1)}, u32[]{:S(2)}, u32[]{:S(2)}) collective-permute-start(f32[10,128,4]{1,2,0:T(4,128)S(1)} %copy.52), channel_id=1, source_target_pairs={{0,1},{1,2},{2,3},{3,4},{4,5},{5,6},{6,7},{8,9},{9,10},{10,11},{11... | collective-permute-start | bytes 61448 | tf_op jit(solution)/shard_map/ppermute | solution.py:27
  200.2 7.2 %collective-permute-start.10 = (f32[10,4,256]{2,1,0:T(4,128)S(1)}, f32[10,4,256]{2,1,0:T(4,128)S(1)}, u32[]{:S(2)}, u32[]{:S(2)}) collective-permute-start(f32[10,4,256]{2,1,0:T(4,128)S(1)} %get-tuple-element.14), channel_id=1, source_target_pairs={{0,8},{1,9},{2,10},{3,11},{4,12},{5,13},{6,14},{7,15},{8,16},{9,17... | collective-permute-start | bytes 122888 | tf_op jit(solution)/shard_map/ppermute | solution.py:27
  205.4 8.0 %collective-permute-start.9 = (f32[10,4,256]{2,1,0:T(4,128)S(1)}, f32[10,4,256]{2,1,0:T(4,128)S(1)}, u32[]{:S(2)}, u32[]{:S(2)}) collective-permute-start(f32[10,4,256]{2,1,0:T(4,128)S(1)} %get-tuple-element.13), channel_id=1, source_target_pairs={{8,0},{9,1},{10,2},{11,3},{12,4},{13,5},{14,6},{15,7},{16,8},{17,9... | collective-permute-start | bytes 122888 | tf_op jit(solution)/shard_map/ppermute | solution.py:27

commit v5 on v4

--- a/solution.py
+++ b/solution.py
@@ -38,28 +38,38 @@
     return jnp.concatenate([wide, south, north], axis=1)
 
 
-def sweeps(ext, visc, invd, force, count, rows, cols):
-    levels, height, lanes = ext.shape
+def sweeps(ext, force, count, rows, cols):
+    levels = ext.shape[0] if force is not None else (ext.shape[0] - 2) // 2
+    height, lanes = ext.shape[1:]
+    vmem = pl.BlockSpec(memory_space=pltpu.VMEM)
 
-    def kernel(x_ref, v_ref, i_ref, f_ref, o_ref):
-        v = v_ref[0]
-        inv = i_ref[0]
+    def kernel(x_ref, f_ref, o_ref):
+        if force is None:
+            f_ref = x_ref
+        nf = f_ref.shape[0]
+        scale = OMEGA * f_ref[nf - 1]
+        visc = f_ref[nf - 2]
+        base = nf - 2 - levels
 
         def level(l, carry):
             x = x_ref[l]
-            f = f_ref[l]
+            f = f_ref[base + l]
             for _ in range(count):
                 beside = pltpu.roll(x, 1, 0) + pltpu.roll(x, height - 1, 0)
                 beside = beside + pltpu.roll(x, 1, 1) + pltpu.roll(x, lanes - 1, 1)
-                x = (1.0 - OMEGA) * x + OMEGA * inv * (f + v * beside)
+                x = (1.0 - OMEGA) * x + scale * (f + visc * beside)
             o_ref[l] = x[:rows, :cols]
             return carry
 
         lax.fori_loop(0, levels, level, 0)
 
+    side = ext if force is None else force
     return pl.pallas_call(
-        kernel, out_shape=jax.ShapeDtypeStruct((levels, rows, cols), jnp.float32)
-    )(ext, visc, invd, force)
+        kernel,
+        out_shape=jax.ShapeDtypeStruct((levels, rows, cols), jnp.float32),
+        in_specs=[vmem, vmem],
+        out_specs=vmem,
+    )(ext, side)
 
 
 def swap_sec(x):
@@ -120,14 +130,10 @@
     invd = 1.0 / (4.0 * viscosity + reaction)
     stacked = jnp.concatenate([adjoint_state[0], forcing[0], viscosity, invd], axis=0)
     ext = halo(stacked, w)
-    field = ext[:levels]
-    force = ext[levels:2 * levels]
-    visc = ext[2 * levels:2 * levels + 1]
-    inv_wide = ext[2 * levels + 1:]
     sel = selectors(source_patch, owner, cavity_map, rows // PATCH)
-    x1 = sweeps(field, visc, inv_wide, force, w, rows, cols)
+    x1 = sweeps(ext, None, w, rows, cols)
     x2 = couple(x1, sel)
-    out = sweeps(halo(x2, w), visc, inv_wide, force, SWEEPS - w, rows, cols)
+    out = sweeps(halo(x2, w), ext, SWEEPS - w, rows, cols)
     return out[None]
 
 

time: 224 us -> 225 us (level)
  local copies, waits for them, and re-layouts: 15.7 us -> 13.2 us
    slice x2 -> x0, local copies, waits for them, and re-layouts: 2.47 us -> none  [the longest x1 1.75 us: body(): force = ext[levels:2 * levels]]
  transfers between devices with their start and end apart: 11 -> 11, of which waited for: 4 -> 4; matrix products, arithmetic and copies ran while one was open for 8% -> 7% of each run, Pallas kernels for 4% -> 4%
where the time goes in v5:
time: 225 us; the launch traced here: 224 us
  blocking collectives  134 us (60%)
  starting transfers between devices  27.5 us (12%)
  Pallas kernels  18.4 us (8%)
  local copies, waits for them, and re-layouts  13.2 us (6%)
  waiting for transfers between devices  11.3 us (5%)
  other arithmetic  11 us (5%)
  matrix products  8.08 us (4%)
    all_to_all x1, blocking collectives, couple(): incoming = lax.all_to_all(outgoing, ('gx', 'gy'), 0, 0, tiled=True)  134 us
    ppermute x8, starting transfers between devices, shifted(): return lax.ppermute(block, ('gx', 'gy'), pairs)  26.8 us
    pallas_call x2, Pallas kernels, sweeps(): pl.pallas_call(kernel, out_shape=jax.ShapeDtypeStruct((levels, rows, cols...  18.4 us
    ppermute x8, waiting for transfers between devices, shifted(): return lax.ppermute(block, ('gx', 'gy'), pairs)  11.3 us
    concatenate x2, other arithmetic, halo(): return jnp.concatenate([wide, south, north], axis=1)  5.69 us
    dot_general x2, matrix products, pick(): return jnp.einsum('jk,lkrc->jlrc', sel, patches, precision=HIGHEST)  4.6 us
  transfers between devices with their start and end apart: 11, of which 4 were waited for; matrix products, arithmetic and copies ran while one was open for 7% of the time, Pallas kernels for 4%

profile of v5, /device:TPU:54, one launch (start us, length us, event | category | flops | bytes accessed | tf_op | source)
XLA Modules:
  0.0 223.9 jit_solution(7708773510027194491)
XLA Ops:
  0.0 0.9 add_divide_fusion
  0.9 0.6 copy-done.3
  1.5 1.4 pad_maximum_fusion.2
  3.5 1.1 copy.38
  4.5 2.0 collective-permute-start
  7.0 3.8 %collective-permute-start.1 = (f32[22,128,4]{1,2,0:T(4,128)S(1)}, f32[22,128,4]{1,2,0:T(4,128)}, u32[]{:S(2)}, u32[]{:S(2)}) collective-permute-start(f32[22,128,4]{1,2,0:T(4,128)S(1)} %copy.39), channel_id=1, source_target_pairs={{0,1},{1,2},{2,3},{3,4},{4,5},{5,6},{6,7},{8,9},{9,10},{10,11},{11... | collective-permute-start | bytes 135176 | tf_op jit(solution)/shard_map/ppermute | solution.py:27
  11.3 1.7 collective-permute-done.1
  13.0 1.2 copy.41
  14.5 1.9 pad_maximum_fusion.10
  16.4 2.7 %collective-permute-start.2 = (f32[22,4,256]{2,1,0:T(4,128)}, f32[22,4,256]{2,1,0:T(4,128)}, u32[]{:S(2)}, u32[]{:S(2)}) collective-permute-start(f32[22,4,256]{2,1,0:T(4,128)} %get-tuple-element.5), channel_id=1, source_target_pairs={{8,0},{9,1},{10,2},{11,3},{12,4},{13,5},{14,6},{15,7},{16,8},{17,9... | collective-permute-start | bytes 270344 | tf_op jit(solution)/shard_map/ppermute | solution.py:27
  19.1 5.2 %collective-permute-start.3 = (f32[22,4,256]{2,1,0:T(4,128)}, f32[22,4,256]{2,1,0:T(4,128)}, u32[]{:S(2)}, u32[]{:S(2)}) collective-permute-start(f32[22,4,256]{2,1,0:T(4,128)} %get-tuple-element.6), channel_id=1, source_target_pairs={{0,8},{1,9},{2,10},{3,11},{4,12},{5,13},{6,14},{7,15},{8,16},{9,17... | collective-permute-start | bytes 270344 | tf_op jit(solution)/shard_map/ppermute | solution.py:27
  24.3 0.7 copy.44
  25.1 1.0 reshape_squeeze.3
  26.2 0.6 collective-permute-done.3
  26.8 4.2 %pad_maximum_fusion.1.x_ref.f_ref = f32[22,136,256]{2,1,0:T(8,128)} fusion(f32[22,4,256]{2,1,0:T(4,128)} %collective-permute-done.3, f32[22,4,256]{2,1,0:T(4,128)} %collective-permute-done.2, f32[22,128,4]{2,1,0:T(8,128)S(1)} %copy.41, f32[22,128,120]{2,1,0:T(8,128)} %copy-done, f32[22,128,4]{2,1,0:T(8,128)S(1)} %copy.40, f32[1,128,128]{2,1,0:T(8,128)} %copy-done.3, ...), kind=kLoop, calls=%fused_computation.1 | loop fusion | flops 6127616 | bytes 6127616 | tf_op jit(solution)/shard_map/concatenate | solution.py:38
  30.9 9.5 %shard_map.73 = f32[10,128,128]{2,1,0:T(8,128)} custom-call(f32[22,136,256]{2,1,0:T(8,128)} %pad_maximum_fusion.1.x_ref.f_ref, f32[22,136,256]{2,1,0:T(8,128)} %pad_maximum_fusion.1.x_ref.f_ref), custom_call_target="tpu_custom_call" | custom-call | tf_op jit(solution)/shard_map/pallas_call | solution.py:67
  40.4 1.1 copy.48
  42.3 3.4 %fusion.17 = f32[256,10,2,128]{3,0,2,1:T(8,128)S(1)} fusion(f32[256,64,1,1]{0,1,3,2:T(8,128)S(1)} %convolution_bitcast_fusion, f32[10,64,2,128]{3,2,1,0:T(2,128)} %bitcast.35), kind=kOutput, calls=%fused_computation.39 | convolution fusion | flops 503316480 | bytes 3342336 | tf_op jit(solution)/shard_map/jk,lkrc->jlrc/dot_general | solution.py:84
  45.7 2.0 copy.43
  47.7 1.2 fusion.12
  49.0 2.0 copy.46
  51.4 134.1 %all_to_all.5 = f32[128,80,128]{2,1,0:T(8,128)S(1)} all-to-all(f32[128,80,128]{2,1,0:T(8,128)S(1)} %pad_maximum_fusion), channel_id=1, replica_groups=mesh['sec'=2,'gx'=16,'gy'=8] {'gx','gy'}, dimensions={0} | all-to-all | bytes 10485760 | tf_op jit(solution)/shard_map/all_to_all | solution.py:118
  185.8 1.2 fusion.5
  187.3 2.1 fusion.4
  190.5 3.4 %collective-permute-start.7 = (f32[10,128,4]{1,2,0:T(4,128)S(1)}, f32[10,128,4]{1,2,0:T(4,128)S(1)}, u32[]{:S(2)}, u32[]{:S(2)}) collective-permute-start(f32[10,128,4]{1,2,0:T(4,128)S(1)} %copy.51), channel_id=1, source_target_pairs={{1,0},{2,1},{3,2},{4,3},{5,4},{6,5},{7,6},{9,8},{10,9},{11,10},{12... | collective-permute-start | bytes 61448 | tf_op jit(solution)/shard_map/ppermute | solution.py:27
  194.1 2.5 %collective-permute-start.8 = (f32[10,128,4]{1,2,0:T(4,128)S(1)}, f32[10,128,4]{1,2,0:T(4,128)S(1)}, u32[]{:S(2)}, u32[]{:S(2)}) collective-permute-start(f32[10,128,4]{1,2,0:T(4,128)S(1)} %copy.52), channel_id=1, source_target_pairs={{0,1},{1,2},{2,3},{3,4},{4,5},{5,6},{6,7},{8,9},{9,10},{10,11},{11... | collective-permute-start | bytes 61448 | tf_op jit(solution)/shard_map/ppermute | solution.py:27
  196.9 2.9 %collective-permute-done.8 = f32[10,128,4]{1,2,0:T(4,128)S(1)} collective-permute-done((f32[10,128,4]{1,2,0:T(4,128)S(1)}, f32[10,128,4]{1,2,0:T(4,128)S(1)}, u32[]{:S(2)}, u32[]{:S(2)}) %collective-permute-start.8) | collective-permute-done | bytes 20512 | tf_op jit(solution)/shard_map/ppermute | solution.py:27
  200.2 5.2 %collective-permute-start.10 = (f32[10,4,256]{2,1,0:T(4,128)S(1)}, f32[10,4,256]{2,1,0:T(4,128)S(1)}, u32[]{:S(2)}, u32[]{:S(2)}) collective-permute-start(f32[10,4,256]{2,1,0:T(4,128)S(1)} %get-tuple-element.10), channel_id=1, source_target_pairs={{0,8},{1,9},{2,10},{3,11},{4,12},{5,13},{6,14},{7,15},{8,16},{9,17... | collective-permute-start | bytes 122888 | tf_op jit(solution)/shard_map/ppermute | solution.py:27
  205.5 1.9 collective-permute-start.9
  207.4 6.1 %collective-permute-done.9 = f32[10,4,256]{2,1,0:T(4,128)S(1)} collective-permute-done((f32[10,4,256]{2,1,0:T(4,128)S(1)}, f32[10,4,256]{2,1,0:T(4,128)S(1)}, u32[]{:S(2)}, u32[]{:S(2)}) %collective-permute-start.9) | collective-permute-done | bytes 40992 | tf_op jit(solution)/shard_map/ppermute | solution.py:27
  213.5 1.5 pad_maximum_fusion.3.x_ref
  215.0 8.9 %shard_map.74 = f32[10,128,128]{2,1,0:T(8,128)} custom-call(f32[10,136,256]{2,1,0:T(8,128)} %pad_maximum_fusion.3.x_ref, f32[22,136,256]{2,1,0:T(8,128)} %pad_maximum_fusion.1.x_ref.f_ref), custom_call_target="tpu_custom_call" | custom-call | tf_op jit(solution)/shard_map/pallas_call | solution.py:67
  (41 shorter events, 5.5 us)
Async XLA Ops:
  0.9 0.6 copy-start.3
  4.5 6.3 %collective-permute-start = (f32[22,128,4]{1,2,0:T(4,128)}, f32[22,128,4]{1,2,0:T(4,128)S(1)}, u32[]{:S(2)}, u32[]{:S(2)}) collective-permute-start(f32[22,128,4]{1,2,0:T(4,128)} %copy.38), channel_id=1, source_target_pairs={{1,0},{2,1},{3,2},{4,3},{5,4},{6,5},{7,6},{9,8},{10,9},{11,10},{12... | collective-permute-start | bytes 135176 | tf_op jit(solution)/shard_map/ppermute | solution.py:27
  6.5 7.9 %copy-start.2 = (f32[1,10,128,128]{3,2,1,0:T(8,128)S(1)}, f32[1,10,128,128]{3,2,1,0:T(8,128)}, u32[]{:S(2)}) copy-start(f32[1,10,128,128]{3,2,1,0:T(8,128)} %param.8) | copy-start | bytes 1966084
  7.0 6.0 %collective-permute-start.1 = (f32[22,128,4]{1,2,0:T(4,128)S(1)}, f32[22,128,4]{1,2,0:T(4,128)}, u32[]{:S(2)}, u32[]{:S(2)}) collective-permute-start(f32[22,128,4]{1,2,0:T(4,128)S(1)} %copy.39), channel_id=1, source_target_pairs={{0,1},{1,2},{2,3},{3,4},{4,5},{5,6},{6,7},{8,9},{9,10},{10,11},{11... | collective-permute-start | bytes 135176 | tf_op jit(solution)/shard_map/ppermute | solution.py:27
  14.5 1.9 copy-start
  14.5 9.9 %copy-start.4 = (s32[1,1,128,2]{2,3,1,0:T(2,128)S(1)}, s32[1,1,128,2]{2,3,1,0:T(2,128)}, u32[]{:S(2)}) copy-start(s32[1,1,128,2]{2,3,1,0:T(2,128)} %param.13) | copy-start | bytes 3076
  16.4 9.8 %collective-permute-start.2 = (f32[22,4,256]{2,1,0:T(4,128)}, f32[22,4,256]{2,1,0:T(4,128)}, u32[]{:S(2)}, u32[]{:S(2)}) collective-permute-start(f32[22,4,256]{2,1,0:T(4,128)} %get-tuple-element.5), channel_id=1, source_target_pairs={{8,0},{9,1},{10,2},{11,3},{12,4},{13,5},{14,6},{15,7},{16,8},{17,9... | collective-permute-start | bytes 270344 | tf_op jit(solution)/shard_map/ppermute | solution.py:27
  19.1 7.7 %collective-permute-start.3 = (f32[22,4,256]{2,1,0:T(4,128)}, f32[22,4,256]{2,1,0:T(4,128)}, u32[]{:S(2)}, u32[]{:S(2)}) collective-permute-start(f32[22,4,256]{2,1,0:T(4,128)} %get-tuple-element.6), channel_id=1, source_target_pairs={{0,8},{1,9},{2,10},{3,11},{4,12},{5,13},{6,14},{7,15},{8,16},{9,17... | collective-permute-start | bytes 270344 | tf_op jit(solution)/shard_map/ppermute | solution.py:27
  26.1 21.6 %collective-permute-start.4 = (s32[256]{0:T(256)S(1)}, s32[256]{0:T(256)S(1)}, u32[]{:S(2)}, u32[]{:S(2)}) collective-permute-start(s32[256]{0:T(256)S(1)} %reshape_squeeze.3), channel_id=1, source_target_pairs={{0,128},{128,0},{1,129},{129,1},{2,130},{130,2},{3,131},{131,3},{4... | collective-permute-start | bytes 3080 | tf_op jit(solution)/shard_map/ppermute | solution.py:76
  30.9 10.9 %copy-start.5 = (s32[1,128,1]{1,2,0:T(1,128)S(1)}, s32[1,128,1]{1,2,0:T(1,128)}, u32[]{:S(2)}) copy-start(s32[1,128,1]{1,2,0:T(1,128)} %param.12) | copy-start | bytes 1540
  30.9 11.1 %copy-start.6 = (s32[1,128]{1,0:T(1,128)S(1)}, s32[1,128]{1,0:T(1,128)}, u32[]{:S(2)}) copy-start(s32[1,128]{1,0:T(1,128)} %param.11) | copy-start | bytes 1540
  41.6 6.2 %collective-permute-start.5 = (f32[10,64,2,128]{3,1,2,0:T(8,128)S(1)}, f32[10,64,2,128]{3,1,2,0:T(8,128)S(1)}, u32[]{:S(2)}, u32[]{:S(2)}) collective-permute-start(f32[10,64,2,128]{3,1,2,0:T(8,128)S(1)} %copy.48), channel_id=1, source_target_pairs={{0,128},{128,0},{1,129},{129,1},{2,130},{130,2},{3,131},{131,3},{4... | collective-permute-start | bytes 1966088 | tf_op jit(solution)/shard_map/ppermute | solution.py:76
  187.0 2.4 %collective-permute-start.6 = (f32[10,64,2,128]{3,1,2,0:T(8,128)S(1)}, f32[10,64,2,128]{3,1,2,0:T(8,128)S(1)}, u32[]{:S(2)}, u32[]{:S(2)}) collective-permute-start(f32[10,64,2,128]{3,1,2,0:T(8,128)S(1)} %fusion.5), channel_id=1, source_target_pairs={{0,128},{128,0},{1,129},{129,1},{2,130},{130,2},{3,131},{131,3},{4... | collective-permute-start | bytes 1966088 | tf_op jit(solution)/shard_map/ppermute | solution.py:76
  187.3 2.1 copy-start.1
  190.5 6.1 %collective-permute-start.7 = (f32[10,128,4]{1,2,0:T(4,128)S(1)}, f32[10,128,4]{1,2,0:T(4,128)S(1)}, u32[]{:S(2)}, u32[]{:S(2)}) collective-permute-start(f32[10,128,4]{1,2,0:T(4,128)S(1)} %copy.51), channel_id=1, source_target_pairs={{1,0},{2,1},{3,2},{4,3},{5,4},{6,5},{7,6},{9,8},{10,9},{11,10},{12... | collective-permute-start | bytes 61448 | tf_op jit(solution)/shard_map/ppermute | solution.py:27
  194.1 5.7 %collective-permute-start.8 = (f32[10,128,4]{1,2,0:T(4,128)S(1)}, f32[10,128,4]{1,2,0:T(4,128)S(1)}, u32[]{:S(2)}, u32[]{:S(2)}) collective-permute-start(f32[10,128,4]{1,2,0:T(4,128)S(1)} %copy.52), channel_id=1, source_target_pairs={{0,1},{1,2},{2,3},{3,4},{4,5},{5,6},{6,7},{8,9},{9,10},{10,11},{11... | collective-permute-start | bytes 61448 | tf_op jit(solution)/shard_map/ppermute | solution.py:27
  200.2 7.2 %collective-permute-start.10 = (f32[10,4,256]{2,1,0:T(4,128)S(1)}, f32[10,4,256]{2,1,0:T(4,128)S(1)}, u32[]{:S(2)}, u32[]{:S(2)}) collective-permute-start(f32[10,4,256]{2,1,0:T(4,128)S(1)} %get-tuple-element.10), channel_id=1, source_target_pairs={{0,8},{1,9},{2,10},{3,11},{4,12},{5,13},{6,14},{7,15},{8,16},{9,17... | collective-permute-start | bytes 122888 | tf_op jit(solution)/shard_map/ppermute | solution.py:27
  205.5 8.0 %collective-permute-start.9 = (f32[10,4,256]{2,1,0:T(4,128)S(1)}, f32[10,4,256]{2,1,0:T(4,128)S(1)}, u32[]{:S(2)}, u32[]{:S(2)}) collective-permute-start(f32[10,4,256]{2,1,0:T(4,128)S(1)} %get-tuple-element.9), channel_id=1, source_target_pairs={{8,0},{9,1},{10,2},{11,3},{12,4},{13,5},{14,6},{15,7},{16,8},{17,9... | collective-permute-start | bytes 122888 | tf_op jit(solution)/shard_map/ppermute | solution.py:27

commit v6 on v5

--- a/solution.py
+++ b/solution.py
@@ -35,30 +35,36 @@
     wide = jnp.concatenate([cells, east, gap, west], axis=2)
     north = shifted(wide[:, -w:], -1, 0)
     south = shifted(wide[:, :w], 1, 0)
-    return jnp.concatenate([wide, south, north], axis=1)
+    return jnp.concatenate([north, wide, south], axis=1)
 
 
 def sweeps(ext, force, count, rows, cols):
     levels = ext.shape[0] if force is not None else (ext.shape[0] - 2) // 2
     height, lanes = ext.shape[1:]
+    w = (height - rows) // 2
+    pad = 8
     vmem = pl.BlockSpec(memory_space=pltpu.VMEM)
 
-    def kernel(x_ref, f_ref, o_ref):
+    def kernel(x_ref, f_ref, o_ref, s_ref):
         if force is None:
             f_ref = x_ref
         nf = f_ref.shape[0]
         scale = OMEGA * f_ref[nf - 1]
         visc = f_ref[nf - 2]
         base = nf - 2 - levels
+        s_ref[0:pad] = jnp.zeros((pad, lanes), jnp.float32)
+        s_ref[pad + height:] = jnp.zeros((pad, lanes), jnp.float32)
 
         def level(l, carry):
             x = x_ref[l]
             f = f_ref[base + l]
             for _ in range(count):
-                beside = pltpu.roll(x, 1, 0) + pltpu.roll(x, height - 1, 0)
-                beside = beside + pltpu.roll(x, 1, 1) + pltpu.roll(x, lanes - 1, 1)
+                s_ref[pad:pad + height] = x
+                beside = s_ref[pad + 1:pad + 1 + height] + s_ref[pad - 1:pad - 1 + height]
+                beside = beside + pltpu.roll(x, lanes - 1, 1) + pltpu.roll(x, 1, 1)
                 x = (1.0 - OMEGA) * x + scale * (f + visc * beside)
-            o_ref[l] = x[:rows, :cols]
+            s_ref[pad:pad + height] = x
+            o_ref[l] = s_ref[pad + w:pad + w + rows, 0:cols]
             return carry
 
         lax.fori_loop(0, levels, level, 0)
@@ -69,6 +75,7 @@
         out_shape=jax.ShapeDtypeStruct((levels, rows, cols), jnp.float32),
         in_specs=[vmem, vmem],
         out_specs=vmem,
+        scratch_shapes=[pltpu.VMEM((height + 2 * pad, lanes), jnp.float32)],
     )(ext, side)
 
 

time: 225 us -> 227 us (level); the launches traced: 224 us -> 222 us
  transfers between devices with their start and end apart: 11 -> 11, of which waited for: 4 -> 4; matrix products, arithmetic and copies ran while one was open for 7% -> 7% of each run, Pallas kernels for 4% -> 5%
where the time goes in v6:
time: 227 us; the launch traced here: 222 us
  blocking collectives  133 us (59%)
  starting transfers between devices  26.1 us (11%)
  Pallas kernels  19.6 us (9%)
  local copies, waits for them, and re-layouts  13.2 us (6%)
  other arithmetic  11.1 us (5%)
  waiting for transfers between devices  10.6 us (5%)
  matrix products  8.08 us (4%)
    all_to_all x1, blocking collectives, couple(): incoming = lax.all_to_all(outgoing, ('gx', 'gy'), 0, 0, tiled=True)  133 us
    ppermute x8, starting transfers between devices, shifted(): return lax.ppermute(block, ('gx', 'gy'), pairs)  25.5 us
    pallas_call x2, Pallas kernels, sweeps(): pl.pallas_call(kernel, out_shape=jax.ShapeDtypeStruct((levels, rows, cols...  19.6 us
    ppermute x8, waiting for transfers between devices, shifted(): return lax.ppermute(block, ('gx', 'gy'), pairs)  10.6 us
    concatenate x2, other arithmetic, halo(): return jnp.concatenate([north, wide, south], axis=1)  5.72 us
    dot_general x2, matrix products, pick(): return jnp.einsum('jk,lkrc->jlrc', sel, patches, precision=HIGHEST)  4.6 us
  transfers between devices with their start and end apart: 11, of which 4 were waited for; matrix products, arithmetic and copies ran while one was open for 7% of the time, Pallas kernels for 5%

profile of v6, /device:TPU:54, one launch (start us, length us, event | category | flops | bytes accessed | tf_op | source)
XLA Modules:
  0.0 222.2 jit_solution(14367303320080351138)
XLA Ops:
  0.0 0.9 add_divide_fusion
  0.9 0.6 copy-done.3
  1.5 1.4 pad_maximum_fusion.2
  3.5 1.1 copy.38
  4.5 2.0 collective-permute-start
  7.0 3.8 %collective-permute-start.1 = (f32[22,128,4]{1,2,0:T(4,128)S(1)}, f32[22,128,4]{1,2,0:T(4,128)}, u32[]{:S(2)}, u32[]{:S(2)}) collective-permute-start(f32[22,128,4]{1,2,0:T(4,128)S(1)} %copy.39), channel_id=1, source_target_pairs={{0,1},{1,2},{2,3},{3,4},{4,5},{5,6},{6,7},{8,9},{9,10},{10,11},{11... | collective-permute-start | bytes 135176 | tf_op jit(solution)/shard_map/ppermute | solution.py:27
  11.3 1.7 collective-permute-done.1
  13.0 1.2 copy.41
  14.5 1.9 pad_maximum_fusion.10
  16.4 3.1 %collective-permute-start.2 = (f32[22,4,256]{2,1,0:T(4,128)}, f32[22,4,256]{2,1,0:T(4,128)}, u32[]{:S(2)}, u32[]{:S(2)}) collective-permute-start(f32[22,4,256]{2,1,0:T(4,128)} %get-tuple-element.5), channel_id=1, source_target_pairs={{0,8},{1,9},{2,10},{3,11},{4,12},{5,13},{6,14},{7,15},{8,16},{9,17... | collective-permute-start | bytes 270344 | tf_op jit(solution)/shard_map/ppermute | solution.py:27
  19.5 2.7 %collective-permute-start.3 = (f32[22,4,256]{2,1,0:T(4,128)}, f32[22,4,256]{2,1,0:T(4,128)}, u32[]{:S(2)}, u32[]{:S(2)}) collective-permute-start(f32[22,4,256]{2,1,0:T(4,128)} %get-tuple-element.6), channel_id=1, source_target_pairs={{8,0},{9,1},{10,2},{11,3},{12,4},{13,5},{14,6},{15,7},{16,8},{17,9... | collective-permute-start | bytes 270344 | tf_op jit(solution)/shard_map/ppermute | solution.py:27
  22.2 0.7 copy.44
  23.0 1.0 reshape_squeeze.3
  24.1 4.3 %collective-permute-done.3 = f32[22,4,256]{2,1,0:T(4,128)} collective-permute-done((f32[22,4,256]{2,1,0:T(4,128)}, f32[22,4,256]{2,1,0:T(4,128)}, u32[]{:S(2)}, u32[]{:S(2)}) %collective-permute-start.3) | collective-permute-done | bytes 90144 | tf_op jit(solution)/shard_map/ppermute | solution.py:27
  28.3 4.2 %pad_maximum_fusion.1.x_ref.f_ref = f32[22,136,256]{2,1,0:T(8,128)} fusion(f32[22,4,256]{2,1,0:T(4,128)} %collective-permute-done.3, f32[22,128,4]{2,1,0:T(8,128)S(1)} %copy.41, f32[22,128,120]{2,1,0:T(8,128)} %copy-done, f32[22,128,4]{2,1,0:T(8,128)S(1)} %copy.40, f32[1,128,128]{2,1,0:T(8,128)} %copy-done.3, f32[1,128,128]{2,1,0:T(8,128)} %param.9, ...), kind=kLoop, calls=%fused_computation.1 | loop fusion | flops 6127616 | bytes 6127616 | tf_op jit(solution)/shard_map/concatenate | solution.py:38
  32.5 10.1 %shard_map.73 = f32[10,128,128]{2,1,0:T(8,128)} custom-call(f32[22,136,256]{2,1,0:T(8,128)} %pad_maximum_fusion.1.x_ref.f_ref, f32[22,136,256]{2,1,0:T(8,128)} %pad_maximum_fusion.1.x_ref.f_ref), custom_call_target="tpu_custom_call" | custom-call | tf_op jit(solution)/shard_map/pallas_call | solution.py:73
  42.6 1.1 copy.48
  44.5 3.4 %fusion.17 = f32[256,10,2,128]{3,0,2,1:T(8,128)S(1)} fusion(f32[256,64,1,1]{0,1,3,2:T(8,128)S(1)} %convolution_bitcast_fusion, f32[10,64,2,128]{3,2,1,0:T(2,128)} %bitcast.35), kind=kOutput, calls=%fused_computation.39 | convolution fusion | flops 503316480 | bytes 3342336 | tf_op jit(solution)/shard_map/jk,lkrc->jlrc/dot_general | solution.py:91
  47.9 2.0 copy.43
  49.9 1.2 fusion.12
  51.2 2.0 copy.46
  53.6 133.1 %all_to_all.5 = f32[128,80,128]{2,1,0:T(8,128)S(1)} all-to-all(f32[128,80,128]{2,1,0:T(8,128)S(1)} %pad_maximum_fusion), channel_id=1, replica_groups=mesh['sec'=2,'gx'=16,'gy'=8] {'gx','gy'}, dimensions={0} | all-to-all | bytes 10485760 | tf_op jit(solution)/shard_map/all_to_all | solution.py:125
  187.1 1.2 fusion.5
  188.6 2.1 fusion.4
  191.8 3.4 %collective-permute-start.7 = (f32[10,128,4]{1,2,0:T(4,128)S(1)}, f32[10,128,4]{1,2,0:T(4,128)S(1)}, u32[]{:S(2)}, u32[]{:S(2)}) collective-permute-start(f32[10,128,4]{1,2,0:T(4,128)S(1)} %copy.51), channel_id=1, source_target_pairs={{1,0},{2,1},{3,2},{4,3},{5,4},{6,5},{7,6},{9,8},{10,9},{11,10},{12... | collective-permute-start | bytes 61448 | tf_op jit(solution)/shard_map/ppermute | solution.py:27
  195.4 2.5 %collective-permute-start.8 = (f32[10,128,4]{1,2,0:T(4,128)S(1)}, f32[10,128,4]{1,2,0:T(4,128)S(1)}, u32[]{:S(2)}, u32[]{:S(2)}) collective-permute-start(f32[10,128,4]{1,2,0:T(4,128)S(1)} %copy.52), channel_id=1, source_target_pairs={{0,1},{1,2},{2,3},{3,4},{4,5},{5,6},{6,7},{8,9},{9,10},{10,11},{11... | collective-permute-start | bytes 61448 | tf_op jit(solution)/shard_map/ppermute | solution.py:27
  198.1 2.9 %collective-permute-done.8 = f32[10,128,4]{1,2,0:T(4,128)S(1)} collective-permute-done((f32[10,128,4]{1,2,0:T(4,128)S(1)}, f32[10,128,4]{1,2,0:T(4,128)S(1)}, u32[]{:S(2)}, u32[]{:S(2)}) %collective-permute-start.8) | collective-permute-done | bytes 20512 | tf_op jit(solution)/shard_map/ppermute | solution.py:27
  201.5 2.4 %collective-permute-start.10 = (f32[10,4,256]{2,1,0:T(4,128)S(1)}, f32[10,4,256]{2,1,0:T(4,128)S(1)}, u32[]{:S(2)}, u32[]{:S(2)}) collective-permute-start(f32[10,4,256]{2,1,0:T(4,128)S(1)} %get-tuple-element.10), channel_id=1, source_target_pairs={{8,0},{9,1},{10,2},{11,3},{12,4},{13,5},{14,6},{15,7},{16,8},{17,9... | collective-permute-start | bytes 122888 | tf_op jit(solution)/shard_map/ppermute | solution.py:27
  203.9 5.5 %collective-permute-start.9 = (f32[10,4,256]{2,1,0:T(4,128)S(1)}, f32[10,4,256]{2,1,0:T(4,128)S(1)}, u32[]{:S(2)}, u32[]{:S(2)}) collective-permute-start(f32[10,4,256]{2,1,0:T(4,128)S(1)} %get-tuple-element.9), channel_id=1, source_target_pairs={{0,8},{1,9},{2,10},{3,11},{4,12},{5,13},{6,14},{7,15},{8,16},{9,17... | collective-permute-start | bytes 122888 | tf_op jit(solution)/shard_map/ppermute | solution.py:27
  209.5 1.6 collective-permute-done.9
  211.1 1.5 pad_maximum_fusion.3.x_ref
  212.6 9.6 %shard_map.74 = f32[10,128,128]{2,1,0:T(8,128)} custom-call(f32[10,136,256]{2,1,0:T(8,128)} %pad_maximum_fusion.3.x_ref, f32[22,136,256]{2,1,0:T(8,128)} %pad_maximum_fusion.1.x_ref.f_ref), custom_call_target="tpu_custom_call" | custom-call | tf_op jit(solution)/shard_map/pallas_call | solution.py:73
  (41 shorter events, 5.5 us)
Async XLA Ops:
  0.9 0.6 copy-start.3
  4.5 6.3 %collective-permute-start = (f32[22,128,4]{1,2,0:T(4,128)}, f32[22,128,4]{1,2,0:T(4,128)S(1)}, u32[]{:S(2)}, u32[]{:S(2)}) collective-permute-start(f32[22,128,4]{1,2,0:T(4,128)} %copy.38), channel_id=1, source_target_pairs={{1,0},{2,1},{3,2},{4,3},{5,4},{6,5},{7,6},{9,8},{10,9},{11,10},{12... | collective-permute-start | bytes 135176 | tf_op jit(solution)/shard_map/ppermute | solution.py:27
  6.5 7.9 %copy-start.2 = (f32[1,10,128,128]{3,2,1,0:T(8,128)S(1)}, f32[1,10,128,128]{3,2,1,0:T(8,128)}, u32[]{:S(2)}) copy-start(f32[1,10,128,128]{3,2,1,0:T(8,128)} %param.8) | copy-start | bytes 1966084
  7.0 6.0 %collective-permute-start.1 = (f32[22,128,4]{1,2,0:T(4,128)S(1)}, f32[22,128,4]{1,2,0:T(4,128)}, u32[]{:S(2)}, u32[]{:S(2)}) collective-permute-start(f32[22,128,4]{1,2,0:T(4,128)S(1)} %copy.39), channel_id=1, source_target_pairs={{0,1},{1,2},{2,3},{3,4},{4,5},{5,6},{6,7},{8,9},{9,10},{10,11},{11... | collective-permute-start | bytes 135176 | tf_op jit(solution)/shard_map/ppermute | solution.py:27
  14.5 1.9 copy-start
  14.5 7.8 %copy-start.4 = (s32[1,1,128,2]{2,3,1,0:T(2,128)S(1)}, s32[1,1,128,2]{2,3,1,0:T(2,128)}, u32[]{:S(2)}) copy-start(s32[1,1,128,2]{2,3,1,0:T(2,128)} %param.13) | copy-start | bytes 3076
  16.4 7.7 %collective-permute-start.2 = (f32[22,4,256]{2,1,0:T(4,128)}, f32[22,4,256]{2,1,0:T(4,128)}, u32[]{:S(2)}, u32[]{:S(2)}) collective-permute-start(f32[22,4,256]{2,1,0:T(4,128)} %get-tuple-element.5), channel_id=1, source_target_pairs={{0,8},{1,9},{2,10},{3,11},{4,12},{5,13},{6,14},{7,15},{8,16},{9,17... | collective-permute-start | bytes 270344 | tf_op jit(solution)/shard_map/ppermute | solution.py:27
  19.5 8.8 %collective-permute-start.3 = (f32[22,4,256]{2,1,0:T(4,128)}, f32[22,4,256]{2,1,0:T(4,128)}, u32[]{:S(2)}, u32[]{:S(2)}) collective-permute-start(f32[22,4,256]{2,1,0:T(4,128)} %get-tuple-element.6), channel_id=1, source_target_pairs={{8,0},{9,1},{10,2},{11,3},{12,4},{13,5},{14,6},{15,7},{16,8},{17,9... | collective-permute-start | bytes 270344 | tf_op jit(solution)/shard_map/ppermute | solution.py:27
  24.0 26.0 %collective-permute-start.4 = (s32[256]{0:T(256)S(1)}, s32[256]{0:T(256)S(1)}, u32[]{:S(2)}, u32[]{:S(2)}) collective-permute-start(s32[256]{0:T(256)S(1)} %reshape_squeeze.3), channel_id=1, source_target_pairs={{0,128},{128,0},{1,129},{129,1},{2,130},{130,2},{3,131},{131,3},{4... | collective-permute-start | bytes 3080 | tf_op jit(solution)/shard_map/ppermute | solution.py:83
  32.5 11.5 %copy-start.5 = (s32[1,128,1]{1,2,0:T(1,128)S(1)}, s32[1,128,1]{1,2,0:T(1,128)}, u32[]{:S(2)}) copy-start(s32[1,128,1]{1,2,0:T(1,128)} %param.12) | copy-start | bytes 1540
  32.5 11.7 %copy-start.6 = (s32[1,128]{1,0:T(1,128)S(1)}, s32[1,128]{1,0:T(1,128)}, u32[]{:S(2)}) copy-start(s32[1,128]{1,0:T(1,128)} %param.11) | copy-start | bytes 1540
  43.8 6.2 %collective-permute-start.5 = (f32[10,64,2,128]{3,1,2,0:T(8,128)S(1)}, f32[10,64,2,128]{3,1,2,0:T(8,128)S(1)}, u32[]{:S(2)}, u32[]{:S(2)}) collective-permute-start(f32[10,64,2,128]{3,1,2,0:T(8,128)S(1)} %copy.48), channel_id=1, source_target_pairs={{0,128},{128,0},{1,129},{129,1},{2,130},{130,2},{3,131},{131,3},{4... | collective-permute-start | bytes 1966088 | tf_op jit(solution)/shard_map/ppermute | solution.py:83
  188.3 2.4 %collective-permute-start.6 = (f32[10,64,2,128]{3,1,2,0:T(8,128)S(1)}, f32[10,64,2,128]{3,1,2,0:T(8,128)S(1)}, u32[]{:S(2)}, u32[]{:S(2)}) collective-permute-start(f32[10,64,2,128]{3,1,2,0:T(8,128)S(1)} %fusion.5), channel_id=1, source_target_pairs={{0,128},{128,0},{1,129},{129,1},{2,130},{130,2},{3,131},{131,3},{4... | collective-permute-start | bytes 1966088 | tf_op jit(solution)/shard_map/ppermute | solution.py:83
  188.6 2.1 copy-start.1
  191.8 6.1 %collective-permute-start.7 = (f32[10,128,4]{1,2,0:T(4,128)S(1)}, f32[10,128,4]{1,2,0:T(4,128)S(1)}, u32[]{:S(2)}, u32[]{:S(2)}) collective-permute-start(f32[10,128,4]{1,2,0:T(4,128)S(1)} %copy.51), channel_id=1, source_target_pairs={{1,0},{2,1},{3,2},{4,3},{5,4},{6,5},{7,6},{9,8},{10,9},{11,10},{12... | collective-permute-start | bytes 61448 | tf_op jit(solution)/shard_map/ppermute | solution.py:27
  195.4 5.7 %collective-permute-start.8 = (f32[10,128,4]{1,2,0:T(4,128)S(1)}, f32[10,128,4]{1,2,0:T(4,128)S(1)}, u32[]{:S(2)}, u32[]{:S(2)}) collective-permute-start(f32[10,128,4]{1,2,0:T(4,128)S(1)} %copy.52), channel_id=1, source_target_pairs={{0,1},{1,2},{2,3},{3,4},{4,5},{5,6},{6,7},{8,9},{9,10},{10,11},{11... | collective-permute-start | bytes 61448 | tf_op jit(solution)/shard_map/ppermute | solution.py:27
  201.5 8.0 %collective-permute-start.10 = (f32[10,4,256]{2,1,0:T(4,128)S(1)}, f32[10,4,256]{2,1,0:T(4,128)S(1)}, u32[]{:S(2)}, u32[]{:S(2)}) collective-permute-start(f32[10,4,256]{2,1,0:T(4,128)S(1)} %get-tuple-element.10), channel_id=1, source_target_pairs={{8,0},{9,1},{10,2},{11,3},{12,4},{13,5},{14,6},{15,7},{16,8},{17,9... | collective-permute-start | bytes 122888 | tf_op jit(solution)/shard_map/ppermute | solution.py:27
  203.9 7.2 %collective-permute-start.9 = (f32[10,4,256]{2,1,0:T(4,128)S(1)}, f32[10,4,256]{2,1,0:T(4,128)S(1)}, u32[]{:S(2)}, u32[]{:S(2)}) collective-permute-start(f32[10,4,256]{2,1,0:T(4,128)S(1)} %get-tuple-element.9), channel_id=1, source_target_pairs={{0,8},{1,9},{2,10},{3,11},{4,12},{5,13},{6,14},{7,15},{8,16},{9,17... | collective-permute-start | bytes 122888 | tf_op jit(solution)/shard_map/ppermute | solution.py:27

commit v7 on v3

--- a/solution.py
+++ b/solution.py
@@ -56,11 +56,11 @@
 
 
 def pick(sel, patches):
-    return jnp.einsum("jk,lkrc->jlrc", sel, patches, precision=HIGHEST)
+    return jnp.einsum("jk,lrkc->jlrc", sel, patches, precision=HIGHEST)
 
 
 def spread(sel, values):
-    return jnp.einsum("jk,jlrc->lkrc", sel, values, precision=HIGHEST)
+    return jnp.einsum("jk,jlrc->lrkc", sel, values, precision=HIGHEST)
 
 
 def selectors(source_patch, owner, cavity_map, npatch):
@@ -83,7 +83,7 @@
     levels, rows, cols = x1.shape
     npatch = rows // PATCH
     nslot = groups * slots_per
-    mine = x1.reshape(levels, npatch, PATCH, cols)
+    mine = x1.reshape(levels, npatch, PATCH, cols).transpose(0, 2, 1, 3)
     other = swap_sec(mine)
     sent = pick(send_sel, mine)
     local = pick(recv_sel, other)
@@ -96,7 +96,7 @@
     for_other = spread(recv_sel, KAPPA * arrived)
     for_mine = spread(send_sel, answer * jnp.tanh(sent))
     updated = mine + swap_sec(for_other) + for_mine
-    return updated.reshape(levels, rows, cols)
+    return updated.transpose(0, 2, 1, 3).reshape(levels, rows, cols)
 
 
 def body(adjoint_state, forcing, viscosity, reaction, source_patch, owner, cavity_map):

time: 221 us -> 221 us (level)
  no operation moved by 1% of the time
where the time goes in v7:
time: 221 us; the launch traced here: 219 us
  blocking collectives  132 us (60%)
  starting transfers between devices  24.8 us (11%)
  other arithmetic  21.8 us (10%)
  waiting for transfers between devices  16.6 us (8%)
  local copies, waits for them, and re-layouts  16.4 us (7%)
  matrix products  6.99 us (3%)
    all_to_all x1, blocking collectives, couple(): incoming = lax.all_to_all(outgoing, ('gx', 'gy'), 0, 0, tiled=True)  132 us
    ppermute x8, starting transfers between devices, shifted(): return lax.ppermute(block, ('gx', 'gy'), pairs)  24.1 us
    ppermute x8, waiting for transfers between devices, shifted(): return lax.ppermute(block, ('gx', 'gy'), pairs)  16.5 us
    add x6, other arithmetic, relax(): return (1.0 - OMEGA) * field + OMEGA * invd * (force + visc * beside)  5.14 us
  transfers between devices with their start and end apart: 11, of which 5 were waited for; matrix products, arithmetic and copies ran while one was open for 9% of the time, Pallas kernels for 0%

profile of v7, /device:TPU:54, one launch (start us, length us, event | category | flops | bytes accessed | tf_op | source)
XLA Modules:
  0.0 218.8 jit_solution(508470238125787108)
XLA Ops:
  1.5 1.4 pad_maximum_fusion.2
  3.5 1.1 copy.30
  4.5 3.8 %collective-permute-start = (f32[22,128,4]{1,2,0:T(4,128)}, f32[22,128,4]{1,2,0:T(4,128)S(1)}, u32[]{:S(2)}, u32[]{:S(2)}) collective-permute-start(f32[22,128,4]{1,2,0:T(4,128)} %copy.30), channel_id=1, source_target_pairs={{0,1},{1,2},{2,3},{3,4},{4,5},{5,6},{6,7},{8,9},{9,10},{10,11},{11... | collective-permute-start | bytes 135176 | tf_op jit(solution)/shard_map/ppermute | solution.py:25
  8.8 2.1 collective-permute-start.1
  11.4 3.5 %collective-permute-done.1 = f32[22,128,4]{1,2,0:T(4,128)} collective-permute-done((f32[22,128,4]{1,2,0:T(4,128)S(1)}, f32[22,128,4]{1,2,0:T(4,128)}, u32[]{:S(2)}, u32[]{:S(2)}) %collective-permute-start.1) | collective-permute-done | bytes 45088 | tf_op jit(solution)/shard_map/ppermute | solution.py:25
  15.0 1.2 copy.33
  16.3 1.9 pad_maximum_fusion.9
  18.2 3.1 %collective-permute-start.2 = (f32[22,4,136]{2,1,0:T(4,128)}, f32[22,4,136]{2,1,0:T(4,128)S(1)}, u32[]{:S(2)}, u32[]{:S(2)}) collective-permute-start(f32[22,4,136]{2,1,0:T(4,128)} %get-tuple-element.7), channel_id=1, source_target_pairs={{0,8},{1,9},{2,10},{3,11},{4,12},{5,13},{6,14},{7,15},{8,16},{9,17... | collective-permute-start | bytes 143624 | tf_op jit(solution)/shard_map/ppermute | solution.py:25
  21.3 2.7 %collective-permute-start.3 = (f32[22,4,136]{2,1,0:T(4,128)}, f32[22,4,136]{2,1,0:T(4,128)S(1)}, u32[]{:S(2)}, u32[]{:S(2)}) collective-permute-start(f32[22,4,136]{2,1,0:T(4,128)} %get-tuple-element.8), channel_id=1, source_target_pairs={{8,0},{9,1},{10,2},{11,3},{12,4},{13,5},{14,6},{15,7},{16,8},{17,9... | collective-permute-start | bytes 143624 | tf_op jit(solution)/shard_map/ppermute | solution.py:25
  24.8 5.2 %collective-permute-done.3 = f32[22,4,136]{2,1,0:T(4,128)S(1)} collective-permute-done((f32[22,4,136]{2,1,0:T(4,128)}, f32[22,4,136]{2,1,0:T(4,128)S(1)}, u32[]{:S(2)}, u32[]{:S(2)}) %collective-permute-start.3) | collective-permute-done | bytes 47904 | tf_op jit(solution)/shard_map/ppermute | solution.py:25
  30.0 3.5 %pad_maximum_fusion.1 = f32[22,136,136]{2,1,0:T(8,128)S(1)} fusion(f32[22,4,136]{2,1,0:T(4,128)S(1)} %collective-permute-done.3, f32[22,128,4]{2,1,0:T(8,128)} %copy-done.3, f32[1,128,128]{2,1,0:T(8,128)} %copy-done.8, f32[1,128,128]{2,1,0:T(8,128)} %param.9, f32[10,128,128]{2,1,0:T(8,128)} %bitcast.55, f32[10,128,128]{2,1,0:T(8,128)} %bitcast.59, ...), kind=kLoop, calls=%fused_computation.1 | loop fusion | flops 2848384 | bytes 3255296 | tf_op jit(solution)/shard_map/concatenate | solution.py:34
  37.3 1.1 fusion.13
  39.2 2.3 %fusion.27 = f32[256,10,2,128]{3,0,2,1:T(8,128)S(1)} fusion(f32[256,64,1,1]{0,1,3,2:T(8,128)S(1)} %convolution_bitcast_fusion, f32[10,64,2,128]{3,2,1,0:T(2,128)S(1)} %bitcast.48), kind=kOutput, calls=%fused_computation.74 | convolution fusion | flops 503316480 | bytes 3342336 | tf_op jit(solution)/shard_map/jk,lrkc->jlrc/dot_general | solution.py:59
  41.5 2.0 copy.35
  43.6 1.2 fusion.22
  44.8 2.0 copy.37
  47.3 131.8 %all_to_all.5 = f32[128,80,128]{2,1,0:T(8,128)S(1)} all-to-all(f32[128,80,128]{2,1,0:T(8,128)S(1)} %pad_maximum_fusion), channel_id=1, replica_groups=mesh['sec'=2,'gx'=16,'gy'=8] {'gx','gy'}, dimensions={0} | all-to-all | bytes 10485760 | tf_op jit(solution)/shard_map/all_to_all | solution.py:93
  179.4 1.2 fusion.5
  180.8 2.1 fusion.4
  184.5 1.3 fusion.30
  185.7 1.3 copy.41
  187.0 2.6 %collective-permute-start.7 = (f32[10,128,4]{1,2,0:T(4,128)S(1)}, f32[10,128,4]{1,2,0:T(4,128)S(1)}, u32[]{:S(2)}, u32[]{:S(2)}) collective-permute-start(f32[10,128,4]{1,2,0:T(4,128)S(1)} %copy.41), channel_id=1, source_target_pairs={{0,1},{1,2},{2,3},{3,4},{4,5},{5,6},{6,7},{8,9},{9,10},{10,11},{11... | collective-permute-start | bytes 61448 | tf_op jit(solution)/shard_map/ppermute | solution.py:25
  189.6 1.3 copy.42
  190.9 3.2 %collective-permute-start.8 = (f32[10,128,4]{1,2,0:T(4,128)S(1)}, f32[10,128,4]{1,2,0:T(4,128)S(1)}, u32[]{:S(2)}, u32[]{:S(2)}) collective-permute-start(f32[10,128,4]{1,2,0:T(4,128)S(1)} %copy.42), channel_id=1, source_target_pairs={{1,0},{2,1},{3,2},{4,3},{5,4},{6,5},{7,6},{9,8},{10,9},{11,10},{12... | collective-permute-start | bytes 61448 | tf_op jit(solution)/shard_map/ppermute | solution.py:25
  194.2 1.1 copy.43
  195.3 1.3 collective-permute-done.8
  196.6 1.1 copy.44
  197.7 1.2 pad_maximum_fusion.12
  198.9 4.6 %collective-permute-start.9 = (f32[10,4,136]{2,1,0:T(4,128)S(1)}, f32[10,4,136]{2,1,0:T(4,128)S(1)}, u32[]{:S(2)}, u32[]{:S(2)}) collective-permute-start(f32[10,4,136]{2,1,0:T(4,128)S(1)} %get-tuple-element.13), channel_id=1, source_target_pairs={{0,8},{1,9},{2,10},{3,11},{4,12},{5,13},{6,14},{7,15},{8,16},{9,17... | collective-permute-start | bytes 65288 | tf_op jit(solution)/shard_map/ppermute | solution.py:25
  203.5 1.9 collective-permute-start.10
  205.4 6.1 %collective-permute-done.10 = f32[10,4,136]{2,1,0:T(4,128)S(1)} collective-permute-done((f32[10,4,136]{2,1,0:T(4,128)S(1)}, f32[10,4,136]{2,1,0:T(4,128)S(1)}, u32[]{:S(2)}, u32[]{:S(2)}) %collective-permute-start.10) | collective-permute-done | bytes 21792 | tf_op jit(solution)/shard_map/ppermute | solution.py:25
  215.5 3.3 %fusion.9 = f32[1,10,128,128]{3,2,1,0:T(8,128)} fusion(f32[10,136,136]{2,1,0:T(8,128)S(1)} %multiply_add_fusion, f32[10,136,136]{2,1,0:T(8,128)S(1)} %get-tuple-element.19, f32[10,136,136]{2,1,0:T(8,128)S(1)} %get-tuple-element.18, f32[10,136,136]{2,1,0:T(8,128)S(1)} %get-tuple-element.17, f32[10,136,136]{2,1,0:T(8,128)} %copy-done.7, ...), kind=kLoop, calls=%fused_computation.33 | loop fusion | flops 1146880 | bytes 4063232 | tf_op jit(solution)/shard_map/broadcast_in_dim | solution.py:116
  (61 shorter events, 14.8 us)
Async XLA Ops:
  0.9 0.6 copy-start.8
  4.5 6.4 %collective-permute-start = (f32[22,128,4]{1,2,0:T(4,128)}, f32[22,128,4]{1,2,0:T(4,128)S(1)}, u32[]{:S(2)}, u32[]{:S(2)}) collective-permute-start(f32[22,128,4]{1,2,0:T(4,128)} %copy.30), channel_id=1, source_target_pairs={{0,1},{1,2},{2,3},{3,4},{4,5},{5,6},{6,7},{8,9},{9,10},{10,11},{11... | collective-permute-start | bytes 135176 | tf_op jit(solution)/shard_map/ppermute | solution.py:25
  8.8 7.4 %copy-start.6 = (f32[1,10,128,128]{3,2,1,0:T(8,128)S(1)}, f32[1,10,128,128]{3,2,1,0:T(8,128)}, u32[]{:S(2)}) copy-start(f32[1,10,128,128]{3,2,1,0:T(8,128)} %param.8) | copy-start | bytes 1966084
  8.8 6.2 %collective-permute-start.1 = (f32[22,128,4]{1,2,0:T(4,128)S(1)}, f32[22,128,4]{1,2,0:T(4,128)}, u32[]{:S(2)}, u32[]{:S(2)}) collective-permute-start(f32[22,128,4]{1,2,0:T(4,128)S(1)} %copy.31), channel_id=1, source_target_pairs={{1,0},{2,1},{3,2},{4,3},{5,4},{6,5},{7,6},{9,8},{10,9},{11,10},{12... | collective-permute-start | bytes 135176 | tf_op jit(solution)/shard_map/ppermute | solution.py:25
  11.4 6.8 %copy-start.2 = (f32[22,128,4]{2,1,0:T(8,128)}, f32[22,128,4]{2,1,0:T(8,128)S(1)}, u32[]{:S(2)}) copy-start(f32[22,128,4]{2,1,0:T(8,128)S(1)} %copy.32) | copy-start | bytes 135172
  16.2 2.0 copy-start.3
  16.2 7.8 %copy-start.9 = (s32[1,1,128,2]{2,3,1,0:T(2,128)S(1)}, s32[1,1,128,2]{2,3,1,0:T(2,128)}, u32[]{:S(2)}) copy-start(s32[1,1,128,2]{2,3,1,0:T(2,128)} %param.13) | copy-start | bytes 3076
  18.2 6.6 %collective-permute-start.2 = (f32[22,4,136]{2,1,0:T(4,128)}, f32[22,4,136]{2,1,0:T(4,128)S(1)}, u32[]{:S(2)}, u32[]{:S(2)}) collective-permute-start(f32[22,4,136]{2,1,0:T(4,128)} %get-tuple-element.7), channel_id=1, source_target_pairs={{0,8},{1,9},{2,10},{3,11},{4,12},{5,13},{6,14},{7,15},{8,16},{9,17... | collective-permute-start | bytes 143624 | tf_op jit(solution)/shard_map/ppermute | solution.py:25
  21.3 8.7 %collective-permute-start.3 = (f32[22,4,136]{2,1,0:T(4,128)}, f32[22,4,136]{2,1,0:T(4,128)S(1)}, u32[]{:S(2)}, u32[]{:S(2)}) collective-permute-start(f32[22,4,136]{2,1,0:T(4,128)} %get-tuple-element.8), channel_id=1, source_target_pairs={{8,0},{9,1},{10,2},{11,3},{12,4},{13,5},{14,6},{15,7},{16,8},{17,9... | collective-permute-start | bytes 143624 | tf_op jit(solution)/shard_map/ppermute | solution.py:25
  24.3 19.2 %collective-permute-start.4 = (s32[256]{0:T(256)S(1)}, s32[256]{0:T(256)S(1)}, u32[]{:S(2)}, u32[]{:S(2)}) collective-permute-start(s32[256]{0:T(256)S(1)} %reshape_squeeze.3), channel_id=1, source_target_pairs={{0,128},{128,0},{1,129},{129,1},{2,130},{130,2},{3,131},{131,3},{4... | collective-permute-start | bytes 3080 | tf_op jit(solution)/shard_map/ppermute | solution.py:51
  34.7 2.6 %copy-start.7 = (f32[10,136,136]{2,1,0:T(8,128)}, f32[10,136,136]{2,1,0:T(8,128)S(1)}, u32[]{:S(2)}) copy-start(f32[10,136,136]{2,1,0:T(8,128)S(1)} %get-tuple-element.9) | copy-start | bytes 2219524
  37.3 1.5 copy-start.10
  37.3 1.6 copy-start.11
  38.5 5.1 %collective-permute-start.5 = (f32[10,2,64,128]{3,2,1,0:T(8,128)S(1)}, f32[10,2,64,128]{3,2,1,0:T(8,128)S(1)}, u32[]{:S(2)}, u32[]{:S(2)}) collective-permute-start(f32[10,2,64,128]{3,2,1,0:T(8,128)S(1)} %bitcast.60), channel_id=1, source_target_pairs={{0,128},{128,0},{1,129},{129,1},{2,130},{130,2},{3,131},{131,3},{4... | collective-permute-start | bytes 1966088 | tf_op jit(solution)/shard_map/ppermute | solution.py:51
  180.5 2.4 %collective-permute-start.6 = (f32[10,2,64,128]{3,2,1,0:T(8,128)S(1)}, f32[10,2,64,128]{3,2,1,0:T(8,128)S(1)}, u32[]{:S(2)}, u32[]{:S(2)}) collective-permute-start(f32[10,2,64,128]{3,2,1,0:T(8,128)S(1)} %fusion.5), channel_id=1, source_target_pairs={{0,128},{128,0},{1,129},{129,1},{2,130},{130,2},{3,131},{131,3},{4... | collective-permute-start | bytes 1966088 | tf_op jit(solution)/shard_map/ppermute | solution.py:51
  183.6 0.8 copy-start
  187.0 7.2 %collective-permute-start.7 = (f32[10,128,4]{1,2,0:T(4,128)S(1)}, f32[10,128,4]{1,2,0:T(4,128)S(1)}, u32[]{:S(2)}, u32[]{:S(2)}) collective-permute-start(f32[10,128,4]{1,2,0:T(4,128)S(1)} %copy.41), channel_id=1, source_target_pairs={{0,1},{1,2},{2,3},{3,4},{4,5},{5,6},{6,7},{8,9},{9,10},{10,11},{11... | collective-permute-start | bytes 61448 | tf_op jit(solution)/shard_map/ppermute | solution.py:25
  190.9 5.7 %collective-permute-start.8 = (f32[10,128,4]{1,2,0:T(4,128)S(1)}, f32[10,128,4]{1,2,0:T(4,128)S(1)}, u32[]{:S(2)}, u32[]{:S(2)}) collective-permute-start(f32[10,128,4]{1,2,0:T(4,128)S(1)} %copy.42), channel_id=1, source_target_pairs={{1,0},{2,1},{3,2},{4,3},{5,4},{6,5},{7,6},{9,8},{10,9},{11,10},{12... | collective-permute-start | bytes 61448 | tf_op jit(solution)/shard_map/ppermute | solution.py:25
  197.7 13.8 %copy-start.1 = (f32[10,64,2,128]{3,2,1,0:T(2,128)S(1)}, f32[10,64,2,128]{3,2,1,0:T(2,128)}, u32[]{:S(2)}) copy-start(f32[10,64,2,128]{3,2,1,0:T(2,128)} %copy-done) | copy-start | bytes 1966084
  197.7 13.8 %copy-start.4 = (f32[10,128,4]{2,1,0:T(8,128)S(1)}, f32[10,128,4]{2,1,0:T(8,128)}, u32[]{:S(2)}) copy-start(f32[10,128,4]{2,1,0:T(8,128)} %copy.43) | copy-start | bytes 61444
  197.7 13.8 %copy-start.5 = (f32[10,128,4]{2,1,0:T(8,128)S(1)}, f32[10,128,4]{2,1,0:T(8,128)}, u32[]{:S(2)}) copy-start(f32[10,128,4]{2,1,0:T(8,128)} %copy.44) | copy-start | bytes 61444
  198.9 6.5 %collective-permute-start.9 = (f32[10,4,136]{2,1,0:T(4,128)S(1)}, f32[10,4,136]{2,1,0:T(4,128)S(1)}, u32[]{:S(2)}, u32[]{:S(2)}) collective-permute-start(f32[10,4,136]{2,1,0:T(4,128)S(1)} %get-tuple-element.13), channel_id=1, source_target_pairs={{0,8},{1,9},{2,10},{3,11},{4,12},{5,13},{6,14},{7,15},{8,16},{9,17... | collective-permute-start | bytes 65288 | tf_op jit(solution)/shard_map/ppermute | solution.py:25
  203.5 8.0 %collective-permute-start.10 = (f32[10,4,136]{2,1,0:T(4,128)S(1)}, f32[10,4,136]{2,1,0:T(4,128)S(1)}, u32[]{:S(2)}, u32[]{:S(2)}) collective-permute-start(f32[10,4,136]{2,1,0:T(4,128)S(1)} %get-tuple-element.14), channel_id=1, source_target_pairs={{8,0},{9,1},{10,2},{11,3},{12,4},{13,5},{14,6},{15,7},{16,8},{17,9... | collective-permute-start | bytes 65288 | tf_op jit(solution)/shard_map/ppermute | solution.py:25

commit v8 on v3

--- a/solution.py
+++ b/solution.py
@@ -42,9 +42,12 @@
 
 
 def sweeps(ext, visc, invd, force, count, w):
-    for _ in range(count):
+    for _ in range(count - 1):
         ext = relax(ext, visc, invd, force)
-    return ext[:, w:-w, w:-w]
+    inner = (slice(None), slice(w, -w), slice(w, -w))
+    beside = ext[:, w + 1:-w + 1, w:-w] + ext[:, w - 1:-w - 1, w:-w]
+    beside = beside + ext[:, w:-w, w + 1:-w + 1] + ext[:, w:-w, w - 1:-w - 1]
+    return (1.0 - OMEGA) * ext[inner] + OMEGA * invd[inner] * (force[inner] + visc[inner] * beside)
 
 
 def swap_sec(x):

time: 221 us -> 219 us (level)
  other arithmetic: 21.1 us -> 17.4 us
  transfers between devices with their start and end apart: 11 -> 11, of which waited for: 5 -> 5; matrix products, arithmetic and copies ran while one was open for 9% -> 8% of each run, Pallas kernels for 0% -> 0%
where the time goes in v8:
time: 219 us; the launch traced here: 216 us
  blocking collectives  132 us (60%)
  starting transfers between devices  24.8 us (11%)
  local copies, waits for them, and re-layouts  19 us (9%)
  other arithmetic  17.4 us (8%)
  waiting for transfers between devices  15.7 us (7%)
  matrix products  6.99 us (3%)
    all_to_all x1, blocking collectives, couple(): incoming = lax.all_to_all(outgoing, ('gx', 'gy'), 0, 0, tiled=True)  132 us
    ppermute x8, starting transfers between devices, shifted(): return lax.ppermute(block, ('gx', 'gy'), pairs)  24.1 us
    ppermute x8, waiting for transfers between devices, shifted(): return lax.ppermute(block, ('gx', 'gy'), pairs)  15.7 us
    slice x4, local copies, waits for them, and re-layouts, halo(): west = shifted(cells[:, :, -w:], 0, -1)  5.98 us
    add x6, other arithmetic, relax(): return (1.0 - OMEGA) * field + OMEGA * invd * (force + visc * beside)  4.91 us
  transfers between devices with their start and end apart: 11, of which 5 were waited for; matrix products, arithmetic and copies ran while one was open for 8% of the time, Pallas kernels for 0%

profile of v8, /device:TPU:54, one launch (start us, length us, event | category | flops | bytes accessed | tf_op | source)
XLA Modules:
  0.0 216.1 jit_solution(14052455363615110528)
XLA Ops:
  0.9 1.4 pad_maximum_fusion.2
  2.3 1.6 fusion.29
  4.0 1.8 copy.34
  5.7 3.8 %collective-permute-start = (f32[22,128,4]{1,2,0:T(4,128)S(1)}, f32[22,128,4]{1,2,0:T(4,128)S(1)}, u32[]{:S(2)}, u32[]{:S(2)}) collective-permute-start(f32[22,128,4]{1,2,0:T(4,128)S(1)} %copy.34), channel_id=1, source_target_pairs={{0,1},{1,2},{2,3},{3,4},{4,5},{5,6},{6,7},{8,9},{9,10},{10,11},{11... | collective-permute-start | bytes 135176 | tf_op jit(solution)/shard_map/ppermute | solution.py:25
  10.0 2.1 collective-permute-start.1
  12.7 3.4 %collective-permute-done.1 = f32[22,128,4]{1,2,0:T(4,128)S(1)} collective-permute-done((f32[22,128,4]{1,2,0:T(4,128)S(1)}, f32[22,128,4]{1,2,0:T(4,128)S(1)}, u32[]{:S(2)}, u32[]{:S(2)}) %collective-permute-start.1) | collective-permute-done | bytes 45088 | tf_op jit(solution)/shard_map/ppermute | solution.py:25
  16.1 1.6 copy.37
  17.7 1.1 pad_maximum_fusion.9
  18.9 3.1 %collective-permute-start.2 = (f32[22,4,136]{2,1,0:T(4,128)S(1)}, f32[22,4,136]{2,1,0:T(4,128)S(1)}, u32[]{:S(2)}, u32[]{:S(2)}) collective-permute-start(f32[22,4,136]{2,1,0:T(4,128)S(1)} %get-tuple-element.9), channel_id=1, source_target_pairs={{0,8},{1,9},{2,10},{3,11},{4,12},{5,13},{6,14},{7,15},{8,16},{9,17... | collective-permute-start | bytes 143624 | tf_op jit(solution)/shard_map/ppermute | solution.py:25
  22.0 2.7 %collective-permute-start.3 = (f32[22,4,136]{2,1,0:T(4,128)S(1)}, f32[22,4,136]{2,1,0:T(4,128)}, u32[]{:S(2)}, u32[]{:S(2)}) collective-permute-start(f32[22,4,136]{2,1,0:T(4,128)S(1)} %get-tuple-element.10), channel_id=1, source_target_pairs={{8,0},{9,1},{10,2},{11,3},{12,4},{13,5},{14,6},{15,7},{16,8},{17,9... | collective-permute-start | bytes 143624 | tf_op jit(solution)/shard_map/ppermute | solution.py:25
  25.9 4.7 %collective-permute-done.3 = f32[22,4,136]{2,1,0:T(4,128)} collective-permute-done((f32[22,4,136]{2,1,0:T(4,128)S(1)}, f32[22,4,136]{2,1,0:T(4,128)}, u32[]{:S(2)}, u32[]{:S(2)}) %collective-permute-start.3) | collective-permute-done | bytes 47904 | tf_op jit(solution)/shard_map/ppermute | solution.py:25
  30.6 3.5 %pad_maximum_fusion.1 = f32[22,136,136]{2,1,0:T(8,128)S(1)} fusion(f32[22,4,136]{2,1,0:T(4,128)} %collective-permute-done.3, f32[22,128,4]{2,1,0:T(8,128)} %copy.37, f32[1,128,128]{2,1,0:T(8,128)S(1)} %get-tuple-element.6, f32[1,128,128]{2,1,0:T(8,128)S(1)} %copy-done.9, f32[10,128,128]{2,1,0:T(8,128)} %bitcast.45, f32[10,128,128]{2,1,0:T(8,128)} %bitcast.55, ...), kind=kLoop, calls=%fused_computation.1 | loop fusion | flops 2848384 | bytes 3255296 | tf_op jit(solution)/shard_map/concatenate | solution.py:34
  38.7 2.3 %fusion.27 = f32[256,10,2,128]{3,0,2,1:T(8,128)S(1)} fusion(f32[256,64,1,1]{0,1,3,2:T(8,128)S(1)} %convolution_bitcast_fusion, f32[10,64,2,128]{3,2,1,0:T(2,128)S(1)} %bitcast.48), kind=kOutput, calls=%fused_computation.70 | convolution fusion | flops 503316480 | bytes 3342336 | tf_op jit(solution)/shard_map/jk,lkrc->jlrc/dot_general | solution.py:62
  41.0 2.0 copy.39
  43.1 1.2 fusion.22
  44.3 2.0 copy.42
  46.8 131.8 %all_to_all.5 = f32[128,80,128]{2,1,0:T(8,128)S(1)} all-to-all(f32[128,80,128]{2,1,0:T(8,128)S(1)} %pad_maximum_fusion), channel_id=1, replica_groups=mesh['sec'=2,'gx'=16,'gy'=8] {'gx','gy'}, dimensions={0} | all-to-all | bytes 10485760 | tf_op jit(solution)/shard_map/all_to_all | solution.py:96
  178.9 1.2 fusion.5
  180.4 2.1 fusion.4
  184.0 1.3 fusion.30
  185.2 1.3 copy.47
  186.5 2.6 %collective-permute-start.7 = (f32[10,128,4]{1,2,0:T(4,128)S(1)}, f32[10,128,4]{1,2,0:T(4,128)S(1)}, u32[]{:S(2)}, u32[]{:S(2)}) collective-permute-start(f32[10,128,4]{1,2,0:T(4,128)S(1)} %copy.47), channel_id=1, source_target_pairs={{0,1},{1,2},{2,3},{3,4},{4,5},{5,6},{6,7},{8,9},{9,10},{10,11},{11... | collective-permute-start | bytes 61448 | tf_op jit(solution)/shard_map/ppermute | solution.py:25
  189.1 1.3 copy.48
  190.4 3.3 %collective-permute-start.8 = (f32[10,128,4]{1,2,0:T(4,128)S(1)}, f32[10,128,4]{1,2,0:T(4,128)S(1)}, u32[]{:S(2)}, u32[]{:S(2)}) collective-permute-start(f32[10,128,4]{1,2,0:T(4,128)S(1)} %copy.48), channel_id=1, source_target_pairs={{1,0},{2,1},{3,2},{4,3},{5,4},{6,5},{7,6},{9,8},{10,9},{11,10},{12... | collective-permute-start | bytes 61448 | tf_op jit(solution)/shard_map/ppermute | solution.py:25
  193.7 1.1 copy.49
  194.8 1.3 collective-permute-done.8
  196.1 1.1 copy.50
  197.2 1.2 pad_maximum_fusion.12
  198.4 4.6 %collective-permute-start.9 = (f32[10,4,136]{2,1,0:T(4,128)S(1)}, f32[10,4,136]{2,1,0:T(4,128)S(1)}, u32[]{:S(2)}, u32[]{:S(2)}) collective-permute-start(f32[10,4,136]{2,1,0:T(4,128)S(1)} %get-tuple-element.13), channel_id=1, source_target_pairs={{0,8},{1,9},{2,10},{3,11},{4,12},{5,13},{6,14},{7,15},{8,16},{9,17... | collective-permute-start | bytes 65288 | tf_op jit(solution)/shard_map/ppermute | solution.py:25
  203.0 1.9 collective-permute-start.10
  204.9 6.1 %collective-permute-done.10 = f32[10,4,136]{2,1,0:T(4,128)S(1)} collective-permute-done((f32[10,4,136]{2,1,0:T(4,128)S(1)}, f32[10,4,136]{2,1,0:T(4,128)S(1)}, u32[]{:S(2)}, u32[]{:S(2)}) %collective-permute-start.10) | collective-permute-done | bytes 21792 | tf_op jit(solution)/shard_map/ppermute | solution.py:25
  214.3 1.8 fusion.12
  (61 shorter events, 13.4 us)
Async XLA Ops:
  5.7 6.4 %collective-permute-start = (f32[22,128,4]{1,2,0:T(4,128)S(1)}, f32[22,128,4]{1,2,0:T(4,128)S(1)}, u32[]{:S(2)}, u32[]{:S(2)}) collective-permute-start(f32[22,128,4]{1,2,0:T(4,128)S(1)} %copy.34), channel_id=1, source_target_pairs={{0,1},{1,2},{2,3},{3,4},{4,5},{5,6},{6,7},{8,9},{9,10},{10,11},{11... | collective-permute-start | bytes 135176 | tf_op jit(solution)/shard_map/ppermute | solution.py:25
  10.0 7.7 %copy-start.2 = (f32[1,10,128,128]{3,2,1,0:T(8,128)S(1)}, f32[1,10,128,128]{3,2,1,0:T(8,128)}, u32[]{:S(2)}) copy-start(f32[1,10,128,128]{3,2,1,0:T(8,128)} %param.8) | copy-start | bytes 1966084
  10.0 7.7 %copy-start.8 = (f32[1,10,128,128]{3,2,1,0:T(8,128)S(1)}, f32[1,10,128,128]{3,2,1,0:T(8,128)}, u32[]{:S(2)}) copy-start(f32[1,10,128,128]{3,2,1,0:T(8,128)} %param.7) | copy-start | bytes 1966084
  10.0 7.7 %copy-start.9 = (f32[1,128,128]{2,1,0:T(8,128)S(1)}, f32[1,128,128]{2,1,0:T(8,128)}, u32[]{:S(2)}) copy-start(f32[1,128,128]{2,1,0:T(8,128)} %param.9) | copy-start | bytes 196612
  10.0 6.1 %collective-permute-start.1 = (f32[22,128,4]{1,2,0:T(4,128)S(1)}, f32[22,128,4]{1,2,0:T(4,128)S(1)}, u32[]{:S(2)}, u32[]{:S(2)}) collective-permute-start(f32[22,128,4]{1,2,0:T(4,128)S(1)} %copy.35), channel_id=1, source_target_pairs={{1,0},{2,1},{3,2},{4,3},{5,4},{6,5},{7,6},{9,8},{10,9},{11,10},{12... | collective-permute-start | bytes 135176 | tf_op jit(solution)/shard_map/ppermute | solution.py:25
  12.7 6.2 %copy-start.5 = (f32[22,128,4]{2,1,0:T(8,128)}, f32[22,128,4]{2,1,0:T(8,128)S(1)}, u32[]{:S(2)}) copy-start(f32[22,128,4]{2,1,0:T(8,128)S(1)} %copy.36) | copy-start | bytes 135172
  17.7 7.0 %copy-start.11 = (s32[1,1,128,2]{2,3,1,0:T(2,128)S(1)}, s32[1,1,128,2]{2,3,1,0:T(2,128)}, u32[]{:S(2)}) copy-start(s32[1,1,128,2]{2,3,1,0:T(2,128)} %param.13) | copy-start | bytes 3076
  18.9 6.4 %collective-permute-start.2 = (f32[22,4,136]{2,1,0:T(4,128)S(1)}, f32[22,4,136]{2,1,0:T(4,128)S(1)}, u32[]{:S(2)}, u32[]{:S(2)}) collective-permute-start(f32[22,4,136]{2,1,0:T(4,128)S(1)} %get-tuple-element.9), channel_id=1, source_target_pairs={{0,8},{1,9},{2,10},{3,11},{4,12},{5,13},{6,14},{7,15},{8,16},{9,17... | collective-permute-start | bytes 143624 | tf_op jit(solution)/shard_map/ppermute | solution.py:25
  22.0 8.6 %collective-permute-start.3 = (f32[22,4,136]{2,1,0:T(4,128)S(1)}, f32[22,4,136]{2,1,0:T(4,128)}, u32[]{:S(2)}, u32[]{:S(2)}) collective-permute-start(f32[22,4,136]{2,1,0:T(4,128)S(1)} %get-tuple-element.10), channel_id=1, source_target_pairs={{8,0},{9,1},{10,2},{11,3},{12,4},{13,5},{14,6},{15,7},{16,8},{17,9... | collective-permute-start | bytes 143624 | tf_op jit(solution)/shard_map/ppermute | solution.py:25
  25.0 18.1 %collective-permute-start.4 = (s32[256]{0:T(256)S(1)}, s32[256]{0:T(256)S(1)}, u32[]{:S(2)}, u32[]{:S(2)}) collective-permute-start(s32[256]{0:T(256)S(1)} %reshape_squeeze.3), channel_id=1, source_target_pairs={{0,128},{128,0},{1,129},{129,1},{2,130},{130,2},{3,131},{131,3},{4... | collective-permute-start | bytes 3080 | tf_op jit(solution)/shard_map/ppermute | solution.py:54
  25.3 0.6 copy-start.10
  35.9 1.1 copy-start.3
  37.0 1.3 copy-start.12
  37.0 1.5 copy-start.13
  38.0 5.1 %collective-permute-start.5 = (f32[10,64,2,128]{3,1,2,0:T(8,128)S(1)}, f32[10,64,2,128]{3,1,2,0:T(8,128)S(1)}, u32[]{:S(2)}, u32[]{:S(2)}) collective-permute-start(f32[10,64,2,128]{3,1,2,0:T(8,128)S(1)} %copy.44), channel_id=1, source_target_pairs={{0,128},{128,0},{1,129},{129,1},{2,130},{130,2},{3,131},{131,3},{4... | collective-permute-start | bytes 1966088 | tf_op jit(solution)/shard_map/ppermute | solution.py:54
  180.0 2.4 %collective-permute-start.6 = (f32[10,64,2,128]{3,1,2,0:T(8,128)S(1)}, f32[10,64,2,128]{3,1,2,0:T(8,128)S(1)}, u32[]{:S(2)}, u32[]{:S(2)}) collective-permute-start(f32[10,64,2,128]{3,1,2,0:T(8,128)S(1)} %fusion.5), channel_id=1, source_target_pairs={{0,128},{128,0},{1,129},{129,1},{2,130},{130,2},{3,131},{131,3},{4... | collective-permute-start | bytes 1966088 | tf_op jit(solution)/shard_map/ppermute | solution.py:54
  183.1 0.8 copy-start
  186.5 7.2 %collective-permute-start.7 = (f32[10,128,4]{1,2,0:T(4,128)S(1)}, f32[10,128,4]{1,2,0:T(4,128)S(1)}, u32[]{:S(2)}, u32[]{:S(2)}) collective-permute-start(f32[10,128,4]{1,2,0:T(4,128)S(1)} %copy.47), channel_id=1, source_target_pairs={{0,1},{1,2},{2,3},{3,4},{4,5},{5,6},{6,7},{8,9},{9,10},{10,11},{11... | collective-permute-start | bytes 61448 | tf_op jit(solution)/shard_map/ppermute | solution.py:25
  190.4 5.7 %collective-permute-start.8 = (f32[10,128,4]{1,2,0:T(4,128)S(1)}, f32[10,128,4]{1,2,0:T(4,128)S(1)}, u32[]{:S(2)}, u32[]{:S(2)}) collective-permute-start(f32[10,128,4]{1,2,0:T(4,128)S(1)} %copy.48), channel_id=1, source_target_pairs={{1,0},{2,1},{3,2},{4,3},{5,4},{6,5},{7,6},{9,8},{10,9},{11,10},{12... | collective-permute-start | bytes 61448 | tf_op jit(solution)/shard_map/ppermute | solution.py:25
  197.2 13.8 %copy-start.1 = (f32[10,64,2,128]{3,2,1,0:T(2,128)S(1)}, f32[10,64,2,128]{3,2,1,0:T(2,128)}, u32[]{:S(2)}) copy-start(f32[10,64,2,128]{3,2,1,0:T(2,128)} %copy-done) | copy-start | bytes 1966084
  197.2 13.8 %copy-start.6 = (f32[10,128,4]{2,1,0:T(8,128)S(1)}, f32[10,128,4]{2,1,0:T(8,128)}, u32[]{:S(2)}) copy-start(f32[10,128,4]{2,1,0:T(8,128)} %copy.49) | copy-start | bytes 61444
  197.2 13.8 %copy-start.7 = (f32[10,128,4]{2,1,0:T(8,128)S(1)}, f32[10,128,4]{2,1,0:T(8,128)}, u32[]{:S(2)}) copy-start(f32[10,128,4]{2,1,0:T(8,128)} %copy.50) | copy-start | bytes 61444
  198.4 6.5 %collective-permute-start.9 = (f32[10,4,136]{2,1,0:T(4,128)S(1)}, f32[10,4,136]{2,1,0:T(4,128)S(1)}, u32[]{:S(2)}, u32[]{:S(2)}) collective-permute-start(f32[10,4,136]{2,1,0:T(4,128)S(1)} %get-tuple-element.13), channel_id=1, source_target_pairs={{0,8},{1,9},{2,10},{3,11},{4,12},{5,13},{6,14},{7,15},{8,16},{9,17... | collective-permute-start | bytes 65288 | tf_op jit(solution)/shard_map/ppermute | solution.py:25
  203.0 8.0 %collective-permute-start.10 = (f32[10,4,136]{2,1,0:T(4,128)S(1)}, f32[10,4,136]{2,1,0:T(4,128)S(1)}, u32[]{:S(2)}, u32[]{:S(2)}) collective-permute-start(f32[10,4,136]{2,1,0:T(4,128)S(1)} %get-tuple-element.14), channel_id=1, source_target_pairs={{8,0},{9,1},{10,2},{11,3},{12,4},{13,5},{14,6},{15,7},{16,8},{17,9... | collective-permute-start | bytes 65288 | tf_op jit(solution)/shard_map/ppermute | solution.py:25
  213.2 1.1 copy-start.4

commit v9 on v3

--- a/solution.py
+++ b/solution.py
@@ -42,9 +42,14 @@
 
 
 def sweeps(ext, visc, invd, force, count, w):
-    for _ in range(count):
-        ext = relax(ext, visc, invd, force)
-    return ext[:, w:-w, w:-w]
+    height, width = ext.shape[1:]
+    for k in range(1, count + 1):
+        rows, cols = slice(k, height - k), slice(k, width - k)
+        beside = ext[:, 2:, 1:-1] + ext[:, :-2, 1:-1]
+        beside = beside + ext[:, 1:-1, 2:] + ext[:, 1:-1, :-2]
+        center = ext[:, 1:-1, 1:-1]
+        ext = (1.0 - OMEGA) * center + OMEGA * invd[:, rows, cols] * (force[:, rows, cols] + visc[:, rows, cols] * beside)
+    return ext
 
 
 def swap_sec(x):

time: 221 us -> 228 us (1.032)
  local copies, waits for them, and re-layouts: 16.9 us -> 20.6 us
  other arithmetic: 21.1 us -> 24.5 us
    add x8 -> x7, other arithmetic: 7.05 us -> 12.2 us  [sweeps(): (1.0 - OMEGA) * center]
    ppermute x4, local copies, waits for them, and re-layouts: 3.14 us -> 5.77 us  [shifted(): return lax.ppermute(block, ('gx', 'gy'), pairs)]
  transfers between devices with their start and end apart: 11 -> 11, of which waited for: 5 -> 5; matrix products, arithmetic and copies ran while one was open for 9% -> 10% of each run, Pallas kernels for 0% -> 0%
where the time goes in v9:
time: 228 us; the launch traced here: 226 us
  blocking collectives  132 us (58%)
  starting transfers between devices  25.9 us (11%)
  other arithmetic  24.5 us (11%)
  local copies, waits for them, and re-layouts  20.6 us (9%)
  waiting for transfers between devices  15.2 us (7%)
  matrix products  6.99 us (3%)
    all_to_all x1, blocking collectives, couple(): incoming = lax.all_to_all(outgoing, ('gx', 'gy'), 0, 0, tiled=True)  132 us
    ppermute x8, starting transfers between devices, shifted(): return lax.ppermute(block, ('gx', 'gy'), pairs)  25.2 us
    ppermute x8, waiting for transfers between devices, shifted(): return lax.ppermute(block, ('gx', 'gy'), pairs)  15.2 us
    add x7, other arithmetic, sweeps(): (1.0 - OMEGA) * center  12.2 us
    slice x4, local copies, waits for them, and re-layouts, halo(): west = shifted(cells[:, :, -w:], 0, -1)  6.63 us
    ppermute x4, local copies, waits for them, and re-layouts, shifted(): return lax.ppermute(block, ('gx', 'gy'), pairs)  5.77 us
  transfers between devices with their start and end apart: 11, of which 5 were waited for; matrix products, arithmetic and copies ran while one was open for 10% of the time, Pallas kernels for 0%

profile of v9, /device:TPU:54, one launch (start us, length us, event | category | flops | bytes accessed | tf_op | source)
XLA Modules:
  0.0 225.6 jit_solution(13188771517494013896)
XLA Ops:
  0.0 1.5 multiply_bitcast_fusion
  2.9 1.7 fusion.55
  4.6 1.8 copy.34
  6.4 3.8 %collective-permute-start = (f32[22,128,4]{1,2,0:T(4,128)S(1)}, f32[22,128,4]{1,2,0:T(4,128)S(1)}, u32[]{:S(2)}, u32[]{:S(2)}) collective-permute-start(f32[22,128,4]{1,2,0:T(4,128)S(1)} %copy.34), channel_id=1, source_target_pairs={{0,1},{1,2},{2,3},{3,4},{4,5},{5,6},{6,7},{8,9},{9,10},{10,11},{11... | collective-permute-start | bytes 135176 | tf_op jit(solution)/shard_map/ppermute | solution.py:25
  10.7 2.1 collective-permute-start.1
  13.3 3.4 %collective-permute-done.1 = f32[22,128,4]{1,2,0:T(4,128)S(1)} collective-permute-done((f32[22,128,4]{1,2,0:T(4,128)S(1)}, f32[22,128,4]{1,2,0:T(4,128)S(1)}, u32[]{:S(2)}, u32[]{:S(2)}) %collective-permute-start.1) | collective-permute-done | bytes 45088 | tf_op jit(solution)/shard_map/ppermute | solution.py:25
  16.8 1.6 copy.37
  19.6 3.1 %collective-permute-start.2 = (f32[22,4,136]{2,1,0:T(4,128)S(1)}, f32[22,4,136]{2,1,0:T(4,128)S(1)}, u32[]{:S(2)}, u32[]{:S(2)}) collective-permute-start(f32[22,4,136]{2,1,0:T(4,128)S(1)} %get-tuple-element.9), channel_id=1, source_target_pairs={{0,8},{1,9},{2,10},{3,11},{4,12},{5,13},{6,14},{7,15},{8,16},{9,17... | collective-permute-start | bytes 143624 | tf_op jit(solution)/shard_map/ppermute | solution.py:25
  22.7 2.7 %collective-permute-start.3 = (f32[22,4,136]{2,1,0:T(4,128)S(1)}, f32[22,4,136]{2,1,0:T(4,128)S(1)}, u32[]{:S(2)}, u32[]{:S(2)}) collective-permute-start(f32[22,4,136]{2,1,0:T(4,128)S(1)} %get-tuple-element.10), channel_id=1, source_target_pairs={{8,0},{9,1},{10,2},{11,3},{12,4},{13,5},{14,6},{15,7},{16,8},{17,9... | collective-permute-start | bytes 143624 | tf_op jit(solution)/shard_map/ppermute | solution.py:25
  26.0 5.2 %collective-permute-done.3 = f32[22,4,136]{2,1,0:T(4,128)S(1)} collective-permute-done((f32[22,4,136]{2,1,0:T(4,128)S(1)}, f32[22,4,136]{2,1,0:T(4,128)S(1)}, u32[]{:S(2)}, u32[]{:S(2)}) %collective-permute-start.3) | collective-permute-done | bytes 47904 | tf_op jit(solution)/shard_map/ppermute | solution.py:25
  31.2 3.4 %pad_maximum_fusion.1 = f32[22,136,136]{2,1,0:T(8,128)S(1)} fusion(f32[22,4,136]{2,1,0:T(4,128)S(1)} %collective-permute-done.3, f32[22,128,4]{2,1,0:T(8,128)} %copy.37, f32[1,128,128]{2,1,0:T(8,128)S(1)} %get-tuple-element.6, f32[1,128,128]{2,1,0:T(8,128)S(1)} %copy-done.9, f32[10,128,128]{2,1,0:T(8,128)} %bitcast.53, f32[10,128,128]{2,1,0:T(8,128)} %bitcast.63, ...), kind=kLoop, calls=%fused_computation.1 | loop fusion | flops 2848384 | bytes 3255296 | tf_op jit(solution)/shard_map/concatenate | solution.py:34
  35.1 1.9 fusion.27
  37.1 1.9 fusion.23
  39.0 1.9 fusion.19
  42.5 2.3 %fusion.53 = f32[256,10,2,128]{3,0,2,1:T(8,128)S(1)} fusion(f32[256,64,1,1]{0,1,3,2:T(8,128)S(1)} %convolution_bitcast_fusion, f32[10,64,2,128]{3,2,1,0:T(2,128)S(1)} %bitcast.56), kind=kOutput, calls=%fused_computation.112 | convolution fusion | flops 503316480 | bytes 3342336 | tf_op jit(solution)/shard_map/jk,lkrc->jlrc/dot_general | solution.py:64
  44.8 2.0 copy.39
  48.1 2.0 copy.42
  50.5 131.8 %all_to_all.5 = f32[128,80,128]{2,1,0:T(8,128)S(1)} all-to-all(f32[128,80,128]{2,1,0:T(8,128)S(1)} %pad_maximum_fusion), channel_id=1, replica_groups=mesh['sec'=2,'gx'=16,'gy'=8] {'gx','gy'}, dimensions={0} | all-to-all | bytes 10485760 | tf_op jit(solution)/shard_map/all_to_all | solution.py:98
  184.1 2.1 fusion.28
  189.0 1.9 copy.47
  190.9 2.6 %collective-permute-start.7 = (f32[10,128,4]{1,2,0:T(4,128)}, f32[10,128,4]{1,2,0:T(4,128)}, u32[]{:S(2)}, u32[]{:S(2)}) collective-permute-start(f32[10,128,4]{1,2,0:T(4,128)} %copy.47), channel_id=1, source_target_pairs={{0,1},{1,2},{2,3},{3,4},{4,5},{5,6},{6,7},{8,9},{9,10},{10,11},{11... | collective-permute-start | bytes 61448 | tf_op jit(solution)/shard_map/ppermute | solution.py:25
  193.5 1.9 copy.48
  195.4 3.8 %collective-permute-start.8 = (f32[10,128,4]{1,2,0:T(4,128)}, f32[10,128,4]{1,2,0:T(4,128)}, u32[]{:S(2)}, u32[]{:S(2)}) collective-permute-start(f32[10,128,4]{1,2,0:T(4,128)} %copy.48), channel_id=1, source_target_pairs={{1,0},{2,1},{3,2},{4,3},{5,4},{6,5},{7,6},{9,8},{10,9},{11,10},{12... | collective-permute-start | bytes 61448 | tf_op jit(solution)/shard_map/ppermute | solution.py:25
  199.3 1.8 copy.49
  201.4 1.8 copy.50
  204.4 4.9 %collective-permute-start.9 = (f32[10,4,136]{2,1,0:T(4,128)S(1)}, f32[10,4,136]{2,1,0:T(4,128)S(1)}, u32[]{:S(2)}, u32[]{:S(2)}) collective-permute-start(f32[10,4,136]{2,1,0:T(4,128)S(1)} %get-tuple-element.17), channel_id=1, source_target_pairs={{0,8},{1,9},{2,10},{3,11},{4,12},{5,13},{6,14},{7,15},{8,16},{9,17... | collective-permute-start | bytes 65288 | tf_op jit(solution)/shard_map/ppermute | solution.py:25
  209.4 2.1 collective-permute-start.10
  211.5 6.1 %collective-permute-done.10 = f32[10,4,136]{2,1,0:T(4,128)S(1)} collective-permute-done((f32[10,4,136]{2,1,0:T(4,128)S(1)}, f32[10,4,136]{2,1,0:T(4,128)S(1)}, u32[]{:S(2)}, u32[]{:S(2)}) %collective-permute-start.10) | collective-permute-done | bytes 21792 | tf_op jit(solution)/shard_map/ppermute | solution.py:25
  218.2 1.9 fusion.15
  220.1 1.9 fusion.11
  222.0 1.9 fusion.7
  224.0 1.6 fusion.36
  (76 shorter events, 14.4 us)
Async XLA Ops:
  6.4 6.4 %collective-permute-start = (f32[22,128,4]{1,2,0:T(4,128)S(1)}, f32[22,128,4]{1,2,0:T(4,128)S(1)}, u32[]{:S(2)}, u32[]{:S(2)}) collective-permute-start(f32[22,128,4]{1,2,0:T(4,128)S(1)} %copy.34), channel_id=1, source_target_pairs={{0,1},{1,2},{2,3},{3,4},{4,5},{5,6},{6,7},{8,9},{9,10},{10,11},{11... | collective-permute-start | bytes 135176 | tf_op jit(solution)/shard_map/ppermute | solution.py:25
  10.7 7.7 %copy-start.2 = (f32[1,10,128,128]{3,2,1,0:T(8,128)S(1)}, f32[1,10,128,128]{3,2,1,0:T(8,128)}, u32[]{:S(2)}) copy-start(f32[1,10,128,128]{3,2,1,0:T(8,128)} %param.8) | copy-start | bytes 1966084
  10.7 7.7 %copy-start.8 = (f32[1,10,128,128]{3,2,1,0:T(8,128)S(1)}, f32[1,10,128,128]{3,2,1,0:T(8,128)}, u32[]{:S(2)}) copy-start(f32[1,10,128,128]{3,2,1,0:T(8,128)} %param.7) | copy-start | bytes 1966084
  10.7 7.7 %copy-start.9 = (f32[1,128,128]{2,1,0:T(8,128)S(1)}, f32[1,128,128]{2,1,0:T(8,128)}, u32[]{:S(2)}) copy-start(f32[1,128,128]{2,1,0:T(8,128)} %param.9) | copy-start | bytes 196612
  10.7 6.1 %collective-permute-start.1 = (f32[22,128,4]{1,2,0:T(4,128)S(1)}, f32[22,128,4]{1,2,0:T(4,128)S(1)}, u32[]{:S(2)}, u32[]{:S(2)}) collective-permute-start(f32[22,128,4]{1,2,0:T(4,128)S(1)} %copy.35), channel_id=1, source_target_pairs={{1,0},{2,1},{3,2},{4,3},{5,4},{6,5},{7,6},{9,8},{10,9},{11,10},{12... | collective-permute-start | bytes 135176 | tf_op jit(solution)/shard_map/ppermute | solution.py:25
  13.3 6.2 %copy-start.5 = (f32[22,128,4]{2,1,0:T(8,128)}, f32[22,128,4]{2,1,0:T(8,128)S(1)}, u32[]{:S(2)}) copy-start(f32[22,128,4]{2,1,0:T(8,128)S(1)} %copy.36) | copy-start | bytes 135172
  18.4 7.0 %copy-start.18 = (s32[1,1,128,2]{2,3,1,0:T(2,128)S(1)}, s32[1,1,128,2]{2,3,1,0:T(2,128)}, u32[]{:S(2)}) copy-start(s32[1,1,128,2]{2,3,1,0:T(2,128)} %param.13) | copy-start | bytes 3076
  19.6 6.4 %collective-permute-start.2 = (f32[22,4,136]{2,1,0:T(4,128)S(1)}, f32[22,4,136]{2,1,0:T(4,128)S(1)}, u32[]{:S(2)}, u32[]{:S(2)}) collective-permute-start(f32[22,4,136]{2,1,0:T(4,128)S(1)} %get-tuple-element.9), channel_id=1, source_target_pairs={{0,8},{1,9},{2,10},{3,11},{4,12},{5,13},{6,14},{7,15},{8,16},{9,17... | collective-permute-start | bytes 143624 | tf_op jit(solution)/shard_map/ppermute | solution.py:25
  22.7 8.5 %collective-permute-start.3 = (f32[22,4,136]{2,1,0:T(4,128)S(1)}, f32[22,4,136]{2,1,0:T(4,128)S(1)}, u32[]{:S(2)}, u32[]{:S(2)}) collective-permute-start(f32[22,4,136]{2,1,0:T(4,128)S(1)} %get-tuple-element.10), channel_id=1, source_target_pairs={{8,0},{9,1},{10,2},{11,3},{12,4},{13,5},{14,6},{15,7},{16,8},{17,9... | collective-permute-start | bytes 143624 | tf_op jit(solution)/shard_map/ppermute | solution.py:25
  25.7 21.1 %collective-permute-start.4 = (s32[256]{0:T(256)S(1)}, s32[256]{0:T(256)S(1)}, u32[]{:S(2)}, u32[]{:S(2)}) collective-permute-start(s32[256]{0:T(256)S(1)} %reshape_squeeze.3), channel_id=1, source_target_pairs={{0,128},{128,0},{1,129},{129,1},{2,130},{130,2},{3,131},{131,3},{4... | collective-permute-start | bytes 3080 | tf_op jit(solution)/shard_map/ppermute | solution.py:56
  34.8 2.2 copy-start.10
  35.1 1.9 copy-start.12
  35.1 1.9 copy-start.14
  39.0 1.9 copy-start.3
  39.0 1.9 copy-start.16
  40.9 1.1 copy-start.19
  40.9 1.3 copy-start.20
  41.8 5.1 %collective-permute-start.5 = (f32[10,64,2,128]{3,1,2,0:T(8,128)S(1)}, f32[10,64,2,128]{3,1,2,0:T(8,128)S(1)}, u32[]{:S(2)}, u32[]{:S(2)}) collective-permute-start(f32[10,64,2,128]{3,1,2,0:T(8,128)S(1)} %copy.44), channel_id=1, source_target_pairs={{0,128},{128,0},{1,129},{129,1},{2,130},{130,2},{3,131},{131,3},{4... | collective-permute-start | bytes 1966088 | tf_op jit(solution)/shard_map/ppermute | solution.py:56
  183.8 2.4 %collective-permute-start.6 = (f32[10,64,2,128]{3,1,2,0:T(8,128)S(1)}, f32[10,64,2,128]{3,1,2,0:T(8,128)S(1)}, u32[]{:S(2)}, u32[]{:S(2)}) collective-permute-start(f32[10,64,2,128]{3,1,2,0:T(8,128)S(1)} %fusion.29), channel_id=1, source_target_pairs={{0,128},{128,0},{1,129},{129,1},{2,130},{130,2},{3,131},{131,3},{4... | collective-permute-start | bytes 1966088 | tf_op jit(solution)/shard_map/ppermute | solution.py:56
  186.9 0.9 copy-start
  190.9 8.3 %collective-permute-start.7 = (f32[10,128,4]{1,2,0:T(4,128)}, f32[10,128,4]{1,2,0:T(4,128)}, u32[]{:S(2)}, u32[]{:S(2)}) collective-permute-start(f32[10,128,4]{1,2,0:T(4,128)} %copy.47), channel_id=1, source_target_pairs={{0,1},{1,2},{2,3},{3,4},{4,5},{5,6},{6,7},{8,9},{9,10},{10,11},{11... | collective-permute-start | bytes 61448 | tf_op jit(solution)/shard_map/ppermute | solution.py:25
  195.4 6.0 %collective-permute-start.8 = (f32[10,128,4]{1,2,0:T(4,128)}, f32[10,128,4]{1,2,0:T(4,128)}, u32[]{:S(2)}, u32[]{:S(2)}) collective-permute-start(f32[10,128,4]{1,2,0:T(4,128)} %copy.48), channel_id=1, source_target_pairs={{1,0},{2,1},{3,2},{4,3},{5,4},{6,5},{7,6},{9,8},{10,9},{11,10},{12... | collective-permute-start | bytes 61448 | tf_op jit(solution)/shard_map/ppermute | solution.py:25
  203.3 14.3 %copy-start.1 = (f32[10,64,2,128]{3,2,1,0:T(2,128)S(1)}, f32[10,64,2,128]{3,2,1,0:T(2,128)}, u32[]{:S(2)}) copy-start(f32[10,64,2,128]{3,2,1,0:T(2,128)} %copy-done) | copy-start | bytes 1966084
  203.3 14.3 %copy-start.6 = (f32[10,128,4]{2,1,0:T(8,128)S(1)}, f32[10,128,4]{2,1,0:T(8,128)}, u32[]{:S(2)}) copy-start(f32[10,128,4]{2,1,0:T(8,128)} %copy.49) | copy-start | bytes 61444
  203.3 14.3 %copy-start.7 = (f32[10,128,4]{2,1,0:T(8,128)S(1)}, f32[10,128,4]{2,1,0:T(8,128)}, u32[]{:S(2)}) copy-start(f32[10,128,4]{2,1,0:T(8,128)} %copy.50) | copy-start | bytes 61444
  204.4 7.0 %collective-permute-start.9 = (f32[10,4,136]{2,1,0:T(4,128)S(1)}, f32[10,4,136]{2,1,0:T(4,128)S(1)}, u32[]{:S(2)}, u32[]{:S(2)}) collective-permute-start(f32[10,4,136]{2,1,0:T(4,128)S(1)} %get-tuple-element.17), channel_id=1, source_target_pairs={{0,8},{1,9},{2,10},{3,11},{4,12},{5,13},{6,14},{7,15},{8,16},{9,17... | collective-permute-start | bytes 65288 | tf_op jit(solution)/shard_map/ppermute | solution.py:25
  209.4 8.8 %copy-start.13 = (f32[134,134]{1,0:T(8,128)S(1)}, f32[134,134]{1,0:T(8,128)}, u32[]{:S(2)}) copy-start(f32[134,134]{1,0:T(8,128)} %copy-done.12) | copy-start | bytes 215476
  209.4 8.8 %copy-start.15 = (f32[134,134]{1,0:T(8,128)S(1)}, f32[134,134]{1,0:T(8,128)}, u32[]{:S(2)}) copy-start(f32[134,134]{1,0:T(8,128)} %copy-done.14) | copy-start | bytes 215476
  209.4 8.1 %collective-permute-start.10 = (f32[10,4,136]{2,1,0:T(4,128)S(1)}, f32[10,4,136]{2,1,0:T(4,128)S(1)}, u32[]{:S(2)}, u32[]{:S(2)}) collective-permute-start(f32[10,4,136]{2,1,0:T(4,128)S(1)} %get-tuple-element.18), channel_id=1, source_target_pairs={{8,0},{9,1},{10,2},{11,3},{12,4},{13,5},{14,6},{15,7},{16,8},{17,9... | collective-permute-start | bytes 65288 | tf_op jit(solution)/shard_map/ppermute | solution.py:25
  218.2 1.9 copy-start.11
  222.0 1.9 copy-start.4
  222.0 1.9 copy-start.17

commit v10 on v8

--- a/solution.py
+++ b/solution.py
@@ -25,9 +25,19 @@
     return lax.ppermute(block, ("gx", "gy"), pairs)
 
 
+def columns(cells, start, w):
+    sel = onehot(start + jnp.arange(w, dtype=jnp.int32), cells.shape[2])
+    return jnp.einsum("jc,lrc->ljr", sel, cells, precision=HIGHEST)
+
+
+def uncolumns(strips):
+    return jnp.einsum("ljr,jm->lrm", strips, jnp.eye(strips.shape[1], dtype=strips.dtype), precision=HIGHEST)
+
+
 def halo(cells, w):
-    west = shifted(cells[:, :, -w:], 0, -1)
-    east = shifted(cells[:, :, :w], 0, 1)
+    cols = cells.shape[2]
+    west = uncolumns(shifted(columns(cells, cols - w, w), 0, -1))
+    east = uncolumns(shifted(columns(cells, 0, w), 0, 1))
     wide = jnp.concatenate([west, cells, east], axis=2)
     north = shifted(wide[:, -w:], -1, 0)
     south = shifted(wide[:, :w], 1, 0)

time: 219 us -> 209 us (0.954)
  local copies, waits for them, and re-layouts: 19 us -> 6.49 us
  matrix products: 6.99 us -> 14.7 us
  other arithmetic: 17.4 us -> 14.3 us
  waiting for transfers between devices: 15.7 us -> 12.8 us
    slice x6 -> x0, local copies, waits for them, and re-layouts: 7.73 us -> none  [the longest x4 5.98 us: halo(): west = shifted(cells[:, :, -w:], 0, -1)]
    dot_general x0 -> x8, matrix products: none -> 7.68 us  [the longest x4 4.02 us: uncolumns(): jnp.einsum('ljr,jm->lrm', strips, jnp.eye(strips.shape[1], dtype=strips.d...]
    ppermute x4 -> x0, local copies, waits for them, and re-layouts: 4.3 us -> none  [shifted(): return lax.ppermute(block, ('gx', 'gy'), pairs)]
    ppermute x8, waiting for transfers between devices: 15.7 us -> 12.8 us  [shifted(): return lax.ppermute(block, ('gx', 'gy'), pairs)]
  transfers between devices with their start and end apart: 11 -> 11, of which waited for: 5 -> 4; matrix products, arithmetic and copies ran while one was open for 8% -> 9% of each run, Pallas kernels for 0% -> 0%
where the time goes in v10:
time: 209 us; the launch traced here: 207 us
  blocking collectives  133 us (64%)
  starting transfers between devices  24.7 us (12%)
  matrix products  14.7 us (7%)
  other arithmetic  14.3 us (7%)
  waiting for transfers between devices  12.8 us (6%)
  local copies, waits for them, and re-layouts  6.49 us (3%)
    all_to_all x1, blocking collectives, couple(): incoming = lax.all_to_all(outgoing, ('gx', 'gy'), 0, 0, tiled=True)  133 us
    ppermute x8, starting transfers between devices, shifted(): return lax.ppermute(block, ('gx', 'gy'), pairs)  24.1 us
    ppermute x8, waiting for transfers between devices, shifted(): return lax.ppermute(block, ('gx', 'gy'), pairs)  12.8 us
    add x6, other arithmetic, relax(): return (1.0 - OMEGA) * field + OMEGA * invd * (force + visc * beside)  4.88 us
  transfers between devices with their start and end apart: 11, of which 4 were waited for; matrix products, arithmetic and copies ran while one was open for 9% of the time, Pallas kernels for 0%

profile of v10, /device:TPU:54, one launch (start us, length us, event | category | flops | bytes accessed | tf_op | source)
XLA Modules:
  0.0 206.6 jit_solution(16105805331434760088)
XLA Ops:
  0.0 1.6 multiply_bitcast_fusion
  1.6 2.1 %convolution_bitcast_fusion.1 = f32[22,4,128]{2,1,0:T(4,128)S(1)} fusion(f32[1,128,128]{2,1,0:T(8,128)S(1)} %get-tuple-element.14, f32[1,128,128]{2,1,0:T(8,128)} %param.9, f32[10,128,128]{2,1,0:T(8,128)} %bitcast.80, f32[10,128,128]{2,1,0:T(8,128)} %bitcast.84), kind=kOutput, calls=%fused_computation.25 | convolution fusion | flops 18383360 | bytes 1486848 | tf_op jit(solution)/shard_map/jc,lrc->ljr/dot_general | solution.py:30
  3.7 2.0 collective-permute-start.1
  6.6 3.8 %collective-permute-start = (f32[22,4,128]{2,1,0:T(4,128)S(1)}, f32[22,4,128]{2,1,0:T(4,128)S(1)}, u32[]{:S(2)}, u32[]{:S(2)}) collective-permute-start(f32[22,4,128]{2,1,0:T(4,128)S(1)} %convolution_bitcast_fusion.2), channel_id=1, source_target_pairs={{0,1},{1,2},{2,3},{3,4},{4,5},{5,6},{6,7},{8,9},{9,10},{10,11},{11... | collective-permute-start | bytes 135176 | tf_op jit(solution)/shard_map/ppermute | solution.py:25
  10.4 1.3 fusion.33
  12.5 1.3 fusion.35
  13.8 0.9 pad_maximum_fusion.11
  14.7 3.1 %collective-permute-start.2 = (f32[22,4,136]{2,1,0:T(4,128)}, f32[22,4,136]{2,1,0:T(4,128)}, u32[]{:S(2)}, u32[]{:S(2)}) collective-permute-start(f32[22,4,136]{2,1,0:T(4,128)} %get-tuple-element.7), channel_id=1, source_target_pairs={{0,8},{1,9},{2,10},{3,11},{4,12},{5,13},{6,14},{7,15},{8,16},{9,17... | collective-permute-start | bytes 143624 | tf_op jit(solution)/shard_map/ppermute | solution.py:25
  17.8 2.7 %collective-permute-start.3 = (f32[22,4,136]{2,1,0:T(4,128)}, f32[22,4,136]{2,1,0:T(4,128)}, u32[]{:S(2)}, u32[]{:S(2)}) collective-permute-start(f32[22,4,136]{2,1,0:T(4,128)} %get-tuple-element.8), channel_id=1, source_target_pairs={{8,0},{9,1},{10,2},{11,3},{12,4},{13,5},{14,6},{15,7},{16,8},{17,9... | collective-permute-start | bytes 143624 | tf_op jit(solution)/shard_map/ppermute | solution.py:25
  21.3 1.0 reshape_squeeze.3
  22.4 4.3 %collective-permute-done.3 = f32[22,4,136]{2,1,0:T(4,128)} collective-permute-done((f32[22,4,136]{2,1,0:T(4,128)}, f32[22,4,136]{2,1,0:T(4,128)}, u32[]{:S(2)}, u32[]{:S(2)}) %collective-permute-start.3) | collective-permute-done | bytes 47904 | tf_op jit(solution)/shard_map/ppermute | solution.py:25
  26.6 2.5 %pad_maximum_fusion.1 = f32[22,136,136]{2,1,0:T(8,128)S(1)} fusion(f32[22,4,136]{2,1,0:T(4,128)} %collective-permute-done.3, f32[22,128,4]{2,1,0:T(8,128)S(1)} %fusion.33, f32[1,128,128]{2,1,0:T(8,128)} %copy-done.5, f32[1,128,128]{2,1,0:T(8,128)} %param.9, f32[10,128,128]{2,1,0:T(8,128)S(1)} %bitcast.83, f32[10,128,128]{2,1,0:T(8,128)} %bitcast.85, ...), kind=kLoop, calls=%fused_computation.1 | loop fusion | flops 2848384 | bytes 3255296 | tf_op jit(solution)/shard_map/concatenate | solution.py:44
  30.1 0.8 multiply_add_fusion.4
  30.9 0.8 multiply_add_fusion.3
  31.8 0.9 fusion.16
  33.5 2.3 %fusion.46 = f32[256,10,2,128]{3,0,2,1:T(8,128)S(1)} fusion(f32[256,64,1,1]{0,1,3,2:T(8,128)S(1)} %convolution_bitcast_fusion, f32[10,64,2,128]{3,2,1,0:T(2,128)S(1)} %bitcast.74), kind=kOutput, calls=%fused_computation.89 | convolution fusion | flops 503316480 | bytes 3342336 | tf_op jit(solution)/shard_map/jk,lkrc->jlrc/dot_general | solution.py:72
  35.8 2.0 copy.28
  37.9 1.2 fusion.22
  39.1 2.0 copy.31
  41.6 133.1 %all_to_all.5 = f32[128,80,128]{2,1,0:T(8,128)S(1)} all-to-all(f32[128,80,128]{2,1,0:T(8,128)S(1)} %pad_maximum_fusion), channel_id=1, replica_groups=mesh['sec'=2,'gx'=16,'gy'=8] {'gx','gy'}, dimensions={0} | all-to-all | bytes 10485760 | tf_op jit(solution)/shard_map/all_to_all | solution.py:106
  175.0 1.2 fusion.5
  176.5 2.1 fusion.4
  179.7 2.6 %collective-permute-start.7 = (f32[10,4,128]{2,1,0:T(4,128)S(1)}, f32[10,4,128]{2,1,0:T(4,128)S(1)}, u32[]{:S(2)}, u32[]{:S(2)}) collective-permute-start(f32[10,4,128]{2,1,0:T(4,128)S(1)} %convolution_bitcast_fusion.4), channel_id=1, source_target_pairs={{0,1},{1,2},{2,3},{3,4},{4,5},{5,6},{6,7},{8,9},{9,10},{10,11},{11... | collective-permute-start | bytes 61448 | tf_op jit(solution)/shard_map/ppermute | solution.py:25
  182.7 3.3 %collective-permute-start.8 = (f32[10,4,128]{2,1,0:T(4,128)S(1)}, f32[10,4,128]{2,1,0:T(4,128)S(1)}, u32[]{:S(2)}, u32[]{:S(2)}) collective-permute-start(f32[10,4,128]{2,1,0:T(4,128)S(1)} %convolution_bitcast_fusion.3), channel_id=1, source_target_pairs={{1,0},{2,1},{3,2},{4,3},{5,4},{6,5},{7,6},{9,8},{10,9},{11,10},{12... | collective-permute-start | bytes 61448 | tf_op jit(solution)/shard_map/ppermute | solution.py:25
  186.7 1.7 collective-permute-done.8
  189.2 4.6 %collective-permute-start.9 = (f32[10,4,136]{2,1,0:T(4,128)S(1)}, f32[10,4,136]{2,1,0:T(4,128)S(1)}, u32[]{:S(2)}, u32[]{:S(2)}) collective-permute-start(f32[10,4,136]{2,1,0:T(4,128)S(1)} %get-tuple-element.11), channel_id=1, source_target_pairs={{0,8},{1,9},{2,10},{3,11},{4,12},{5,13},{6,14},{7,15},{8,16},{9,17... | collective-permute-start | bytes 65288 | tf_op jit(solution)/shard_map/ppermute | solution.py:25
  193.8 1.9 collective-permute-start.10
  195.7 6.1 %collective-permute-done.10 = f32[10,4,136]{2,1,0:T(4,128)S(1)} collective-permute-done((f32[10,4,136]{2,1,0:T(4,128)S(1)}, f32[10,4,136]{2,1,0:T(4,128)S(1)}, u32[]{:S(2)}, u32[]{:S(2)}) %collective-permute-start.10) | collective-permute-done | bytes 21792 | tf_op jit(solution)/shard_map/ppermute | solution.py:25
  202.4 0.8 multiply_add_fusion.2
  203.2 0.8 multiply_add_fusion.1
  204.1 0.8 multiply_add_fusion
  204.9 1.8 fusion.12
  (49 shorter events, 8.9 us)
Async XLA Ops:
  0.0 5.8 %copy-start.2 = (f32[1,128,128]{2,1,0:T(8,128)S(1)}, f32[1,128,128]{2,1,0:T(8,128)}, u32[]{:S(2)}) copy-start(f32[1,128,128]{2,1,0:T(8,128)} %param.9) | copy-start | bytes 196612
  0.0 5.8 %copy-start = (f32[1,10,128,128]{3,2,1,0:T(8,128)S(1)}, f32[1,10,128,128]{3,2,1,0:T(8,128)}, u32[]{:S(2)}) copy-start(f32[1,10,128,128]{3,2,1,0:T(8,128)} %param.8) | copy-start | bytes 1966084
  0.0 5.8 %copy-start.1 = (f32[1,10,128,128]{3,2,1,0:T(8,128)S(1)}, f32[1,10,128,128]{3,2,1,0:T(8,128)}, u32[]{:S(2)}) copy-start(f32[1,10,128,128]{3,2,1,0:T(8,128)} %param.7) | copy-start | bytes 1966084
  1.6 13.1 %copy-start.5 = (f32[1,128,128]{2,1,0:T(8,128)}, f32[1,128,128]{2,1,0:T(8,128)S(1)}, u32[]{:S(2)}) copy-start(f32[1,128,128]{2,1,0:T(8,128)S(1)} %get-tuple-element.14) | copy-start | bytes 196612
  3.7 6.7 %collective-permute-start.1 = (f32[22,4,128]{2,1,0:T(4,128)S(1)}, f32[22,4,128]{2,1,0:T(4,128)S(1)}, u32[]{:S(2)}, u32[]{:S(2)}) collective-permute-start(f32[22,4,128]{2,1,0:T(4,128)S(1)} %convolution_bitcast_fusion.1), channel_id=1, source_target_pairs={{1,0},{2,1},{3,2},{4,3},{5,4},{6,5},{7,6},{9,8},{10,9},{11,10},{12... | collective-permute-start | bytes 135176 | tf_op jit(solution)/shard_map/ppermute | solution.py:25
  6.6 5.9 %collective-permute-start = (f32[22,4,128]{2,1,0:T(4,128)S(1)}, f32[22,4,128]{2,1,0:T(4,128)S(1)}, u32[]{:S(2)}, u32[]{:S(2)}) collective-permute-start(f32[22,4,128]{2,1,0:T(4,128)S(1)} %convolution_bitcast_fusion.2), channel_id=1, source_target_pairs={{0,1},{1,2},{2,3},{3,4},{4,5},{5,6},{6,7},{8,9},{9,10},{10,11},{11... | collective-permute-start | bytes 135176 | tf_op jit(solution)/shard_map/ppermute | solution.py:25
  13.8 6.7 %copy-start.6 = (s32[1,1,128,2]{2,3,1,0:T(2,128)S(1)}, s32[1,1,128,2]{2,3,1,0:T(2,128)}, u32[]{:S(2)}) copy-start(s32[1,1,128,2]{2,3,1,0:T(2,128)} %param.13) | copy-start | bytes 3076
  14.7 7.7 %collective-permute-start.2 = (f32[22,4,136]{2,1,0:T(4,128)}, f32[22,4,136]{2,1,0:T(4,128)}, u32[]{:S(2)}, u32[]{:S(2)}) collective-permute-start(f32[22,4,136]{2,1,0:T(4,128)} %get-tuple-element.7), channel_id=1, source_target_pairs={{0,8},{1,9},{2,10},{3,11},{4,12},{5,13},{6,14},{7,15},{8,16},{9,17... | collective-permute-start | bytes 143624 | tf_op jit(solution)/shard_map/ppermute | solution.py:25
  17.8 8.8 %collective-permute-start.3 = (f32[22,4,136]{2,1,0:T(4,128)}, f32[22,4,136]{2,1,0:T(4,128)}, u32[]{:S(2)}, u32[]{:S(2)}) collective-permute-start(f32[22,4,136]{2,1,0:T(4,128)} %get-tuple-element.8), channel_id=1, source_target_pairs={{8,0},{9,1},{10,2},{11,3},{12,4},{13,5},{14,6},{15,7},{16,8},{17,9... | collective-permute-start | bytes 143624 | tf_op jit(solution)/shard_map/ppermute | solution.py:25
  22.3 15.6 %collective-permute-start.4 = (s32[256]{0:T(256)S(1)}, s32[256]{0:T(256)S(1)}, u32[]{:S(2)}, u32[]{:S(2)}) collective-permute-start(s32[256]{0:T(256)S(1)} %reshape_squeeze.3), channel_id=1, source_target_pairs={{0,128},{128,0},{1,129},{129,1},{2,130},{130,2},{3,131},{131,3},{4... | collective-permute-start | bytes 3080 | tf_op jit(solution)/shard_map/ppermute | solution.py:64
  30.9 0.8 copy-start.3
  30.9 0.9 copy-start.4
  31.8 1.3 copy-start.7
  31.8 1.5 copy-start.8
  32.8 5.1 %collective-permute-start.5 = (f32[10,64,2,128]{3,1,2,0:T(8,128)S(1)}, f32[10,64,2,128]{3,1,2,0:T(8,128)S(1)}, u32[]{:S(2)}, u32[]{:S(2)}) collective-permute-start(f32[10,64,2,128]{3,1,2,0:T(8,128)S(1)} %copy.33), channel_id=1, source_target_pairs={{0,128},{128,0},{1,129},{129,1},{2,130},{130,2},{3,131},{131,3},{4... | collective-permute-start | bytes 1966088 | tf_op jit(solution)/shard_map/ppermute | solution.py:64
  176.2 2.4 %collective-permute-start.6 = (f32[10,64,2,128]{3,1,2,0:T(8,128)S(1)}, f32[10,64,2,128]{3,1,2,0:T(8,128)S(1)}, u32[]{:S(2)}, u32[]{:S(2)}) collective-permute-start(f32[10,64,2,128]{3,1,2,0:T(8,128)S(1)} %fusion.5), channel_id=1, source_target_pairs={{0,128},{128,0},{1,129},{129,1},{2,130},{130,2},{3,131},{131,3},{4... | collective-permute-start | bytes 1966088 | tf_op jit(solution)/shard_map/ppermute | solution.py:64
  179.7 6.3 %collective-permute-start.7 = (f32[10,4,128]{2,1,0:T(4,128)S(1)}, f32[10,4,128]{2,1,0:T(4,128)S(1)}, u32[]{:S(2)}, u32[]{:S(2)}) collective-permute-start(f32[10,4,128]{2,1,0:T(4,128)S(1)} %convolution_bitcast_fusion.4), channel_id=1, source_target_pairs={{0,1},{1,2},{2,3},{3,4},{4,5},{5,6},{6,7},{8,9},{9,10},{10,11},{11... | collective-permute-start | bytes 61448 | tf_op jit(solution)/shard_map/ppermute | solution.py:25
  182.7 5.7 %collective-permute-start.8 = (f32[10,4,128]{2,1,0:T(4,128)S(1)}, f32[10,4,128]{2,1,0:T(4,128)S(1)}, u32[]{:S(2)}, u32[]{:S(2)}) collective-permute-start(f32[10,4,128]{2,1,0:T(4,128)S(1)} %convolution_bitcast_fusion.3), channel_id=1, source_target_pairs={{1,0},{2,1},{3,2},{4,3},{5,4},{6,5},{7,6},{9,8},{10,9},{11,10},{12... | collective-permute-start | bytes 61448 | tf_op jit(solution)/shard_map/ppermute | solution.py:25
  189.2 6.5 %collective-permute-start.9 = (f32[10,4,136]{2,1,0:T(4,128)S(1)}, f32[10,4,136]{2,1,0:T(4,128)S(1)}, u32[]{:S(2)}, u32[]{:S(2)}) collective-permute-start(f32[10,4,136]{2,1,0:T(4,128)S(1)} %get-tuple-element.11), channel_id=1, source_target_pairs={{0,8},{1,9},{2,10},{3,11},{4,12},{5,13},{6,14},{7,15},{8,16},{9,17... | collective-permute-start | bytes 65288 | tf_op jit(solution)/shard_map/ppermute | solution.py:25
  193.8 8.0 %collective-permute-start.10 = (f32[10,4,136]{2,1,0:T(4,128)S(1)}, f32[10,4,136]{2,1,0:T(4,128)S(1)}, u32[]{:S(2)}, u32[]{:S(2)}) collective-permute-start(f32[10,4,136]{2,1,0:T(4,128)S(1)} %get-tuple-element.12), channel_id=1, source_target_pairs={{8,0},{9,1},{10,2},{11,3},{12,4},{13,5},{14,6},{15,7},{16,8},{17,9... | collective-permute-start | bytes 65288 | tf_op jit(solution)/shard_map/ppermute | solution.py:25

commit v11 on v10

--- a/solution.py
+++ b/solution.py
@@ -34,10 +34,12 @@
     return jnp.einsum("ljr,jm->lrm", strips, jnp.eye(strips.shape[1], dtype=strips.dtype), precision=HIGHEST)
 
 
-def halo(cells, w):
+def halo(cells, w, right=None, left=None):
     cols = cells.shape[2]
-    west = uncolumns(shifted(columns(cells, cols - w, w), 0, -1))
-    east = uncolumns(shifted(columns(cells, 0, w), 0, 1))
+    if right is None:
+        right, left = columns(cells, cols - w, w), columns(cells, 0, w)
+    west = uncolumns(shifted(right, 0, -1))
+    east = uncolumns(shifted(left, 0, 1))
     wide = jnp.concatenate([west, cells, east], axis=2)
     north = shifted(wide[:, -w:], -1, 0)
     south = shifted(wide[:, :w], 1, 0)
@@ -117,7 +119,10 @@
     levels, rows, cols = adjoint_state.shape[1:]
     invd = 1.0 / (4.0 * viscosity + reaction)
     stacked = jnp.concatenate([adjoint_state[0], forcing[0], viscosity, invd], axis=0)
-    ext = halo(stacked, w)
+    parts = [adjoint_state[0], forcing[0], viscosity, invd]
+    right = jnp.concatenate([columns(p, cols - w, w) for p in parts], axis=0)
+    left = jnp.concatenate([columns(p, 0, w) for p in parts], axis=0)
+    ext = halo(stacked, w, right, left)
     field = ext[:levels]
     force = ext[levels:2 * levels]
     visc = ext[2 * levels:2 * levels + 1]

time: 209 us -> 212 us (1.014)
  matrix products: 14.7 us -> 17.3 us
    dot_general x4 -> x10, matrix products: 3.66 us -> 6.3 us  [columns(): return jnp.einsum('jc,lrc->ljr', sel, cells, precision=HIGHEST)]
where the time goes in v11:
time: 212 us; the launch traced here: 209 us
  blocking collectives  133 us (63%)
  starting transfers between devices  24.7 us (12%)
  matrix products  17.3 us (8%)
  other arithmetic  14.4 us (7%)
  waiting for transfers between devices  12.8 us (6%)
  local copies, waits for them, and re-layouts  6.49 us (3%)
    all_to_all x1, blocking collectives, couple(): incoming = lax.all_to_all(outgoing, ('gx', 'gy'), 0, 0, tiled=True)  133 us
    ppermute x8, starting transfers between devices, shifted(): return lax.ppermute(block, ('gx', 'gy'), pairs)  24 us
    ppermute x8, waiting for transfers between devices, shifted(): return lax.ppermute(block, ('gx', 'gy'), pairs)  12.8 us
    dot_general x10, matrix products, columns(): return jnp.einsum('jc,lrc->ljr', sel, cells, precision=HIGHEST)  6.3 us
    add x6, other arithmetic, relax(): return (1.0 - OMEGA) * field + OMEGA * invd * (force + visc * beside)  4.88 us
  transfers between devices with their start and end apart: 11, of which 4 were waited for; matrix products, arithmetic and copies ran while one was open for 9% of the time, Pallas kernels for 0%

profile of v11, /device:TPU:54, one launch (start us, length us, event | category | flops | bytes accessed | tf_op | source)
XLA Modules:
  0.0 209.3 jit_solution(14090733208482868506)
XLA Ops:
  0.0 1.1 convolution_bitcast_fusion.8
  1.1 1.5 convolution_bitcast_fusion.4
  2.6 1.5 convolution_bitcast_fusion.3
  4.1 1.5 multiply_bitcast_fusion
  5.8 2.0 collective-permute-start.1
  9.2 3.8 %collective-permute-start = (f32[22,4,128]{2,1,0:T(4,128)S(1)}, f32[22,4,128]{2,1,0:T(4,128)S(1)}, u32[]{:S(2)}, u32[]{:S(2)}) collective-permute-start(f32[22,4,128]{2,1,0:T(4,128)S(1)} %pad_maximum_fusion.9), channel_id=1, source_target_pairs={{0,1},{1,2},{2,3},{3,4},{4,5},{5,6},{6,7},{8,9},{9,10},{10,11},{11... | collective-permute-start | bytes 135176 | tf_op jit(solution)/shard_map/ppermute | solution.py:25
  13.0 1.3 fusion.39
  15.1 1.3 fusion.41
  16.5 0.9 pad_maximum_fusion.8
  17.3 3.1 %collective-permute-start.2 = (f32[22,4,136]{2,1,0:T(4,128)}, f32[22,4,136]{2,1,0:T(4,128)}, u32[]{:S(2)}, u32[]{:S(2)}) collective-permute-start(f32[22,4,136]{2,1,0:T(4,128)} %get-tuple-element.9), channel_id=1, source_target_pairs={{0,8},{1,9},{2,10},{3,11},{4,12},{5,13},{6,14},{7,15},{8,16},{9,17... | collective-permute-start | bytes 143624 | tf_op jit(solution)/shard_map/ppermute | solution.py:25
  20.4 2.7 %collective-permute-start.3 = (f32[22,4,136]{2,1,0:T(4,128)}, f32[22,4,136]{2,1,0:T(4,128)}, u32[]{:S(2)}, u32[]{:S(2)}) collective-permute-start(f32[22,4,136]{2,1,0:T(4,128)} %get-tuple-element.10), channel_id=1, source_target_pairs={{8,0},{9,1},{10,2},{11,3},{12,4},{13,5},{14,6},{15,7},{16,8},{17,9... | collective-permute-start | bytes 143624 | tf_op jit(solution)/shard_map/ppermute | solution.py:25
  23.9 1.0 reshape_squeeze.3
  25.0 4.3 %collective-permute-done.3 = f32[22,4,136]{2,1,0:T(4,128)} collective-permute-done((f32[22,4,136]{2,1,0:T(4,128)}, f32[22,4,136]{2,1,0:T(4,128)}, u32[]{:S(2)}, u32[]{:S(2)}) %collective-permute-start.3) | collective-permute-done | bytes 47904 | tf_op jit(solution)/shard_map/ppermute | solution.py:25
  29.3 2.5 %pad_maximum_fusion.1 = f32[22,136,136]{2,1,0:T(8,128)S(1)} fusion(f32[22,4,136]{2,1,0:T(4,128)} %collective-permute-done.3, f32[22,128,4]{2,1,0:T(8,128)S(1)} %fusion.39, f32[1,128,128]{2,1,0:T(8,128)} %copy-done.4, f32[1,128,128]{2,1,0:T(8,128)} %param.9, f32[10,128,128]{2,1,0:T(8,128)S(1)} %bitcast.113, f32[10,128,128]{2,1,0:T(8,128)} %bitcast.125, ...), kind=kLoop, calls=%fused_computation.1 | loop fusion | flops 2848384 | bytes 3255296 | tf_op jit(solution)/shard_map/concatenate | solution.py:46
  31.9 0.8 multiply_add_fusion.5
  32.7 0.8 multiply_add_fusion.4
  33.6 0.8 multiply_add_fusion.3
  34.4 0.9 fusion.16
  36.2 2.3 %fusion.54 = f32[256,10,2,128]{3,0,2,1:T(8,128)S(1)} fusion(f32[256,64,1,1]{0,1,3,2:T(8,128)S(1)} %convolution_bitcast_fusion, f32[10,64,2,128]{3,2,1,0:T(2,128)S(1)} %bitcast.119), kind=kOutput, calls=%fused_computation.102 | convolution fusion | flops 503316480 | bytes 3342336 | tf_op jit(solution)/shard_map/jk,lkrc->jlrc/dot_general | solution.py:74
  38.4 2.0 copy.28
  40.5 1.2 fusion.24
  41.8 2.0 copy.31
  44.2 133.1 %all_to_all.5 = f32[128,80,128]{2,1,0:T(8,128)S(1)} all-to-all(f32[128,80,128]{2,1,0:T(8,128)S(1)} %pad_maximum_fusion), channel_id=1, replica_groups=mesh['sec'=2,'gx'=16,'gy'=8] {'gx','gy'}, dimensions={0} | all-to-all | bytes 10485760 | tf_op jit(solution)/shard_map/all_to_all | solution.py:108
  177.7 1.2 fusion.5
  179.1 2.1 fusion.4
  182.3 2.6 %collective-permute-start.7 = (f32[10,4,128]{2,1,0:T(4,128)S(1)}, f32[10,4,128]{2,1,0:T(4,128)S(1)}, u32[]{:S(2)}, u32[]{:S(2)}) collective-permute-start(f32[10,4,128]{2,1,0:T(4,128)S(1)} %convolution_bitcast_fusion.2), channel_id=1, source_target_pairs={{0,1},{1,2},{2,3},{3,4},{4,5},{5,6},{6,7},{8,9},{9,10},{10,11},{11... | collective-permute-start | bytes 61448 | tf_op jit(solution)/shard_map/ppermute | solution.py:25
  185.3 3.3 %collective-permute-start.8 = (f32[10,4,128]{2,1,0:T(4,128)S(1)}, f32[10,4,128]{2,1,0:T(4,128)S(1)}, u32[]{:S(2)}, u32[]{:S(2)}) collective-permute-start(f32[10,4,128]{2,1,0:T(4,128)S(1)} %convolution_bitcast_fusion.1), channel_id=1, source_target_pairs={{1,0},{2,1},{3,2},{4,3},{5,4},{6,5},{7,6},{9,8},{10,9},{11,10},{12... | collective-permute-start | bytes 61448 | tf_op jit(solution)/shard_map/ppermute | solution.py:25
  189.3 1.7 collective-permute-done.8
  191.9 4.6 %collective-permute-start.9 = (f32[10,4,136]{2,1,0:T(4,128)S(1)}, f32[10,4,136]{2,1,0:T(4,128)S(1)}, u32[]{:S(2)}, u32[]{:S(2)}) collective-permute-start(f32[10,4,136]{2,1,0:T(4,128)S(1)} %get-tuple-element.13), channel_id=1, source_target_pairs={{0,8},{1,9},{2,10},{3,11},{4,12},{5,13},{6,14},{7,15},{8,16},{9,17... | collective-permute-start | bytes 65288 | tf_op jit(solution)/shard_map/ppermute | solution.py:25
  196.5 1.9 collective-permute-start.10
  198.4 6.1 %collective-permute-done.10 = f32[10,4,136]{2,1,0:T(4,128)S(1)} collective-permute-done((f32[10,4,136]{2,1,0:T(4,128)S(1)}, f32[10,4,136]{2,1,0:T(4,128)S(1)}, u32[]{:S(2)}, u32[]{:S(2)}) %collective-permute-start.10) | collective-permute-done | bytes 21792 | tf_op jit(solution)/shard_map/ppermute | solution.py:25
  207.5 1.8 fusion.12
  (57 shorter events, 11.2 us)
Async XLA Ops:
  0.0 4.1 %copy-start.2 = (f32[1,128,128]{2,1,0:T(8,128)S(1)}, f32[1,128,128]{2,1,0:T(8,128)}, u32[]{:S(2)}) copy-start(f32[1,128,128]{2,1,0:T(8,128)} %param.9) | copy-start | bytes 196612
  0.0 8.5 %copy-start.1 = (f32[1,10,128,128]{3,2,1,0:T(8,128)S(1)}, f32[1,10,128,128]{3,2,1,0:T(8,128)}, u32[]{:S(2)}) copy-start(f32[1,10,128,128]{3,2,1,0:T(8,128)} %param.7) | copy-start | bytes 1966084
  0.0 8.0 %copy-start = (f32[1,10,128,128]{3,2,1,0:T(8,128)S(1)}, f32[1,10,128,128]{3,2,1,0:T(8,128)}, u32[]{:S(2)}) copy-start(f32[1,10,128,128]{3,2,1,0:T(8,128)} %param.8) | copy-start | bytes 1966084
  5.6 10.8 %copy-start.4 = (f32[1,128,128]{2,1,0:T(8,128)}, f32[1,128,128]{2,1,0:T(8,128)S(1)}, u32[]{:S(2)}) copy-start(f32[1,128,128]{2,1,0:T(8,128)S(1)} %get-tuple-element.6) | copy-start | bytes 196612
  5.8 7.2 %collective-permute-start.1 = (f32[22,4,128]{2,1,0:T(4,128)S(1)}, f32[22,4,128]{2,1,0:T(4,128)S(1)}, u32[]{:S(2)}, u32[]{:S(2)}) collective-permute-start(f32[22,4,128]{2,1,0:T(4,128)S(1)} %pad_maximum_fusion.10), channel_id=1, source_target_pairs={{1,0},{2,1},{3,2},{4,3},{5,4},{6,5},{7,6},{9,8},{10,9},{11,10},{12... | collective-permute-start | bytes 135176 | tf_op jit(solution)/shard_map/ppermute | solution.py:25
  9.2 5.9 %collective-permute-start = (f32[22,4,128]{2,1,0:T(4,128)S(1)}, f32[22,4,128]{2,1,0:T(4,128)S(1)}, u32[]{:S(2)}, u32[]{:S(2)}) collective-permute-start(f32[22,4,128]{2,1,0:T(4,128)S(1)} %pad_maximum_fusion.9), channel_id=1, source_target_pairs={{0,1},{1,2},{2,3},{3,4},{4,5},{5,6},{6,7},{8,9},{9,10},{10,11},{11... | collective-permute-start | bytes 135176 | tf_op jit(solution)/shard_map/ppermute | solution.py:25
  16.5 6.7 %copy-start.6 = (s32[1,1,128,2]{2,3,1,0:T(2,128)S(1)}, s32[1,1,128,2]{2,3,1,0:T(2,128)}, u32[]{:S(2)}) copy-start(s32[1,1,128,2]{2,3,1,0:T(2,128)} %param.13) | copy-start | bytes 3076
  17.3 7.7 %collective-permute-start.2 = (f32[22,4,136]{2,1,0:T(4,128)}, f32[22,4,136]{2,1,0:T(4,128)}, u32[]{:S(2)}, u32[]{:S(2)}) collective-permute-start(f32[22,4,136]{2,1,0:T(4,128)} %get-tuple-element.9), channel_id=1, source_target_pairs={{0,8},{1,9},{2,10},{3,11},{4,12},{5,13},{6,14},{7,15},{8,16},{9,17... | collective-permute-start | bytes 143624 | tf_op jit(solution)/shard_map/ppermute | solution.py:25
  20.4 8.8 %collective-permute-start.3 = (f32[22,4,136]{2,1,0:T(4,128)}, f32[22,4,136]{2,1,0:T(4,128)}, u32[]{:S(2)}, u32[]{:S(2)}) collective-permute-start(f32[22,4,136]{2,1,0:T(4,128)} %get-tuple-element.10), channel_id=1, source_target_pairs={{8,0},{9,1},{10,2},{11,3},{12,4},{13,5},{14,6},{15,7},{16,8},{17,9... | collective-permute-start | bytes 143624 | tf_op jit(solution)/shard_map/ppermute | solution.py:25
  24.9 15.6 %collective-permute-start.4 = (s32[256]{0:T(256)S(1)}, s32[256]{0:T(256)S(1)}, u32[]{:S(2)}, u32[]{:S(2)}) collective-permute-start(s32[256]{0:T(256)S(1)} %reshape_squeeze.3), channel_id=1, source_target_pairs={{0,128},{128,0},{1,129},{129,1},{2,130},{130,2},{3,131},{131,3},{4... | collective-permute-start | bytes 3080 | tf_op jit(solution)/shard_map/ppermute | solution.py:66
  33.5 0.8 copy-start.3
  33.6 0.9 copy-start.5
  34.4 1.3 copy-start.7
  34.4 1.5 copy-start.8
  35.4 5.1 %collective-permute-start.5 = (f32[10,64,2,128]{3,1,2,0:T(8,128)S(1)}, f32[10,64,2,128]{3,1,2,0:T(8,128)S(1)}, u32[]{:S(2)}, u32[]{:S(2)}) collective-permute-start(f32[10,64,2,128]{3,1,2,0:T(8,128)S(1)} %copy.33), channel_id=1, source_target_pairs={{0,128},{128,0},{1,129},{129,1},{2,130},{130,2},{3,131},{131,3},{4... | collective-permute-start | bytes 1966088 | tf_op jit(solution)/shard_map/ppermute | solution.py:66
  178.8 2.4 %collective-permute-start.6 = (f32[10,64,2,128]{3,1,2,0:T(8,128)S(1)}, f32[10,64,2,128]{3,1,2,0:T(8,128)S(1)}, u32[]{:S(2)}, u32[]{:S(2)}) collective-permute-start(f32[10,64,2,128]{3,1,2,0:T(8,128)S(1)} %fusion.5), channel_id=1, source_target_pairs={{0,128},{128,0},{1,129},{129,1},{2,130},{130,2},{3,131},{131,3},{4... | collective-permute-start | bytes 1966088 | tf_op jit(solution)/shard_map/ppermute | solution.py:66
  182.3 6.3 %collective-permute-start.7 = (f32[10,4,128]{2,1,0:T(4,128)S(1)}, f32[10,4,128]{2,1,0:T(4,128)S(1)}, u32[]{:S(2)}, u32[]{:S(2)}) collective-permute-start(f32[10,4,128]{2,1,0:T(4,128)S(1)} %convolution_bitcast_fusion.2), channel_id=1, source_target_pairs={{0,1},{1,2},{2,3},{3,4},{4,5},{5,6},{6,7},{8,9},{9,10},{10,11},{11... | collective-permute-start | bytes 61448 | tf_op jit(solution)/shard_map/ppermute | solution.py:25
  185.3 5.7 %collective-permute-start.8 = (f32[10,4,128]{2,1,0:T(4,128)S(1)}, f32[10,4,128]{2,1,0:T(4,128)S(1)}, u32[]{:S(2)}, u32[]{:S(2)}) collective-permute-start(f32[10,4,128]{2,1,0:T(4,128)S(1)} %convolution_bitcast_fusion.1), channel_id=1, source_target_pairs={{1,0},{2,1},{3,2},{4,3},{5,4},{6,5},{7,6},{9,8},{10,9},{11,10},{12... | collective-permute-start | bytes 61448 | tf_op jit(solution)/shard_map/ppermute | solution.py:25
  191.9 6.5 %collective-permute-start.9 = (f32[10,4,136]{2,1,0:T(4,128)S(1)}, f32[10,4,136]{2,1,0:T(4,128)S(1)}, u32[]{:S(2)}, u32[]{:S(2)}) collective-permute-start(f32[10,4,136]{2,1,0:T(4,128)S(1)} %get-tuple-element.13), channel_id=1, source_target_pairs={{0,8},{1,9},{2,10},{3,11},{4,12},{5,13},{6,14},{7,15},{8,16},{9,17... | collective-permute-start | bytes 65288 | tf_op jit(solution)/shard_map/ppermute | solution.py:25
  196.5 8.0 %collective-permute-start.10 = (f32[10,4,136]{2,1,0:T(4,128)S(1)}, f32[10,4,136]{2,1,0:T(4,128)S(1)}, u32[]{:S(2)}, u32[]{:S(2)}) collective-permute-start(f32[10,4,136]{2,1,0:T(4,128)S(1)} %get-tuple-element.14), channel_id=1, source_target_pairs={{8,0},{9,1},{10,2},{11,3},{12,4},{13,5},{14,6},{15,7},{16,8},{17,9... | collective-permute-start | bytes 65288 | tf_op jit(solution)/shard_map/ppermute | solution.py:25

commit v12 on v10

--- a/solution.py
+++ b/solution.py
@@ -36,8 +36,10 @@
 
 def halo(cells, w):
     cols = cells.shape[2]
-    west = uncolumns(shifted(columns(cells, cols - w, w), 0, -1))
-    east = uncolumns(shifted(columns(cells, 0, w), 0, 1))
+    index = jnp.concatenate([jnp.arange(cols - w, cols, dtype=jnp.int32), jnp.arange(w, dtype=jnp.int32)])
+    both = jnp.einsum("jc,lrc->ljr", onehot(index, cols), cells, precision=HIGHEST)
+    west = uncolumns(shifted(both[:, :w], 0, -1))
+    east = uncolumns(shifted(both[:, w:], 0, 1))
     wide = jnp.concatenate([west, cells, east], axis=2)
     north = shifted(wide[:, -w:], -1, 0)
     south = shifted(wide[:, :w], 1, 0)

time: 209 us -> 208 us (level)
  transfers between devices with their start and end apart: 11 -> 11, of which waited for: 4 -> 4; matrix products, arithmetic and copies ran while one was open for 9% -> 8% of each run, Pallas kernels for 0% -> 0%
where the time goes in v12:
time: 208 us; the launch traced here: 207 us
  blocking collectives  133 us (64%)
  starting transfers between devices  25.5 us (12%)
  other arithmetic  14.3 us (7%)
  waiting for transfers between devices  13.6 us (7%)
  matrix products  13.5 us (6%)
  local copies, waits for them, and re-layouts  6.56 us (3%)
    all_to_all x1, blocking collectives, couple(): incoming = lax.all_to_all(outgoing, ('gx', 'gy'), 0, 0, tiled=True)  133 us
    ppermute x8, starting transfers between devices, shifted(): return lax.ppermute(block, ('gx', 'gy'), pairs)  24.8 us
    ppermute x8, waiting for transfers between devices, shifted(): return lax.ppermute(block, ('gx', 'gy'), pairs)  13.6 us
    add x6, other arithmetic, relax(): return (1.0 - OMEGA) * field + OMEGA * invd * (force + visc * beside)  4.88 us
  transfers between devices with their start and end apart: 11, of which 4 were waited for; matrix products, arithmetic and copies ran while one was open for 8% of the time, Pallas kernels for 0%

profile of v12, /device:TPU:54, one launch (start us, length us, event | category | flops | bytes accessed | tf_op | source)
XLA Modules:
  0.0 207.1 jit_solution(14659480111931336436)
XLA Ops:
  0.1 1.5 multiply_bitcast_fusion
  1.6 2.1 %fusion.16 = f32[22,8,128]{2,1,0:T(8,128)S(1)} fusion(f32[1,128,128]{2,1,0:T(8,128)S(1)} %get-tuple-element.6, f32[1,128,128]{2,1,0:T(8,128)} %param.9, f32[10,128,128]{2,1,0:T(8,128)} %bitcast.67, f32[10,128,128]{2,1,0:T(8,128)} %bitcast.73, s32[8]{0:T(128)S(1)} %pad_add_fusion), kind=kOutput, calls=%fused_computation.31 | convolution fusion | flops 35685376 | bytes 1531936 | tf_op jit(solution)/shard_map/jc,lrc->ljr/dot_general | solution.py:40
  3.7 2.0 collective-permute-start.1
  5.8 4.0 %collective-permute-start = (f32[22,4,128]{2,1,0:T(4,128)S(1)}, f32[22,4,128]{2,1,0:T(4,128)S(1)}, u32[]{:S(2)}, u32[]{:S(2)}) collective-permute-start(f32[22,4,128]{2,1,0:T(4,128)S(1)} %get-tuple-element.15), channel_id=1, source_target_pairs={{0,1},{1,2},{2,3},{3,4},{4,5},{5,6},{6,7},{8,9},{9,10},{10,11},{11... | collective-permute-start | bytes 135176 | tf_op jit(solution)/shard_map/ppermute | solution.py:25
  9.8 1.3 fusion.48
  11.9 1.3 fusion.50
  13.2 0.9 pad_maximum_fusion.8
  14.1 3.1 %collective-permute-start.2 = (f32[22,4,136]{2,1,0:T(4,128)}, f32[22,4,136]{2,1,0:T(4,128)}, u32[]{:S(2)}, u32[]{:S(2)}) collective-permute-start(f32[22,4,136]{2,1,0:T(4,128)} %get-tuple-element.9), channel_id=1, source_target_pairs={{0,8},{1,9},{2,10},{3,11},{4,12},{5,13},{6,14},{7,15},{8,16},{9,17... | collective-permute-start | bytes 143624 | tf_op jit(solution)/shard_map/ppermute | solution.py:25
  17.2 2.7 %collective-permute-start.3 = (f32[22,4,136]{2,1,0:T(4,128)}, f32[22,4,136]{2,1,0:T(4,128)}, u32[]{:S(2)}, u32[]{:S(2)}) collective-permute-start(f32[22,4,136]{2,1,0:T(4,128)} %get-tuple-element.10), channel_id=1, source_target_pairs={{8,0},{9,1},{10,2},{11,3},{12,4},{13,5},{14,6},{15,7},{16,8},{17,9... | collective-permute-start | bytes 143624 | tf_op jit(solution)/shard_map/ppermute | solution.py:25
  20.7 1.0 reshape_squeeze.3
  21.8 4.3 %collective-permute-done.3 = f32[22,4,136]{2,1,0:T(4,128)} collective-permute-done((f32[22,4,136]{2,1,0:T(4,128)}, f32[22,4,136]{2,1,0:T(4,128)}, u32[]{:S(2)}, u32[]{:S(2)}) %collective-permute-start.3) | collective-permute-done | bytes 47904 | tf_op jit(solution)/shard_map/ppermute | solution.py:25
  26.1 2.5 %pad_maximum_fusion.1 = f32[22,136,136]{2,1,0:T(8,128)S(1)} fusion(f32[22,4,136]{2,1,0:T(4,128)} %collective-permute-done.3, f32[22,128,4]{2,1,0:T(8,128)S(1)} %fusion.48, f32[1,128,128]{2,1,0:T(8,128)} %copy-done.5, f32[1,128,128]{2,1,0:T(8,128)} %param.9, f32[10,128,128]{2,1,0:T(8,128)S(1)} %bitcast.69, f32[10,128,128]{2,1,0:T(8,128)} %bitcast.74, ...), kind=kLoop, calls=%fused_computation.1 | loop fusion | flops 2848384 | bytes 3255296 | tf_op jit(solution)/shard_map/concatenate | solution.py:46
  28.7 0.8 multiply_add_fusion.5
  29.5 0.8 multiply_add_fusion.4
  30.3 0.8 multiply_add_fusion.3
  31.2 0.9 fusion.27
  32.9 2.3 %fusion.53 = f32[256,10,2,128]{3,0,2,1:T(8,128)S(1)} fusion(f32[256,64,1,1]{0,1,3,2:T(8,128)S(1)} %convolution_bitcast_fusion, f32[10,64,2,128]{3,2,1,0:T(2,128)S(1)} %bitcast.61), kind=kOutput, calls=%fused_computation.92 | convolution fusion | flops 503316480 | bytes 3342336 | tf_op jit(solution)/shard_map/jk,lkrc->jlrc/dot_general | solution.py:74
  35.2 2.0 copy.32
  37.3 1.2 fusion.33
  38.5 2.0 copy.35
  41.0 133.1 %all_to_all.5 = f32[128,80,128]{2,1,0:T(8,128)S(1)} all-to-all(f32[128,80,128]{2,1,0:T(8,128)S(1)} %pad_maximum_fusion), channel_id=1, replica_groups=mesh['sec'=2,'gx'=16,'gy'=8] {'gx','gy'}, dimensions={0} | all-to-all | bytes 10485760 | tf_op jit(solution)/shard_map/all_to_all | solution.py:108
  174.4 1.2 fusion.13
  175.9 2.1 fusion.12
  179.1 3.4 %collective-permute-start.8 = (f32[10,4,128]{2,1,0:T(4,128)S(1)}, f32[10,4,128]{2,1,0:T(4,128)S(1)}, u32[]{:S(2)}, u32[]{:S(2)}) collective-permute-start(f32[10,4,128]{2,1,0:T(4,128)S(1)} %get-tuple-element.18), channel_id=1, source_target_pairs={{1,0},{2,1},{3,2},{4,3},{5,4},{6,5},{7,6},{9,8},{10,9},{11,10},{12... | collective-permute-start | bytes 61448 | tf_op jit(solution)/shard_map/ppermute | solution.py:25
  182.5 2.5 %collective-permute-start.7 = (f32[10,4,128]{2,1,0:T(4,128)S(1)}, f32[10,4,128]{2,1,0:T(4,128)S(1)}, u32[]{:S(2)}, u32[]{:S(2)}) collective-permute-start(f32[10,4,128]{2,1,0:T(4,128)S(1)} %get-tuple-element.17), channel_id=1, source_target_pairs={{0,1},{1,2},{2,3},{3,4},{4,5},{5,6},{6,7},{8,9},{9,10},{10,11},{11... | collective-permute-start | bytes 61448 | tf_op jit(solution)/shard_map/ppermute | solution.py:25
  185.7 2.5 %collective-permute-done.7 = f32[10,4,128]{2,1,0:T(4,128)S(1)} collective-permute-done((f32[10,4,128]{2,1,0:T(4,128)S(1)}, f32[10,4,128]{2,1,0:T(4,128)S(1)}, u32[]{:S(2)}, u32[]{:S(2)}) %collective-permute-start.7) | collective-permute-done | bytes 20512 | tf_op jit(solution)/shard_map/ppermute | solution.py:25
  189.0 5.2 %collective-permute-start.9 = (f32[10,4,136]{2,1,0:T(4,128)S(1)}, f32[10,4,136]{2,1,0:T(4,128)S(1)}, u32[]{:S(2)}, u32[]{:S(2)}) collective-permute-start(f32[10,4,136]{2,1,0:T(4,128)S(1)} %get-tuple-element.13), channel_id=1, source_target_pairs={{0,8},{1,9},{2,10},{3,11},{4,12},{5,13},{6,14},{7,15},{8,16},{9,17... | collective-permute-start | bytes 65288 | tf_op jit(solution)/shard_map/ppermute | solution.py:25
  194.3 1.9 collective-permute-start.10
  196.2 6.1 %collective-permute-done.10 = f32[10,4,136]{2,1,0:T(4,128)S(1)} collective-permute-done((f32[10,4,136]{2,1,0:T(4,128)S(1)}, f32[10,4,136]{2,1,0:T(4,128)S(1)}, u32[]{:S(2)}, u32[]{:S(2)}) %collective-permute-start.10) | collective-permute-done | bytes 21792 | tf_op jit(solution)/shard_map/ppermute | solution.py:25
  202.9 0.8 multiply_add_fusion.2
  203.7 0.8 multiply_add_fusion.1
  205.3 1.8 fusion.23
  (51 shorter events, 7.8 us)
Async XLA Ops:
  1.6 11.6 %copy-start.5 = (f32[1,128,128]{2,1,0:T(8,128)}, f32[1,128,128]{2,1,0:T(8,128)S(1)}, u32[]{:S(2)}) copy-start(f32[1,128,128]{2,1,0:T(8,128)S(1)} %get-tuple-element.6) | copy-start | bytes 196612
  3.7 6.0 %collective-permute-start.1 = (f32[22,4,128]{2,1,0:T(4,128)S(1)}, f32[22,4,128]{2,1,0:T(4,128)S(1)}, u32[]{:S(2)}, u32[]{:S(2)}) collective-permute-start(f32[22,4,128]{2,1,0:T(4,128)S(1)} %get-tuple-element.16), channel_id=1, source_target_pairs={{1,0},{2,1},{3,2},{4,3},{5,4},{6,5},{7,6},{9,8},{10,9},{11,10},{12... | collective-permute-start | bytes 135176 | tf_op jit(solution)/shard_map/ppermute | solution.py:25
  5.8 7.4 %copy-start = (f32[1,10,128,128]{3,2,1,0:T(8,128)S(1)}, f32[1,10,128,128]{3,2,1,0:T(8,128)}, u32[]{:S(2)}) copy-start(f32[1,10,128,128]{3,2,1,0:T(8,128)} %param.8) | copy-start | bytes 1966084
  5.8 7.4 %copy-start.1 = (f32[1,10,128,128]{3,2,1,0:T(8,128)S(1)}, f32[1,10,128,128]{3,2,1,0:T(8,128)}, u32[]{:S(2)}) copy-start(f32[1,10,128,128]{3,2,1,0:T(8,128)} %param.7) | copy-start | bytes 1966084
  5.8 7.4 %copy-start.2 = (f32[1,128,128]{2,1,0:T(8,128)S(1)}, f32[1,128,128]{2,1,0:T(8,128)}, u32[]{:S(2)}) copy-start(f32[1,128,128]{2,1,0:T(8,128)} %param.9) | copy-start | bytes 196612
  5.8 6.1 %collective-permute-start = (f32[22,4,128]{2,1,0:T(4,128)S(1)}, f32[22,4,128]{2,1,0:T(4,128)S(1)}, u32[]{:S(2)}, u32[]{:S(2)}) collective-permute-start(f32[22,4,128]{2,1,0:T(4,128)S(1)} %get-tuple-element.15), channel_id=1, source_target_pairs={{0,1},{1,2},{2,3},{3,4},{4,5},{5,6},{6,7},{8,9},{9,10},{10,11},{11... | collective-permute-start | bytes 135176 | tf_op jit(solution)/shard_map/ppermute | solution.py:25
  13.2 6.7 %copy-start.6 = (s32[1,1,128,2]{2,3,1,0:T(2,128)S(1)}, s32[1,1,128,2]{2,3,1,0:T(2,128)}, u32[]{:S(2)}) copy-start(s32[1,1,128,2]{2,3,1,0:T(2,128)} %param.13) | copy-start | bytes 3076
  14.1 7.7 %collective-permute-start.2 = (f32[22,4,136]{2,1,0:T(4,128)}, f32[22,4,136]{2,1,0:T(4,128)}, u32[]{:S(2)}, u32[]{:S(2)}) collective-permute-start(f32[22,4,136]{2,1,0:T(4,128)} %get-tuple-element.9), channel_id=1, source_target_pairs={{0,8},{1,9},{2,10},{3,11},{4,12},{5,13},{6,14},{7,15},{8,16},{9,17... | collective-permute-start | bytes 143624 | tf_op jit(solution)/shard_map/ppermute | solution.py:25
  17.2 8.8 %collective-permute-start.3 = (f32[22,4,136]{2,1,0:T(4,128)}, f32[22,4,136]{2,1,0:T(4,128)}, u32[]{:S(2)}, u32[]{:S(2)}) collective-permute-start(f32[22,4,136]{2,1,0:T(4,128)} %get-tuple-element.10), channel_id=1, source_target_pairs={{8,0},{9,1},{10,2},{11,3},{12,4},{13,5},{14,6},{15,7},{16,8},{17,9... | collective-permute-start | bytes 143624 | tf_op jit(solution)/shard_map/ppermute | solution.py:25
  21.7 15.6 %collective-permute-start.4 = (s32[256]{0:T(256)S(1)}, s32[256]{0:T(256)S(1)}, u32[]{:S(2)}, u32[]{:S(2)}) collective-permute-start(s32[256]{0:T(256)S(1)} %reshape_squeeze.3), channel_id=1, source_target_pairs={{0,128},{128,0},{1,129},{129,1},{2,130},{130,2},{3,131},{131,3},{4... | collective-permute-start | bytes 3080 | tf_op jit(solution)/shard_map/ppermute | solution.py:66
  30.3 0.8 copy-start.3
  30.3 0.9 copy-start.4
  31.2 1.3 copy-start.7
  31.2 1.5 copy-start.8
  32.2 5.1 %collective-permute-start.5 = (f32[10,64,2,128]{3,1,2,0:T(8,128)S(1)}, f32[10,64,2,128]{3,1,2,0:T(8,128)S(1)}, u32[]{:S(2)}, u32[]{:S(2)}) collective-permute-start(f32[10,64,2,128]{3,1,2,0:T(8,128)S(1)} %copy.37), channel_id=1, source_target_pairs={{0,128},{128,0},{1,129},{129,1},{2,130},{130,2},{3,131},{131,3},{4... | collective-permute-start | bytes 1966088 | tf_op jit(solution)/shard_map/ppermute | solution.py:66
  175.6 2.4 %collective-permute-start.6 = (f32[10,64,2,128]{3,1,2,0:T(8,128)S(1)}, f32[10,64,2,128]{3,1,2,0:T(8,128)S(1)}, u32[]{:S(2)}, u32[]{:S(2)}) collective-permute-start(f32[10,64,2,128]{3,1,2,0:T(8,128)S(1)} %fusion.13), channel_id=1, source_target_pairs={{0,128},{128,0},{1,129},{129,1},{2,130},{130,2},{3,131},{131,3},{4... | collective-permute-start | bytes 1966088 | tf_op jit(solution)/shard_map/ppermute | solution.py:66
  179.1 5.9 %collective-permute-start.8 = (f32[10,4,128]{2,1,0:T(4,128)S(1)}, f32[10,4,128]{2,1,0:T(4,128)S(1)}, u32[]{:S(2)}, u32[]{:S(2)}) collective-permute-start(f32[10,4,128]{2,1,0:T(4,128)S(1)} %get-tuple-element.18), channel_id=1, source_target_pairs={{1,0},{2,1},{3,2},{4,3},{5,4},{6,5},{7,6},{9,8},{10,9},{11,10},{12... | collective-permute-start | bytes 61448 | tf_op jit(solution)/shard_map/ppermute | solution.py:25
  182.5 5.7 %collective-permute-start.7 = (f32[10,4,128]{2,1,0:T(4,128)S(1)}, f32[10,4,128]{2,1,0:T(4,128)S(1)}, u32[]{:S(2)}, u32[]{:S(2)}) collective-permute-start(f32[10,4,128]{2,1,0:T(4,128)S(1)} %get-tuple-element.17), channel_id=1, source_target_pairs={{0,1},{1,2},{2,3},{3,4},{4,5},{5,6},{6,7},{8,9},{9,10},{10,11},{11... | collective-permute-start | bytes 61448 | tf_op jit(solution)/shard_map/ppermute | solution.py:25
  189.0 7.2 %collective-permute-start.9 = (f32[10,4,136]{2,1,0:T(4,128)S(1)}, f32[10,4,136]{2,1,0:T(4,128)S(1)}, u32[]{:S(2)}, u32[]{:S(2)}) collective-permute-start(f32[10,4,136]{2,1,0:T(4,128)S(1)} %get-tuple-element.13), channel_id=1, source_target_pairs={{0,8},{1,9},{2,10},{3,11},{4,12},{5,13},{6,14},{7,15},{8,16},{9,17... | collective-permute-start | bytes 65288 | tf_op jit(solution)/shard_map/ppermute | solution.py:25
  194.3 8.0 %collective-permute-start.10 = (f32[10,4,136]{2,1,0:T(4,128)S(1)}, f32[10,4,136]{2,1,0:T(4,128)S(1)}, u32[]{:S(2)}, u32[]{:S(2)}) collective-permute-start(f32[10,4,136]{2,1,0:T(4,128)S(1)} %get-tuple-element.14), channel_id=1, source_target_pairs={{8,0},{9,1},{10,2},{11,3},{12,4},{13,5},{14,6},{15,7},{16,8},{17,9... | collective-permute-start | bytes 65288 | tf_op jit(solution)/shard_map/ppermute | solution.py:25

commit v13 on v12

--- a/solution.py
+++ b/solution.py
@@ -38,8 +38,8 @@
     cols = cells.shape[2]
     index = jnp.concatenate([jnp.arange(cols - w, cols, dtype=jnp.int32), jnp.arange(w, dtype=jnp.int32)])
     both = jnp.einsum("jc,lrc->ljr", onehot(index, cols), cells, precision=HIGHEST)
-    west = uncolumns(shifted(both[:, :w], 0, -1))
-    east = uncolumns(shifted(both[:, w:], 0, 1))
+    back = uncolumns(jnp.concatenate([shifted(both[:, :w], 0, -1), shifted(both[:, w:], 0, 1)], axis=1))
+    west, east = back[:, :, :w], back[:, :, w:]
     wide = jnp.concatenate([west, cells, east], axis=2)
     north = shifted(wide[:, -w:], -1, 0)
     south = shifted(wide[:, :w], 1, 0)

time: 208 us -> 210 us (level)
  waiting for transfers between devices: 13.6 us -> 16.7 us
    ppermute x8, waiting for transfers between devices: 13.6 us -> 16.7 us  [shifted(): return lax.ppermute(block, ('gx', 'gy'), pairs)]
  transfers between devices with their start and end apart: 11 -> 11, of which waited for: 4 -> 5; matrix products, arithmetic and copies ran while one was open for 8% -> 7% of each run, Pallas kernels for 0% -> 0%
where the time goes in v13:
time: 210 us; the launch traced here: 207 us
  blocking collectives  132 us (63%)
  starting transfers between devices  24.7 us (12%)
  waiting for transfers between devices  16.7 us (8%)
  other arithmetic  14.3 us (7%)
  matrix products  11.5 us (5%)
  local copies, waits for them, and re-layouts  8.03 us (4%)
    all_to_all x1, blocking collectives, couple(): incoming = lax.all_to_all(outgoing, ('gx', 'gy'), 0, 0, tiled=True)  132 us
    ppermute x8, starting transfers between devices, shifted(): return lax.ppermute(block, ('gx', 'gy'), pairs)  24 us
    ppermute x8, waiting for transfers between devices, shifted(): return lax.ppermute(block, ('gx', 'gy'), pairs)  16.7 us
    add x6, other arithmetic, relax(): return (1.0 - OMEGA) * field + OMEGA * invd * (force + visc * beside)  4.88 us
  transfers between devices with their start and end apart: 11, of which 5 were waited for; matrix products, arithmetic and copies ran while one was open for 7% of the time, Pallas kernels for 0%

profile of v13, /device:TPU:54, one launch (start us, length us, event | category | flops | bytes accessed | tf_op | source)
XLA Modules:
  0.0 207.4 jit_solution(18293229551652850211)
XLA Ops:
  0.1 1.5 multiply_bitcast_fusion
  1.6 2.1 %fusion.16 = f32[22,8,128]{2,1,0:T(8,128)S(1)} fusion(f32[1,128,128]{2,1,0:T(8,128)S(1)} %get-tuple-element.6, f32[1,128,128]{2,1,0:T(8,128)} %param.9, f32[10,128,128]{2,1,0:T(8,128)} %bitcast.61, f32[10,128,128]{2,1,0:T(8,128)} %bitcast.67, s32[8]{0:T(128)S(1)} %pad_add_fusion), kind=kOutput, calls=%fused_computation.31 | convolution fusion | flops 35685376 | bytes 1531936 | tf_op jit(solution)/shard_map/jc,lrc->ljr/dot_general | solution.py:40
  3.7 3.8 %collective-permute-start = (f32[22,4,128]{2,1,0:T(4,128)S(1)}, f32[22,4,128]{2,1,0:T(4,128)S(1)}, u32[]{:S(2)}, u32[]{:S(2)}) collective-permute-start(f32[22,4,128]{2,1,0:T(4,128)S(1)} %get-tuple-element.19), channel_id=1, source_target_pairs={{0,1},{1,2},{2,3},{3,4},{4,5},{5,6},{6,7},{8,9},{9,10},{10,11},{11... | collective-permute-start | bytes 135176 | tf_op jit(solution)/shard_map/ppermute | solution.py:25
  7.6 2.0 collective-permute-start.1
  9.7 3.8 %collective-permute-done.1 = f32[22,4,128]{2,1,0:T(4,128)S(1)} collective-permute-done((f32[22,4,128]{2,1,0:T(4,128)S(1)}, f32[22,4,128]{2,1,0:T(4,128)S(1)}, u32[]{:S(2)}, u32[]{:S(2)}) %collective-permute-start.1) | collective-permute-done | bytes 45088 | tf_op jit(solution)/shard_map/ppermute | solution.py:25
  13.5 1.3 fusion.29
  16.1 0.9 pad_maximum_fusion.8
  17.0 3.1 %collective-permute-start.2 = (f32[22,4,136]{2,1,0:T(4,128)}, f32[22,4,136]{2,1,0:T(4,128)}, u32[]{:S(2)}, u32[]{:S(2)}) collective-permute-start(f32[22,4,136]{2,1,0:T(4,128)} %get-tuple-element.9), channel_id=1, source_target_pairs={{0,8},{1,9},{2,10},{3,11},{4,12},{5,13},{6,14},{7,15},{8,16},{9,17... | collective-permute-start | bytes 143624 | tf_op jit(solution)/shard_map/ppermute | solution.py:25
  20.1 2.7 %collective-permute-start.3 = (f32[22,4,136]{2,1,0:T(4,128)}, f32[22,4,136]{2,1,0:T(4,128)}, u32[]{:S(2)}, u32[]{:S(2)}) collective-permute-start(f32[22,4,136]{2,1,0:T(4,128)} %get-tuple-element.10), channel_id=1, source_target_pairs={{8,0},{9,1},{10,2},{11,3},{12,4},{13,5},{14,6},{15,7},{16,8},{17,9... | collective-permute-start | bytes 143624 | tf_op jit(solution)/shard_map/ppermute | solution.py:25
  23.6 1.0 reshape_squeeze.3
  24.7 4.3 %collective-permute-done.3 = f32[22,4,136]{2,1,0:T(4,128)} collective-permute-done((f32[22,4,136]{2,1,0:T(4,128)}, f32[22,4,136]{2,1,0:T(4,128)}, u32[]{:S(2)}, u32[]{:S(2)}) %collective-permute-start.3) | collective-permute-done | bytes 47904 | tf_op jit(solution)/shard_map/ppermute | solution.py:25
  28.9 2.5 %pad_maximum_fusion.1 = f32[22,136,136]{2,1,0:T(8,128)S(1)} fusion(f32[22,4,136]{2,1,0:T(4,128)} %collective-permute-done.3, f32[22,128,4]{2,1,0:T(8,128)S(1)} %get-tuple-element.16, f32[1,128,128]{2,1,0:T(8,128)} %copy-done.5, f32[1,128,128]{2,1,0:T(8,128)} %param.9, f32[10,128,128]{2,1,0:T(8,128)S(1)} %bitcast.63, f32[10,128,128]{2,1,0:T(8,128)} %bitcast.68, ...), kind=kLoop, calls=%fused_computation.1 | loop fusion | flops 2848384 | bytes 3255296 | tf_op jit(solution)/shard_map/concatenate | solution.py:46
  31.5 0.8 multiply_add_fusion.5
  32.4 0.8 multiply_add_fusion.4
  33.2 0.8 multiply_add_fusion.3
  34.1 0.9 fusion.27
  35.8 2.3 %fusion.57 = f32[256,10,2,128]{3,0,2,1:T(8,128)S(1)} fusion(f32[256,64,1,1]{0,1,3,2:T(8,128)S(1)} %convolution_bitcast_fusion, f32[10,64,2,128]{3,2,1,0:T(2,128)S(1)} %bitcast.55), kind=kOutput, calls=%fused_computation.98 | convolution fusion | flops 503316480 | bytes 3342336 | tf_op jit(solution)/shard_map/jk,lkrc->jlrc/dot_general | solution.py:74
  38.1 2.0 copy.32
  40.2 1.2 fusion.37
  41.4 2.0 copy.35
  43.8 131.8 %all_to_all.5 = f32[128,80,128]{2,1,0:T(8,128)S(1)} all-to-all(f32[128,80,128]{2,1,0:T(8,128)S(1)} %pad_maximum_fusion), channel_id=1, replica_groups=mesh['sec'=2,'gx'=16,'gy'=8] {'gx','gy'}, dimensions={0} | all-to-all | bytes 10485760 | tf_op jit(solution)/shard_map/all_to_all | solution.py:108
  176.0 1.2 fusion.13
  177.4 2.1 fusion.12
  180.7 2.6 %collective-permute-start.7 = (f32[10,4,128]{2,1,0:T(4,128)S(1)}, f32[10,4,128]{2,1,0:T(4,128)S(1)}, u32[]{:S(2)}, u32[]{:S(2)}) collective-permute-start(f32[10,4,128]{2,1,0:T(4,128)S(1)} %get-tuple-element.21), channel_id=1, source_target_pairs={{0,1},{1,2},{2,3},{3,4},{4,5},{5,6},{6,7},{8,9},{9,10},{10,11},{11... | collective-permute-start | bytes 61448 | tf_op jit(solution)/shard_map/ppermute | solution.py:25
  183.3 3.2 %collective-permute-start.8 = (f32[10,4,128]{2,1,0:T(4,128)S(1)}, f32[10,4,128]{2,1,0:T(4,128)S(1)}, u32[]{:S(2)}, u32[]{:S(2)}) collective-permute-start(f32[10,4,128]{2,1,0:T(4,128)S(1)} %get-tuple-element.22), channel_id=1, source_target_pairs={{1,0},{2,1},{3,2},{4,3},{5,4},{6,5},{7,6},{9,8},{10,9},{11,10},{12... | collective-permute-start | bytes 61448 | tf_op jit(solution)/shard_map/ppermute | solution.py:25
  186.5 2.4 %collective-permute-done.8 = f32[10,4,128]{2,1,0:T(4,128)S(1)} collective-permute-done((f32[10,4,128]{2,1,0:T(4,128)S(1)}, f32[10,4,128]{2,1,0:T(4,128)S(1)}, u32[]{:S(2)}, u32[]{:S(2)}) %collective-permute-start.8) | collective-permute-done | bytes 20512 | tf_op jit(solution)/shard_map/ppermute | solution.py:25
  190.0 4.6 %collective-permute-start.9 = (f32[10,4,136]{2,1,0:T(4,128)S(1)}, f32[10,4,136]{2,1,0:T(4,128)S(1)}, u32[]{:S(2)}, u32[]{:S(2)}) collective-permute-start(f32[10,4,136]{2,1,0:T(4,128)S(1)} %get-tuple-element.13), channel_id=1, source_target_pairs={{0,8},{1,9},{2,10},{3,11},{4,12},{5,13},{6,14},{7,15},{8,16},{9,17... | collective-permute-start | bytes 65288 | tf_op jit(solution)/shard_map/ppermute | solution.py:25
  194.6 1.9 collective-permute-start.10
  196.5 6.1 %collective-permute-done.10 = f32[10,4,136]{2,1,0:T(4,128)S(1)} collective-permute-done((f32[10,4,136]{2,1,0:T(4,128)S(1)}, f32[10,4,136]{2,1,0:T(4,128)S(1)}, u32[]{:S(2)}, u32[]{:S(2)}) %collective-permute-start.10) | collective-permute-done | bytes 21792 | tf_op jit(solution)/shard_map/ppermute | solution.py:25
  204.0 0.8 multiply_add_fusion.1
  204.9 0.8 multiply_add_fusion
  205.7 1.8 fusion.23
  (51 shorter events, 7.9 us)
Async XLA Ops:
  1.6 13.8 %copy-start.5 = (f32[1,128,128]{2,1,0:T(8,128)}, f32[1,128,128]{2,1,0:T(8,128)S(1)}, u32[]{:S(2)}) copy-start(f32[1,128,128]{2,1,0:T(8,128)S(1)} %get-tuple-element.6) | copy-start | bytes 196612
  3.7 5.9 %collective-permute-start = (f32[22,4,128]{2,1,0:T(4,128)S(1)}, f32[22,4,128]{2,1,0:T(4,128)S(1)}, u32[]{:S(2)}, u32[]{:S(2)}) collective-permute-start(f32[22,4,128]{2,1,0:T(4,128)S(1)} %get-tuple-element.19), channel_id=1, source_target_pairs={{0,1},{1,2},{2,3},{3,4},{4,5},{5,6},{6,7},{8,9},{9,10},{10,11},{11... | collective-permute-start | bytes 135176 | tf_op jit(solution)/shard_map/ppermute | solution.py:25
  7.6 5.9 %collective-permute-start.1 = (f32[22,4,128]{2,1,0:T(4,128)S(1)}, f32[22,4,128]{2,1,0:T(4,128)S(1)}, u32[]{:S(2)}, u32[]{:S(2)}) collective-permute-start(f32[22,4,128]{2,1,0:T(4,128)S(1)} %get-tuple-element.20), channel_id=1, source_target_pairs={{1,0},{2,1},{3,2},{4,3},{5,4},{6,5},{7,6},{9,8},{10,9},{11,10},{12... | collective-permute-start | bytes 135176 | tf_op jit(solution)/shard_map/ppermute | solution.py:25
  14.8 1.1 copy-start
  14.8 1.3 copy-start.1
  14.8 1.3 copy-start.2
  16.1 6.7 %copy-start.6 = (s32[1,1,128,2]{2,3,1,0:T(2,128)S(1)}, s32[1,1,128,2]{2,3,1,0:T(2,128)}, u32[]{:S(2)}) copy-start(s32[1,1,128,2]{2,3,1,0:T(2,128)} %param.13) | copy-start | bytes 3076
  17.0 7.7 %collective-permute-start.2 = (f32[22,4,136]{2,1,0:T(4,128)}, f32[22,4,136]{2,1,0:T(4,128)}, u32[]{:S(2)}, u32[]{:S(2)}) collective-permute-start(f32[22,4,136]{2,1,0:T(4,128)} %get-tuple-element.9), channel_id=1, source_target_pairs={{0,8},{1,9},{2,10},{3,11},{4,12},{5,13},{6,14},{7,15},{8,16},{9,17... | collective-permute-start | bytes 143624 | tf_op jit(solution)/shard_map/ppermute | solution.py:25
  20.1 8.8 %collective-permute-start.3 = (f32[22,4,136]{2,1,0:T(4,128)}, f32[22,4,136]{2,1,0:T(4,128)}, u32[]{:S(2)}, u32[]{:S(2)}) collective-permute-start(f32[22,4,136]{2,1,0:T(4,128)} %get-tuple-element.10), channel_id=1, source_target_pairs={{8,0},{9,1},{10,2},{11,3},{12,4},{13,5},{14,6},{15,7},{16,8},{17,9... | collective-permute-start | bytes 143624 | tf_op jit(solution)/shard_map/ppermute | solution.py:25
  24.6 15.6 %collective-permute-start.4 = (s32[256]{0:T(256)S(1)}, s32[256]{0:T(256)S(1)}, u32[]{:S(2)}, u32[]{:S(2)}) collective-permute-start(s32[256]{0:T(256)S(1)} %reshape_squeeze.3), channel_id=1, source_target_pairs={{0,128},{128,0},{1,129},{129,1},{2,130},{130,2},{3,131},{131,3},{4... | collective-permute-start | bytes 3080 | tf_op jit(solution)/shard_map/ppermute | solution.py:66
  33.2 0.8 copy-start.3
  33.2 0.9 copy-start.4
  34.1 1.3 copy-start.7
  34.1 1.5 copy-start.8
  35.1 5.1 %collective-permute-start.5 = (f32[10,64,2,128]{3,1,2,0:T(8,128)S(1)}, f32[10,64,2,128]{3,1,2,0:T(8,128)S(1)}, u32[]{:S(2)}, u32[]{:S(2)}) collective-permute-start(f32[10,64,2,128]{3,1,2,0:T(8,128)S(1)} %copy.37), channel_id=1, source_target_pairs={{0,128},{128,0},{1,129},{129,1},{2,130},{130,2},{3,131},{131,3},{4... | collective-permute-start | bytes 1966088 | tf_op jit(solution)/shard_map/ppermute | solution.py:66
  177.1 2.4 %collective-permute-start.6 = (f32[10,64,2,128]{3,1,2,0:T(8,128)S(1)}, f32[10,64,2,128]{3,1,2,0:T(8,128)S(1)}, u32[]{:S(2)}, u32[]{:S(2)}) collective-permute-start(f32[10,64,2,128]{3,1,2,0:T(8,128)S(1)} %fusion.13), channel_id=1, source_target_pairs={{0,128},{128,0},{1,129},{129,1},{2,130},{130,2},{3,131},{131,3},{4... | collective-permute-start | bytes 1966088 | tf_op jit(solution)/shard_map/ppermute | solution.py:66
  180.7 5.9 %collective-permute-start.7 = (f32[10,4,128]{2,1,0:T(4,128)S(1)}, f32[10,4,128]{2,1,0:T(4,128)S(1)}, u32[]{:S(2)}, u32[]{:S(2)}) collective-permute-start(f32[10,4,128]{2,1,0:T(4,128)S(1)} %get-tuple-element.21), channel_id=1, source_target_pairs={{0,1},{1,2},{2,3},{3,4},{4,5},{5,6},{6,7},{8,9},{9,10},{10,11},{11... | collective-permute-start | bytes 61448 | tf_op jit(solution)/shard_map/ppermute | solution.py:25
  183.3 5.7 %collective-permute-start.8 = (f32[10,4,128]{2,1,0:T(4,128)S(1)}, f32[10,4,128]{2,1,0:T(4,128)S(1)}, u32[]{:S(2)}, u32[]{:S(2)}) collective-permute-start(f32[10,4,128]{2,1,0:T(4,128)S(1)} %get-tuple-element.22), channel_id=1, source_target_pairs={{1,0},{2,1},{3,2},{4,3},{5,4},{6,5},{7,6},{9,8},{10,9},{11,10},{12... | collective-permute-start | bytes 61448 | tf_op jit(solution)/shard_map/ppermute | solution.py:25
  190.0 6.5 %collective-permute-start.9 = (f32[10,4,136]{2,1,0:T(4,128)S(1)}, f32[10,4,136]{2,1,0:T(4,128)S(1)}, u32[]{:S(2)}, u32[]{:S(2)}) collective-permute-start(f32[10,4,136]{2,1,0:T(4,128)S(1)} %get-tuple-element.13), channel_id=1, source_target_pairs={{0,8},{1,9},{2,10},{3,11},{4,12},{5,13},{6,14},{7,15},{8,16},{9,17... | collective-permute-start | bytes 65288 | tf_op jit(solution)/shard_map/ppermute | solution.py:25
  194.6 8.0 %collective-permute-start.10 = (f32[10,4,136]{2,1,0:T(4,128)S(1)}, f32[10,4,136]{2,1,0:T(4,128)S(1)}, u32[]{:S(2)}, u32[]{:S(2)}) collective-permute-start(f32[10,4,136]{2,1,0:T(4,128)S(1)} %get-tuple-element.14), channel_id=1, source_target_pairs={{8,0},{9,1},{10,2},{11,3},{12,4},{13,5},{14,6},{15,7},{16,8},{17,9... | collective-permute-start | bytes 65288 | tf_op jit(solution)/shard_map/ppermute | solution.py:25

commit v14 on v12

--- a/solution.py
+++ b/solution.py
@@ -104,10 +104,10 @@
     local = pick(recv_sel, other)
     half = slots_per * levels * PATCH
     chunk = (groups, half, cols)
-    outgoing = jnp.concatenate([sent.reshape(chunk), local.reshape(chunk)], axis=1)
+    outgoing = jnp.stack([sent.reshape(chunk), local.reshape(chunk)], axis=1)
     incoming = lax.all_to_all(outgoing, ("gx", "gy"), 0, 0, tiled=True)
-    arrived = incoming[:, :half].reshape(nslot, levels, PATCH, cols)
-    answer = incoming[:, half:].reshape(nslot, levels, PATCH, cols)
+    arrived = incoming[:, 0].reshape(nslot, levels, PATCH, cols)
+    answer = incoming[:, 1].reshape(nslot, levels, PATCH, cols)
     for_other = spread(recv_sel, KAPPA * arrived)
     for_mine = spread(send_sel, answer * jnp.tanh(sent))
     updated = mine + swap_sec(for_other) + for_mine

time: 208 us -> 208 us (level)
  no operation moved by 1% of the time
where the time goes in v14:
time: 208 us; the launch traced here: 207 us
  blocking collectives  133 us (64%)
  starting transfers between devices  25.5 us (12%)
  other arithmetic  14.1 us (7%)
  waiting for transfers between devices  13.6 us (7%)
  matrix products  13.5 us (6%)
  local copies, waits for them, and re-layouts  7.12 us (3%)
    all_to_all x1, blocking collectives, couple(): incoming = lax.all_to_all(outgoing, ('gx', 'gy'), 0, 0, tiled=True)  133 us
    ppermute x8, starting transfers between devices, shifted(): return lax.ppermute(block, ('gx', 'gy'), pairs)  24.8 us
    ppermute x8, waiting for transfers between devices, shifted(): return lax.ppermute(block, ('gx', 'gy'), pairs)  13.6 us
    add x6, other arithmetic, relax(): return (1.0 - OMEGA) * field + OMEGA * invd * (force + visc * beside)  4.88 us
  transfers between devices with their start and end apart: 11, of which 4 were waited for; matrix products, arithmetic and copies ran while one was open for 8% of the time, Pallas kernels for 0%

profile of v14, /device:TPU:54, one launch (start us, length us, event | category | flops | bytes accessed | tf_op | source)
XLA Modules:
  0.0 207.5 jit_solution(7217267960458301352)
XLA Ops:
  0.1 1.5 multiply_bitcast_fusion
  1.6 2.1 %fusion.17 = f32[22,8,128]{2,1,0:T(8,128)S(1)} fusion(f32[1,128,128]{2,1,0:T(8,128)S(1)} %get-tuple-element.6, f32[1,128,128]{2,1,0:T(8,128)} %param.9, f32[10,128,128]{2,1,0:T(8,128)} %bitcast.73, f32[10,128,128]{2,1,0:T(8,128)} %bitcast.79, s32[8]{0:T(128)S(1)} %pad_add_fusion), kind=kOutput, calls=%fused_computation.32 | convolution fusion | flops 35685376 | bytes 1531936 | tf_op jit(solution)/shard_map/jc,lrc->ljr/dot_general | solution.py:40
  3.7 2.0 collective-permute-start.1
  5.8 4.0 %collective-permute-start = (f32[22,4,128]{2,1,0:T(4,128)S(1)}, f32[22,4,128]{2,1,0:T(4,128)S(1)}, u32[]{:S(2)}, u32[]{:S(2)}) collective-permute-start(f32[22,4,128]{2,1,0:T(4,128)S(1)} %get-tuple-element.13), channel_id=1, source_target_pairs={{0,1},{1,2},{2,3},{3,4},{4,5},{5,6},{6,7},{8,9},{9,10},{10,11},{11... | collective-permute-start | bytes 135176 | tf_op jit(solution)/shard_map/ppermute | solution.py:25
  9.8 1.3 fusion.49
  11.9 1.3 fusion.51
  13.2 0.9 pad_maximum_fusion.8
  14.1 3.1 %collective-permute-start.2 = (f32[22,4,136]{2,1,0:T(4,128)}, f32[22,4,136]{2,1,0:T(4,128)}, u32[]{:S(2)}, u32[]{:S(2)}) collective-permute-start(f32[22,4,136]{2,1,0:T(4,128)} %get-tuple-element.7), channel_id=1, source_target_pairs={{0,8},{1,9},{2,10},{3,11},{4,12},{5,13},{6,14},{7,15},{8,16},{9,17... | collective-permute-start | bytes 143624 | tf_op jit(solution)/shard_map/ppermute | solution.py:25
  17.2 2.7 %collective-permute-start.3 = (f32[22,4,136]{2,1,0:T(4,128)}, f32[22,4,136]{2,1,0:T(4,128)}, u32[]{:S(2)}, u32[]{:S(2)}) collective-permute-start(f32[22,4,136]{2,1,0:T(4,128)} %get-tuple-element.8), channel_id=1, source_target_pairs={{8,0},{9,1},{10,2},{11,3},{12,4},{13,5},{14,6},{15,7},{16,8},{17,9... | collective-permute-start | bytes 143624 | tf_op jit(solution)/shard_map/ppermute | solution.py:25
  20.7 1.0 reshape_squeeze.7
  21.8 4.3 %collective-permute-done.3 = f32[22,4,136]{2,1,0:T(4,128)} collective-permute-done((f32[22,4,136]{2,1,0:T(4,128)}, f32[22,4,136]{2,1,0:T(4,128)}, u32[]{:S(2)}, u32[]{:S(2)}) %collective-permute-start.3) | collective-permute-done | bytes 47904 | tf_op jit(solution)/shard_map/ppermute | solution.py:25
  26.1 2.5 %pad_maximum_fusion.1 = f32[22,136,136]{2,1,0:T(8,128)S(1)} fusion(f32[22,4,136]{2,1,0:T(4,128)} %collective-permute-done.3, f32[22,128,4]{2,1,0:T(8,128)S(1)} %fusion.49, f32[1,128,128]{2,1,0:T(8,128)} %copy-done.5, f32[1,128,128]{2,1,0:T(8,128)} %param.9, f32[10,128,128]{2,1,0:T(8,128)S(1)} %bitcast.75, f32[10,128,128]{2,1,0:T(8,128)} %bitcast.80, ...), kind=kLoop, calls=%fused_computation.1 | loop fusion | flops 2848384 | bytes 3255296 | tf_op jit(solution)/shard_map/concatenate | solution.py:46
  28.7 0.8 multiply_add_fusion.5
  30.3 0.8 multiply_add_fusion.3
  31.2 0.9 fusion.28
  32.9 2.3 %fusion.54 = f32[256,10,2,128]{3,0,2,1:T(8,128)S(1)} fusion(f32[256,64,1,1]{0,1,3,2:T(8,128)S(1)} %convolution_bitcast_fusion, f32[10,64,2,128]{3,2,1,0:T(2,128)S(1)} %bitcast.67), kind=kOutput, calls=%fused_computation.93 | convolution fusion | flops 503316480 | bytes 3342336 | tf_op jit(solution)/shard_map/jk,lkrc->jlrc/dot_general | solution.py:74
  35.2 2.0 copy.48
  37.3 1.2 fusion.34
  38.5 2.0 copy.51
  41.3 133.1 %all_to_all.5 = f32[128,2,40,128]{3,2,1,0:T(8,128)S(1)} all-to-all(f32[128,2,40,128]{3,2,1,0:T(8,128)S(1)} %copy.52), channel_id=1, replica_groups=mesh['sec'=2,'gx'=16,'gy'=8] {'gx','gy'}, dimensions={0} | all-to-all | bytes 10485760 | tf_op jit(solution)/shard_map/all_to_all | solution.py:108
  174.6 1.2 fusion.14
  176.3 2.1 fusion.13
  179.5 3.4 %collective-permute-start.8 = (f32[10,4,128]{2,1,0:T(4,128)S(1)}, f32[10,4,128]{2,1,0:T(4,128)S(1)}, u32[]{:S(2)}, u32[]{:S(2)}) collective-permute-start(f32[10,4,128]{2,1,0:T(4,128)S(1)} %get-tuple-element.16), channel_id=1, source_target_pairs={{1,0},{2,1},{3,2},{4,3},{5,4},{6,5},{7,6},{9,8},{10,9},{11,10},{12... | collective-permute-start | bytes 61448 | tf_op jit(solution)/shard_map/ppermute | solution.py:25
  182.9 2.5 %collective-permute-start.7 = (f32[10,4,128]{2,1,0:T(4,128)S(1)}, f32[10,4,128]{2,1,0:T(4,128)S(1)}, u32[]{:S(2)}, u32[]{:S(2)}) collective-permute-start(f32[10,4,128]{2,1,0:T(4,128)S(1)} %get-tuple-element.15), channel_id=1, source_target_pairs={{0,1},{1,2},{2,3},{3,4},{4,5},{5,6},{6,7},{8,9},{9,10},{10,11},{11... | collective-permute-start | bytes 61448 | tf_op jit(solution)/shard_map/ppermute | solution.py:25
  186.1 2.5 %collective-permute-done.7 = f32[10,4,128]{2,1,0:T(4,128)S(1)} collective-permute-done((f32[10,4,128]{2,1,0:T(4,128)S(1)}, f32[10,4,128]{2,1,0:T(4,128)S(1)}, u32[]{:S(2)}, u32[]{:S(2)}) %collective-permute-start.7) | collective-permute-done | bytes 20512 | tf_op jit(solution)/shard_map/ppermute | solution.py:25
  189.4 5.2 %collective-permute-start.9 = (f32[10,4,136]{2,1,0:T(4,128)S(1)}, f32[10,4,136]{2,1,0:T(4,128)S(1)}, u32[]{:S(2)}, u32[]{:S(2)}) collective-permute-start(f32[10,4,136]{2,1,0:T(4,128)S(1)} %get-tuple-element.11), channel_id=1, source_target_pairs={{0,8},{1,9},{2,10},{3,11},{4,12},{5,13},{6,14},{7,15},{8,16},{9,17... | collective-permute-start | bytes 65288 | tf_op jit(solution)/shard_map/ppermute | solution.py:25
  194.6 1.9 collective-permute-start.10
  196.6 6.1 %collective-permute-done.10 = f32[10,4,136]{2,1,0:T(4,128)S(1)} collective-permute-done((f32[10,4,136]{2,1,0:T(4,128)S(1)}, f32[10,4,136]{2,1,0:T(4,128)S(1)}, u32[]{:S(2)}, u32[]{:S(2)}) %collective-permute-start.10) | collective-permute-done | bytes 21792 | tf_op jit(solution)/shard_map/ppermute | solution.py:25
  203.2 0.8 multiply_add_fusion.2
  204.1 0.8 multiply_add_fusion.1
  204.9 0.8 multiply_add_fusion
  205.7 1.8 fusion.24
  (53 shorter events, 8.1 us)
Async XLA Ops:
  1.6 11.6 %copy-start.5 = (f32[1,128,128]{2,1,0:T(8,128)}, f32[1,128,128]{2,1,0:T(8,128)S(1)}, u32[]{:S(2)}) copy-start(f32[1,128,128]{2,1,0:T(8,128)S(1)} %get-tuple-element.6) | copy-start | bytes 196612
  3.7 6.0 %collective-permute-start.1 = (f32[22,4,128]{2,1,0:T(4,128)S(1)}, f32[22,4,128]{2,1,0:T(4,128)S(1)}, u32[]{:S(2)}, u32[]{:S(2)}) collective-permute-start(f32[22,4,128]{2,1,0:T(4,128)S(1)} %get-tuple-element.14), channel_id=1, source_target_pairs={{1,0},{2,1},{3,2},{4,3},{5,4},{6,5},{7,6},{9,8},{10,9},{11,10},{12... | collective-permute-start | bytes 135176 | tf_op jit(solution)/shard_map/ppermute | solution.py:25
  5.8 7.4 %copy-start = (f32[1,10,128,128]{3,2,1,0:T(8,128)S(1)}, f32[1,10,128,128]{3,2,1,0:T(8,128)}, u32[]{:S(2)}) copy-start(f32[1,10,128,128]{3,2,1,0:T(8,128)} %param.8) | copy-start | bytes 1966084
  5.8 7.4 %copy-start.1 = (f32[1,10,128,128]{3,2,1,0:T(8,128)S(1)}, f32[1,10,128,128]{3,2,1,0:T(8,128)}, u32[]{:S(2)}) copy-start(f32[1,10,128,128]{3,2,1,0:T(8,128)} %param.7) | copy-start | bytes 1966084
  5.8 7.4 %copy-start.2 = (f32[1,128,128]{2,1,0:T(8,128)S(1)}, f32[1,128,128]{2,1,0:T(8,128)}, u32[]{:S(2)}) copy-start(f32[1,128,128]{2,1,0:T(8,128)} %param.9) | copy-start | bytes 196612
  5.8 6.1 %collective-permute-start = (f32[22,4,128]{2,1,0:T(4,128)S(1)}, f32[22,4,128]{2,1,0:T(4,128)S(1)}, u32[]{:S(2)}, u32[]{:S(2)}) collective-permute-start(f32[22,4,128]{2,1,0:T(4,128)S(1)} %get-tuple-element.13), channel_id=1, source_target_pairs={{0,1},{1,2},{2,3},{3,4},{4,5},{5,6},{6,7},{8,9},{9,10},{10,11},{11... | collective-permute-start | bytes 135176 | tf_op jit(solution)/shard_map/ppermute | solution.py:25
  13.2 6.7 %copy-start.6 = (s32[1,1,128,2]{2,3,1,0:T(2,128)S(1)}, s32[1,1,128,2]{2,3,1,0:T(2,128)}, u32[]{:S(2)}) copy-start(s32[1,1,128,2]{2,3,1,0:T(2,128)} %param.13) | copy-start | bytes 3076
  14.1 7.7 %collective-permute-start.2 = (f32[22,4,136]{2,1,0:T(4,128)}, f32[22,4,136]{2,1,0:T(4,128)}, u32[]{:S(2)}, u32[]{:S(2)}) collective-permute-start(f32[22,4,136]{2,1,0:T(4,128)} %get-tuple-element.7), channel_id=1, source_target_pairs={{0,8},{1,9},{2,10},{3,11},{4,12},{5,13},{6,14},{7,15},{8,16},{9,17... | collective-permute-start | bytes 143624 | tf_op jit(solution)/shard_map/ppermute | solution.py:25
  17.2 8.8 %collective-permute-start.3 = (f32[22,4,136]{2,1,0:T(4,128)}, f32[22,4,136]{2,1,0:T(4,128)}, u32[]{:S(2)}, u32[]{:S(2)}) collective-permute-start(f32[22,4,136]{2,1,0:T(4,128)} %get-tuple-element.8), channel_id=1, source_target_pairs={{8,0},{9,1},{10,2},{11,3},{12,4},{13,5},{14,6},{15,7},{16,8},{17,9... | collective-permute-start | bytes 143624 | tf_op jit(solution)/shard_map/ppermute | solution.py:25
  21.7 15.6 %collective-permute-start.4 = (s32[256]{0:T(256)S(1)}, s32[256]{0:T(256)S(1)}, u32[]{:S(2)}, u32[]{:S(2)}) collective-permute-start(s32[256]{0:T(256)S(1)} %reshape_squeeze.7), channel_id=1, source_target_pairs={{0,128},{128,0},{1,129},{129,1},{2,130},{130,2},{3,131},{131,3},{4... | collective-permute-start | bytes 3080 | tf_op jit(solution)/shard_map/ppermute | solution.py:66
  30.3 0.8 copy-start.3
  30.3 0.9 copy-start.4
  31.2 1.3 copy-start.7
  31.2 1.5 copy-start.8
  32.2 5.1 %collective-permute-start.5 = (f32[10,64,2,128]{3,1,2,0:T(8,128)S(1)}, f32[10,64,2,128]{3,1,2,0:T(8,128)S(1)}, u32[]{:S(2)}, u32[]{:S(2)}) collective-permute-start(f32[10,64,2,128]{3,1,2,0:T(8,128)S(1)} %copy.55), channel_id=1, source_target_pairs={{0,128},{128,0},{1,129},{129,1},{2,130},{130,2},{3,131},{131,3},{4... | collective-permute-start | bytes 1966088 | tf_op jit(solution)/shard_map/ppermute | solution.py:66
  175.8 2.6 %collective-permute-start.6 = (f32[10,64,2,128]{3,1,2,0:T(8,128)S(1)}, f32[10,64,2,128]{3,1,2,0:T(8,128)S(1)}, u32[]{:S(2)}, u32[]{:S(2)}) collective-permute-start(f32[10,64,2,128]{3,1,2,0:T(8,128)S(1)} %fusion.14), channel_id=1, source_target_pairs={{0,128},{128,0},{1,129},{129,1},{2,130},{130,2},{3,131},{131,3},{4... | collective-permute-start | bytes 1966088 | tf_op jit(solution)/shard_map/ppermute | solution.py:66
  179.5 5.9 %collective-permute-start.8 = (f32[10,4,128]{2,1,0:T(4,128)S(1)}, f32[10,4,128]{2,1,0:T(4,128)S(1)}, u32[]{:S(2)}, u32[]{:S(2)}) collective-permute-start(f32[10,4,128]{2,1,0:T(4,128)S(1)} %get-tuple-element.16), channel_id=1, source_target_pairs={{1,0},{2,1},{3,2},{4,3},{5,4},{6,5},{7,6},{9,8},{10,9},{11,10},{12... | collective-permute-start | bytes 61448 | tf_op jit(solution)/shard_map/ppermute | solution.py:25
  182.9 5.7 %collective-permute-start.7 = (f32[10,4,128]{2,1,0:T(4,128)S(1)}, f32[10,4,128]{2,1,0:T(4,128)S(1)}, u32[]{:S(2)}, u32[]{:S(2)}) collective-permute-start(f32[10,4,128]{2,1,0:T(4,128)S(1)} %get-tuple-element.15), channel_id=1, source_target_pairs={{0,1},{1,2},{2,3},{3,4},{4,5},{5,6},{6,7},{8,9},{9,10},{10,11},{11... | collective-permute-start | bytes 61448 | tf_op jit(solution)/shard_map/ppermute | solution.py:25
  189.4 7.2 %collective-permute-start.9 = (f32[10,4,136]{2,1,0:T(4,128)S(1)}, f32[10,4,136]{2,1,0:T(4,128)S(1)}, u32[]{:S(2)}, u32[]{:S(2)}) collective-permute-start(f32[10,4,136]{2,1,0:T(4,128)S(1)} %get-tuple-element.11), channel_id=1, source_target_pairs={{0,8},{1,9},{2,10},{3,11},{4,12},{5,13},{6,14},{7,15},{8,16},{9,17... | collective-permute-start | bytes 65288 | tf_op jit(solution)/shard_map/ppermute | solution.py:25
  194.6 8.0 %collective-permute-start.10 = (f32[10,4,136]{2,1,0:T(4,128)S(1)}, f32[10,4,136]{2,1,0:T(4,128)S(1)}, u32[]{:S(2)}, u32[]{:S(2)}) collective-permute-start(f32[10,4,136]{2,1,0:T(4,128)S(1)} %get-tuple-element.12), channel_id=1, source_target_pairs={{8,0},{9,1},{10,2},{11,3},{12,4},{13,5},{14,6},{15,7},{16,8},{17,9... | collective-permute-start | bytes 65288 | tf_op jit(solution)/shard_map/ppermute | solution.py:25
